TPU v7x, 512 devices: a whole 4x4x16 slice. The times are simulated.
512 devices in a mesh: dp: 32 (over y, z_lo, core), ctx: 16 (over x, z_hi).
Axes of the slice: x: 4, y: 4, z: 16 (z_hi: 4, z_lo: 4; z = z_hi * 4 + z_lo), core: 2. Of those that a mesh axis runs over, the one named last changes fastest.
Arguments:
- branch_in: bfloat16 [32, 2048, 2816], P('dp', 'ctx'), may hold values from -6 to 6
- cotangent: bfloat16 [32, 2048, 2816], P('dp', 'ctx'), may hold values from -6 to 6
- weight_a: bfloat16 [256, 2816], P('dp', 'ctx'), may hold values from -0.375 to 0.375
- weight_x: bfloat16 [256, 2816], P('dp', 'ctx'), may hold values from -0.375 to 0.375
- conv_weight: bfloat16 [4, 2816], P(None, 'ctx'), may hold values from -3 to 3
- conv_bias: bfloat16 [2816], P('ctx'), may hold values from -3 to 3
- bias_a: bfloat16 [2816], P('ctx'), may hold values from -4 to 4
- bias_x: bfloat16 [2816], P('ctx'), may hold values from -4 to 4
- rate: bfloat16 [2816], P('ctx'), may hold values from 0 to 0.016, as said below
Outputs:
- grad_input: bfloat16 [32, 2048, 2816], P('dp', 'ctx')
- grad_weight_a: float32 [256, 2816], P('dp', 'ctx')
- grad_rate: float32 [2816], replicated
Inputs may be any that keep to these rules, and one draw needn't show every extreme that they name: `rate`: positive in every channel.
All inputs are finite; a program needn't handle non-finite values.
Results may differ from a plain program's by a relative error of at most 0.006.
Values may be sent and summed in bfloat16 or wider, within the bound.
No kernel may reach another device: no remote copies, remote signals or barrier semaphores. Data moves between devices by JAX's collectives and lax.ppermute only.
A program may use at most 128 MiB of HBM per device.

v0:
```python
import jax
import jax.numpy as jnp
from jax import lax
from jax.sharding import PartitionSpec as P

floor_value = 2.5e-07
exact = lax.Precision.HIGHEST


def passed_along(array, axis, by):
    length = lax.axis_size(axis)
    pairs = [(i, i + by) for i in range(length) if 0 <= i + by < length]
    return lax.ppermute(array, axis, pairs)


def mix_heads(values, weights):
    tokens = values.shape[0]
    head_count, head_width, _ = weights.shape
    left = values.reshape(tokens, head_count, head_width)
    result = jnp.einsum("thk,hkj->thj", left, weights, preferred_element_type=jnp.float32)
    return result.reshape(tokens, head_count * head_width)


def back_heads(grads, weights):
    tokens = grads.shape[0]
    head_count, head_width, _ = weights.shape
    left = grads.reshape(tokens, head_count, head_width)
    result = jnp.einsum("thj,hkj->thk", left, weights, preferred_element_type=jnp.float32)
    return result.reshape(tokens, head_count * head_width)


def grad_heads(values, grads, head_width):
    tokens = values.shape[0]
    head_count = values.shape[1] // head_width
    left = values.reshape(tokens, head_count, head_width)
    right = grads.reshape(tokens, head_count, head_width)
    result = jnp.einsum("thk,thj->khj", left, right, preferred_element_type=jnp.float32)
    return result.reshape(head_width, head_count * head_width)


def compose(own, received):
    return (own[0] * received[0], own[0] * received[1] + own[1])


def block_prefix(decay_all, forward_all, backward_all, axis):
    span = lax.axis_size(axis)
    me = lax.axis_index(axis)
    ones = jnp.ones_like(decay_all)
    zeros = jnp.zeros_like(decay_all)
    group = (decay_all, forward_all, backward_all)
    before = (ones, zeros)
    after = (ones, zeros)
    stride = 1
    while stride < span:
        got = exchanged(jnp.stack(group), axis, stride)
        other = (got[0], got[1], got[2])
        right_half = (me // stride) % 2 == 1
        mixed_before = compose(before, (other[0], other[1]))
        mixed_after = compose(after, (other[0], other[2]))
        before = tuple(jnp.where(right_half, n, o) for n, o in zip(mixed_before, before))
        after = tuple(jnp.where(right_half, o, n) for n, o in zip(mixed_after, after))
        forward_total = jnp.where(
            right_half, group[0] * other[1] + group[1], other[0] * group[1] + other[1]
        )
        backward_total = jnp.where(
            right_half, other[0] * group[2] + other[2], group[0] * other[2] + group[2]
        )
        group = (group[0] * other[0], forward_total, backward_total)
        stride *= 2
    return before[1], after[1]

def bit_steps(length):
    return [[stride] for step in digit_steps(length) for stride in step]


def digit_steps(length):
    bits = []
    stride = 1
    while stride < length:
        bits.append(stride)
        stride *= 2
    return [bits[i : i + 2] for i in range(0, len(bits), 2)]


def exchanged(array, axis, mask):
    length = lax.axis_size(axis)
    return lax.ppermute(array, axis, [(i, i ^ mask) for i in range(length)])


def patterns(step):
    masks = [0]
    for stride in step:
        masks = masks + [m + stride for m in masks]
    return masks


def digit_of(me, step):
    value = jnp.int32(0)
    for place, stride in enumerate(step):
        value = value + ((me // stride) % 2) * (2**place)
    return value


def mask_of(pattern_index, step):
    mask = 0
    for place, stride in enumerate(step):
        if (pattern_index >> place) & 1:
            mask += stride
    return mask


def gathered_by_doubling(piece, axis, steps):
    length = lax.axis_size(axis)
    me = lax.axis_index(axis)
    held = piece
    done = 0
    order = []
    for step in steps:
        size = 2 ** len(step)
        mine = digit_of(me, step)
        sources = [held] + [exchanged(held, axis, mask_of(p, step)) for p in range(1, size)]
        pool = jnp.stack(sources, 0)
        slots = [
            lax.dynamic_index_in_dim(pool, jnp.bitwise_xor(mine, v), 0, keepdims=False)
            for v in range(size)
        ]
        held = jnp.stack(slots, done)
        held = held.reshape(held.shape[:done] + (2,) * len(step) + held.shape[done + 1 :])
        order = order + step[::-1]
        done += len(step)
    rank = sorted(range(done), key=lambda j: -order[j])
    held = held.transpose(rank + list(range(done, held.ndim)))
    return held.reshape((length,) + piece.shape)


def summed_by_halving(blocks, axis, steps):
    length = lax.axis_size(axis)
    me = lax.axis_index(axis)
    bits = []
    stride = length // 2
    while stride >= 1:
        bits.append(stride)
        stride //= 2
    held = blocks
    for step in steps:
        size = 2 ** len(step)
        mine = digit_of(me, step)
        rest = [b for b in bits if b not in step]
        front = held.reshape((2,) * len(bits) + blocks.shape[1:]) if bits else held
        lead = [bits.index(b) for b in step[::-1]] + [bits.index(b) for b in rest]
        front = front.transpose(lead + list(range(len(bits), front.ndim)))
        front = front.reshape((size,) + (2 ** len(rest),) + blocks.shape[1:])
        total = lax.dynamic_index_in_dim(front, mine, 0, keepdims=False)
        for p in range(1, size):
            give = lax.dynamic_index_in_dim(front, jnp.bitwise_xor(mine, p), 0, keepdims=False)
            total = total + exchanged(give, axis, mask_of(p, step))
        held = total
        bits = rest
    return held[0]

def summed_apart(parts, shared, axis, steps):
    count, height, size = parts.shape
    shared_rows = shared.reshape(height, -1)
    stacked = jnp.concatenate(
        [parts, jnp.broadcast_to(shared_rows[None], (count,) + shared_rows.shape)], 2
    )
    mine = summed_by_halving(stacked, axis, steps)
    return mine[:, :size], mine[:, size:].reshape(-1)

def on_device(
    branch_in, cotangent, weight_a, weight_x, conv_weight, conv_bias, bias_a, bias_x, rate
):
    inputs = branch_in[0]
    upstream = cotangent[0].astype(jnp.float32)
    length = inputs.shape[0]
    taps = conv_weight.shape[0]
    rows, cols = weight_a.shape
    dp_size = lax.axis_size("dp")
    ctx_size = lax.axis_size("ctx")
    packed = jnp.concatenate(
        [conv_weight, conv_bias[None], bias_a[None], bias_x[None], rate[None]], 0
    )
    width = ctx_size * cols
    head_width = dp_size * rows
    joined = jnp.concatenate([weight_a, weight_x, packed], 0)
    by_ctx = gathered_by_doubling(joined, "ctx", bit_steps(ctx_size))
    by_ctx = by_ctx.transpose(1, 0, 2).reshape(joined.shape[0], width)
    params = by_ctx[2 * rows :]
    heads = by_ctx[: 2 * rows].reshape(2 * rows, -1, head_width).transpose(1, 0, 2)
    by_dp = gathered_by_doubling(heads, "dp", bit_steps(dp_size)[::-1])
    head_count = heads.shape[0]

    def head_major(part):
        return part.transpose(1, 0, 2, 3).reshape(head_count, dp_size * rows, head_width)

    full_a = head_major(by_dp[:, :, :rows])
    full_x = head_major(by_dp[:, :, rows:])
    params = params.astype(jnp.float32)
    taps_f = params[:taps]
    cbias = params[taps]
    abias = params[taps + 1]
    xbias = params[taps + 2]
    rates = params[taps + 3]
    tail = passed_along(inputs[length - (taps - 1) :], "ctx", 1)
    padded = jnp.concatenate([tail, inputs], 0).astype(jnp.float32)
    conv = cbias
    for tap in range(taps):
        conv = conv + taps_f[tap] * padded[tap : tap + length]
    conv_b = conv.astype(jnp.bfloat16)
    conv_f = conv_b.astype(jnp.float32)
    recur_gate = jax.nn.sigmoid(mix_heads(conv_b, full_a) + abias)
    input_gate = jax.nn.sigmoid(mix_heads(conv_b, full_x) + xbias)
    log_decay = -8.0 * recur_gate * rates
    decay = jnp.exp(log_decay)
    one_minus = -jnp.expm1(2.0 * log_decay)
    multiplier = jnp.sqrt(jnp.maximum(one_minus, floor_value))
    drive = multiplier * input_gate * conv_f

    row_id = lax.broadcasted_iota(jnp.int32, (length, length), 0)
    col_id = lax.broadcasted_iota(jnp.int32, (length, length), 1)
    lower = (row_id >= col_id).astype(jnp.float32)
    upper = (row_id <= col_id).astype(jnp.float32)
    cum_log = jnp.dot(lower, log_decay, precision=exact)
    grow = jnp.exp(cum_log)
    shrink = jnp.exp(-cum_log)
    local_hidden = grow * jnp.dot(lower, shrink * drive, precision=exact)
    weighted_back = jnp.dot(upper, grow * upstream, precision=exact)
    local_back = shrink * weighted_back
    block_decay = grow[-1]
    state_in, back_in = block_prefix(block_decay, local_hidden[-1], weighted_back[0], "ctx")
    hidden = local_hidden + grow * state_in
    previous = jnp.concatenate([state_in[None], hidden[:-1]], 0)
    back = local_back + (block_decay * shrink) * back_in
    slope = jnp.where(one_minus > floor_value, 0.5 / multiplier, 0.0)
    d_mult = back * input_gate * conv_f
    d_log = back * previous * decay - 2.0 * decay * decay * d_mult * slope
    d_recur = (d_log * (-8.0 * rates) * recur_gate * (1.0 - recur_gate)).astype(jnp.bfloat16)
    d_input = (back * multiplier * conv_f * input_gate * (1.0 - input_gate)).astype(jnp.bfloat16)
    d_conv = (
        back * multiplier * input_gate + back_heads(d_recur, full_a) + back_heads(d_input, full_x)
    )
    following = passed_along(d_conv[: taps - 1], "ctx", -1)
    dpad = jnp.concatenate([d_conv, following], 0)
    grad_in = jnp.zeros((length, width), jnp.float32)
    for tap in range(taps):
        start = taps - 1 - tap
        grad_in = grad_in + taps_f[tap] * dpad[start : start + length]
    local_wgrad = grad_heads(conv_b, d_recur, head_width)
    local_rgrad = jnp.sum(d_log * (-8.0 * recur_gate), axis=0)
    by_row = local_wgrad.reshape(dp_size, rows, width)
    row_sum, rgrad = summed_apart(by_row, local_rgrad, "dp", digit_steps(dp_size))
    by_channel = row_sum.reshape(rows, ctx_size, cols).transpose(1, 0, 2)
    wgrad, rgrad = summed_apart(by_channel, rgrad, "ctx", digit_steps(ctx_size))
    return (grad_in.astype(jnp.bfloat16)[None], wgrad, rgrad)


def solution(mesh):
    placed = (
        P("dp", "ctx", None),
        P("dp", "ctx", None),
        P("dp", "ctx"),
        P("dp", "ctx"),
        P(None, "ctx"),
        P("ctx"),
        P("ctx"),
        P("ctx"),
        P("ctx"),
    )
    return jax.shard_map(
        on_device,
        mesh=mesh,
        in_specs=placed,
        out_specs=(P("dp", "ctx", None), P("dp", "ctx"), P()),
        check_vma=False,
    )
```

profile of v0, /device:TPU:6, one launch (start us, length us, event | category | flops | bytes accessed | tf_op | source)
XLA Modules:
  0.0 313.7 jit_solution(7417659089978247618)
XLA Ops:
  5.3 9.1 %collective-permute-start = (bf16[24,176]{1,0:T(8,128)(2,1)S(1)}, bf16[24,176]{1,0:T(8,128)(2,1)S(1)}, u32[]{:S(2)}, u32[]{:S(2)}) collective-permute-start(bf16[24,176]{1,0:T(8,128)(2,1)S(1)} %concatenate.21), channel_id=1, source_target_pairs={{0,1},{1,0},{2,3},{3,2},{4,5},{5,4},{6,7},{7,6},{8,9},{9,8},{10,11... | collective-permute-start | bytes 25352 | tf_op jit(solution)/shard_map/ppermute | solution.py:87
  16.1 14.5 %collective-permute-start.1 = (bf16[2,24,176]{2,1,0:T(8,128)(2,1)S(1)}, bf16[2,24,176]{2,1,0:T(8,128)(2,1)S(1)}, u32[]{:S(2)}, u32[]{:S(2)}) collective-permute-start(bf16[2,24,176]{2,1,0:T(8,128)(2,1)S(1)} %get-tuple-element.72), channel_id=1, source_target_pairs={{0,2},{1,3},{2,0},{3,1},{4,6},{5,7},{6,4},{7,5},{8,10},{9,11},{10,... | collective-permute-start | bytes 50696 | tf_op jit(solution)/shard_map/ppermute | solution.py:87
  32.5 2.7 collective-permute-start.2
  35.2 3.2 %collective-permute-done.2 = bf16[2,2,24,176]{3,2,1,0:T(8,128)(2,1)S(1)} collective-permute-done((bf16[2,2,24,176]{3,2,1,0:T(8,128)(2,1)S(1)}, bf16[2,2,24,176]{3,2,1,0:T(8,128)(2,1)S(1)}, u32[]{:S(2)}, u32[]{:S(2)}) %collective-permute-start.2) | collective-permute-done | bytes 33824 | tf_op jit(solution)/shard_map/ppermute | solution.py:87
  38.5 4.2 %collective-permute-start.3 = (bf16[2,2,2,24,176]{4,3,2,1,0:T(8,128)(2,1)S(1)}, bf16[2,2,2,24,176]{4,3,2,1,0:T(8,128)(2,1)S(1)}, u32[]{:S(2)}, u32[]{:S(2)}) collective-permute-start(bf16[2,2,2,24,176]{4,3,2,1,0:T(8,128)(2,1)S(1)} %get-tuple-element.55), channel_id=1, source_target_pairs={{0,8},{1,9},{2,10},{3,11},{4,12},{5,13},{6,14},{7,15},{8,0},{9,1},... | collective-permute-start | bytes 202760 | tf_op jit(solution)/shard_map/ppermute | solution.py:87
  42.8 3.8 %collective-permute-done.3 = bf16[2,2,2,24,176]{4,3,2,1,0:T(8,128)(2,1)S(1)} collective-permute-done((bf16[2,2,2,24,176]{4,3,2,1,0:T(8,128)(2,1)S(1)}, bf16[2,2,2,24,176]{4,3,2,1,0:T(8,128)(2,1)S(1)}, u32[]{:S(2)}, u32[]{:S(2)}) %collective-permute-start.3) | collective-permute-done | bytes 67616 | tf_op jit(solution)/shard_map/ppermute | solution.py:87
  47.1 5.1 %collective-permute-start.4 = (bf16[11,16,256]{2,0,1:T(8,128)(2,1)S(1)}, bf16[11,16,256]{2,0,1:T(8,128)(2,1)S(1)}, u32[]{:S(2)}, u32[]{:S(2)}) collective-permute-start(bf16[11,16,256]{2,0,1:T(8,128)(2,1)S(1)} %bitcast.197), channel_id=1, source_target_pairs={{0,256},{16,272},{32,288},{48,304},{64,320},{80,336},{96,352},{112... | collective-permute-start | bytes 270344 | tf_op jit(solution)/shard_map/ppermute | solution.py:87
  52.2 3.5 %collective-permute-done.4 = bf16[11,16,256]{2,0,1:T(8,128)(2,1)S(1)} collective-permute-done((bf16[11,16,256]{2,0,1:T(8,128)(2,1)S(1)}, bf16[11,16,256]{2,0,1:T(8,128)(2,1)S(1)}, u32[]{:S(2)}, u32[]{:S(2)}) %collective-permute-start.4) | collective-permute-done | bytes 90144 | tf_op jit(solution)/shard_map/ppermute | solution.py:87
  55.9 3.2 %collective-permute-start.5 = (bf16[2,11,16,256]{3,1,2,0:T(8,128)(2,1)S(1)}, bf16[2,11,16,256]{3,1,2,0:T(8,128)(2,1)S(1)}, u32[]{:S(2)}, u32[]{:S(2)}) collective-permute-start(bf16[2,11,16,256]{3,1,2,0:T(8,128)(2,1)S(1)} %get-tuple-element.48), channel_id=1, source_target_pairs={{0,128},{16,144},{32,160},{48,176},{64,192},{80,208},{96,224},{112... | collective-permute-start | bytes 540680 | tf_op jit(solution)/shard_map/ppermute | solution.py:87
  59.1 5.0 %collective-permute-done.5 = bf16[2,11,16,256]{3,1,2,0:T(8,128)(2,1)S(1)} collective-permute-done((bf16[2,11,16,256]{3,1,2,0:T(8,128)(2,1)S(1)}, bf16[2,11,16,256]{3,1,2,0:T(8,128)(2,1)S(1)}, u32[]{:S(2)}, u32[]{:S(2)}) %collective-permute-start.5) | collective-permute-done | bytes 180256 | tf_op jit(solution)/shard_map/ppermute | solution.py:87
  64.6 3.4 %collective-permute-start.6 = (bf16[2,2,11,16,256]{4,3,2,0,1:T(8,128)(2,1)S(1)}, bf16[2,2,11,16,256]{4,3,2,0,1:T(8,128)(2,1)S(1)}, u32[]{:S(2)}, u32[]{:S(2)}) collective-permute-start(bf16[2,2,11,16,256]{4,3,2,0,1:T(8,128)(2,1)S(1)} %get-tuple-element.43), channel_id=1, source_target_pairs={{0,64},{16,80},{32,96},{48,112},{64,0},{80,16},{96,32},{112,48},{1... | collective-permute-start | bytes 1081352 | tf_op jit(solution)/shard_map/ppermute | solution.py:87
  68.0 11.7 %collective-permute-done.6 = bf16[2,2,11,16,256]{4,3,2,0,1:T(8,128)(2,1)S(1)} collective-permute-done((bf16[2,2,11,16,256]{4,3,2,0,1:T(8,128)(2,1)S(1)}, bf16[2,2,11,16,256]{4,3,2,0,1:T(8,128)(2,1)S(1)}, u32[]{:S(2)}, u32[]{:S(2)}) %collective-permute-start.6) | collective-permute-done | bytes 360480 | tf_op jit(solution)/shard_map/ppermute | solution.py:87
  82.8 7.2 %collective-permute-start.9 = (bf16[3,2816]{1,0:T(4,128)(2,1)S(1)}, bf16[3,2816]{1,0:T(4,128)(2,1)S(1)}, u32[]{:S(2)}, u32[]{:S(2)}) collective-permute-start(bf16[3,2816]{1,0:T(4,128)(2,1)S(1)} %slice_bitcast_fusion.2), channel_id=1, source_target_pairs={{0,1},{1,2},{2,3},{3,4},{4,5},{5,6},{6,7},{7,8},{8,9},{9,10},{10,1... | collective-permute-start | bytes 50696 | tf_op jit(solution)/shard_map/ppermute | solution.py:13
  90.1 7.1 %collective-permute-done.7 = bf16[2,2,2,11,16,256]{5,4,3,1,0,2:T(8,128)(2,1)S(1)} collective-permute-done((bf16[2,2,2,11,16,256]{5,4,3,1,0,2:T(8,128)(2,1)S(1)}, bf16[2,2,2,11,16,256]{5,4,3,1,0,2:T(8,128)(2,1)S(1)}, u32[]{:S(2)}, u32[]{:S(2)}) %collective-permute-start.7) | collective-permute-done | bytes 720928 | tf_op jit(solution)/shard_map/ppermute | solution.py:87
  101.3 3.0 collective-permute-done.9
  109.3 2.4 fusion.17
  115.4 2.9 copy.127
  118.4 2.8 fusion.28
  121.2 3.0 copy.131
  125.8 2.8 convolution_multiply_fusion
  130.9 3.4 %collective-permute-start.10 = (f32[3,2816]{1,0:T(4,128)S(1)}, f32[3,2816]{1,0:T(4,128)S(1)}, u32[]{:S(2)}, u32[]{:S(2)}) collective-permute-start(f32[3,2816]{1,0:T(4,128)S(1)} %pad_maximum_fusion.10), channel_id=1, source_target_pairs={{0,1},{1,0},{2,3},{3,2},{4,5},{5,4},{6,7},{7,6},{8,9},{9,8},{10,11... | collective-permute-start | bytes 101384 | tf_op jit(solution)/shard_map/ppermute | solution.py:87
  134.3 7.0 %collective-permute-done.10 = f32[3,2816]{1,0:T(4,128)S(1)} collective-permute-done((f32[3,2816]{1,0:T(4,128)S(1)}, f32[3,2816]{1,0:T(4,128)S(1)}, u32[]{:S(2)}, u32[]{:S(2)}) %collective-permute-start.10) | collective-permute-done | bytes 33824 | tf_op jit(solution)/shard_map/ppermute | solution.py:87
  142.5 8.4 %collective-permute-start.11 = (f32[3,2816]{1,0:T(4,128)S(1)}, f32[3,2816]{1,0:T(4,128)S(1)}, u32[]{:S(2)}, u32[]{:S(2)}) collective-permute-start(f32[3,2816]{1,0:T(4,128)S(1)} %pad_maximum_fusion.11), channel_id=1, source_target_pairs={{0,2},{1,3},{2,0},{3,1},{4,6},{5,7},{6,4},{7,5},{8,10},{9,11},{10,... | collective-permute-start | bytes 101384 | tf_op jit(solution)/shard_map/ppermute | solution.py:87
  151.0 6.5 %collective-permute-done.11 = f32[3,2816]{1,0:T(4,128)S(1)} collective-permute-done((f32[3,2816]{1,0:T(4,128)S(1)}, f32[3,2816]{1,0:T(4,128)S(1)}, u32[]{:S(2)}, u32[]{:S(2)}) %collective-permute-start.11) | collective-permute-done | bytes 33824 | tf_op jit(solution)/shard_map/ppermute | solution.py:87
  157.6 2.5 collective-permute-start.12
  160.1 3.4 %collective-permute-done.12 = f32[3,2816]{1,0:T(4,128)S(1)} collective-permute-done((f32[3,2816]{1,0:T(4,128)S(1)}, f32[3,2816]{1,0:T(4,128)S(1)}, u32[]{:S(2)}, u32[]{:S(2)}) %collective-permute-start.12) | collective-permute-done | bytes 33824 | tf_op jit(solution)/shard_map/ppermute | solution.py:87
  163.6 4.7 %collective-permute-start.13 = (f32[3,2816]{1,0:T(4,128)S(1)}, f32[3,2816]{1,0:T(4,128)S(1)}, u32[]{:S(2)}, u32[]{:S(2)}) collective-permute-start(f32[3,2816]{1,0:T(4,128)S(1)} %pad_maximum_fusion.13), channel_id=1, source_target_pairs={{0,8},{1,9},{2,10},{3,11},{4,12},{5,13},{6,14},{7,15},{8,0},{9,1},... | collective-permute-start | bytes 101384 | tf_op jit(solution)/shard_map/ppermute | solution.py:87
  168.3 2.7 collective-permute-done.13
  174.3 4.6 %multiply_reduce_fusion = (f32[2816]{0:T(1024)S(1)}, f32[128,2816]{1,0:T(8,128)S(1)}, bf16[128,2816]{1,0:T(8,128)(2,1)}, f32[128,2816]{1,0:T(8,128)}) fusion(f32[128,2816]{1,0:T(8,128)S(1)} %copy-done.4, f32[2816]{0:T(1024)S(1)} %add.402, f32[128,2816]{1,0:T(8,128)S(1)} %copy-done.6, f32[2816]{0:T(1024)S(1)} %add.406, f32[2816]{0:T(1024)S(1)} %mul.339, ...), kind=kLoop, calls=%fused_computation.67 | loop fusion | flops 17659136 | bytes 16704512 | tf_op jit(solution)/shard_map/reduce_sum | solution.py:249
  182.4 3.4 %copy.139 = f32[256,11,256]{2,1,0:T(8,128)} copy(f32[256,11,256]{0,2,1:T(8,128)S(1)} %convolution_bitcast_fusion) | data formatting | bytes 5767168 | tf_op jit(solution)/shard_map/thk,thj->khj/transpose | solution.py:37
  185.8 4.7 %concatenate.25 = f32[2,2,2,2,2,8,2816]{6,5,4,3,2,1,0:T(8,128)} reshape(f32[256,11,256]{2,1,0:T(8,128)} %copy.139) | data formatting | bytes 5767168 | tf_op jit(solution)/shard_map/concatenate | solution.py:164
  198.1 3.7 %collective-permute-start.17 = (f32[8,8,3168]{2,1,0:T(8,128)}, f32[8,8,3168]{2,1,0:T(8,128)}, u32[]{:S(2)}, u32[]{:S(2)}) collective-permute-start(f32[8,8,3168]{2,1,0:T(8,128)} %get-tuple-element.20), channel_id=1, source_target_pairs={{0,48},{16,32},{32,16},{48,0},{64,112},{80,96},{96,80},{112,64},{1... | collective-permute-start | bytes 2433032 | tf_op jit(solution)/shard_map/ppermute | solution.py:87
  201.9 2.3 copy.135
  204.2 15.2 %collective-permute-done.16 = f32[8,8,3168]{2,1,0:T(8,128)} collective-permute-done((f32[8,8,3168]{2,1,0:T(8,128)}, f32[8,8,3168]{2,1,0:T(8,128)}, u32[]{:S(2)}, u32[]{:S(2)}) %collective-permute-start.16) | collective-permute-done | bytes 811040 | tf_op jit(solution)/shard_map/ppermute | solution.py:87
  219.4 16.8 %collective-permute-done.17 = f32[8,8,3168]{2,1,0:T(8,128)} collective-permute-done((f32[8,8,3168]{2,1,0:T(8,128)}, f32[8,8,3168]{2,1,0:T(8,128)}, u32[]{:S(2)}, u32[]{:S(2)}) %collective-permute-start.17) | collective-permute-done | bytes 811040 | tf_op jit(solution)/shard_map/ppermute | solution.py:87
  238.1 4.7 %collective-permute-start.18 = (f32[2,8,3168]{2,1,0:T(8,128)S(1)}, f32[2,8,3168]{2,1,0:T(8,128)S(1)}, u32[]{:S(2)}, u32[]{:S(2)}) collective-permute-start(f32[2,8,3168]{2,1,0:T(8,128)S(1)} %get-tuple-element.34), channel_id=1, source_target_pairs={{0,64},{16,80},{32,96},{48,112},{64,0},{80,16},{96,32},{112,48},{1... | collective-permute-start | bytes 608264 | tf_op jit(solution)/shard_map/ppermute | solution.py:87
  242.9 3.8 %collective-permute-start.19 = (f32[2,8,3168]{2,1,0:T(8,128)S(1)}, f32[2,8,3168]{2,1,0:T(8,128)S(1)}, u32[]{:S(2)}, u32[]{:S(2)}) collective-permute-start(f32[2,8,3168]{2,1,0:T(8,128)S(1)} %get-tuple-element.36), channel_id=1, source_target_pairs={{0,128},{16,144},{32,160},{48,176},{64,192},{80,208},{96,224},{112... | collective-permute-start | bytes 608264 | tf_op jit(solution)/shard_map/ppermute | solution.py:87
  249.1 7.9 %collective-permute-done.18 = f32[2,8,3168]{2,1,0:T(8,128)S(1)} collective-permute-done((f32[2,8,3168]{2,1,0:T(8,128)S(1)}, f32[2,8,3168]{2,1,0:T(8,128)S(1)}, u32[]{:S(2)}, u32[]{:S(2)}) %collective-permute-start.18) | collective-permute-done | bytes 202784 | tf_op jit(solution)/shard_map/ppermute | solution.py:87
  257.0 5.6 %collective-permute-done.20 = f32[2,8,3168]{2,1,0:T(8,128)S(1)} collective-permute-done((f32[2,8,3168]{2,1,0:T(8,128)S(1)}, f32[2,8,3168]{2,1,0:T(8,128)S(1)}, u32[]{:S(2)}, u32[]{:S(2)}) %collective-permute-start.20) | collective-permute-done | bytes 202784 | tf_op jit(solution)/shard_map/ppermute | solution.py:87
  268.3 2.6 collective-permute-done.21
  271.4 4.8 %collective-permute-start.22 = (f32[4,8,528]{2,1,0:T(8,128)S(1)}, f32[4,8,528]{2,1,0:T(8,128)S(1)}, u32[]{:S(2)}, u32[]{:S(2)}) collective-permute-start(f32[4,8,528]{2,1,0:T(8,128)S(1)} %get-tuple-element.45), channel_id=1, source_target_pairs={{0,1},{1,0},{2,3},{3,2},{4,5},{5,4},{6,7},{7,6},{8,9},{9,8},{10,11... | collective-permute-start | bytes 202760 | tf_op jit(solution)/shard_map/ppermute | solution.py:87
  276.3 9.7 %collective-permute-start.23 = (f32[4,8,528]{2,1,0:T(8,128)S(1)}, f32[4,8,528]{2,1,0:T(8,128)S(1)}, u32[]{:S(2)}, u32[]{:S(2)}) collective-permute-start(f32[4,8,528]{2,1,0:T(8,128)S(1)} %get-tuple-element.47), channel_id=1, source_target_pairs={{0,2},{1,3},{2,0},{3,1},{4,6},{5,7},{6,4},{7,5},{8,10},{9,11},{10,... | collective-permute-start | bytes 202760 | tf_op jit(solution)/shard_map/ppermute | solution.py:87
  285.9 2.5 collective-permute-start.24
  288.5 2.6 add_add_fusion
  291.1 7.7 %collective-permute-start.14 = (f32[3,2816]{1,0:T(4,128)S(1)}, f32[3,2816]{1,0:T(4,128)S(1)}, u32[]{:S(2)}, u32[]{:S(2)}) collective-permute-start(f32[3,2816]{1,0:T(4,128)S(1)} %slice.215), channel_id=1, source_target_pairs={{1,0},{2,1},{3,2},{4,3},{5,4},{6,5},{7,6},{8,7},{9,8},{10,9},{11,1... | collective-permute-start | bytes 101384 | tf_op jit(solution)/shard_map/ppermute | solution.py:13
  300.1 2.6 collective-permute-start.25
  302.7 2.6 collective-permute-start.26
  305.3 5.3 %collective-permute-start.27 = (f32[1,8,528]{2,1,0:T(8,128)S(1)}, f32[1,8,528]{2,1,0:T(8,128)S(1)}, u32[]{:S(2)}, u32[]{:S(2)}) collective-permute-start(f32[1,8,528]{2,1,0:T(8,128)S(1)} %get-tuple-element.60), channel_id=1, source_target_pairs={{0,12},{1,13},{2,14},{3,15},{4,8},{5,9},{6,10},{7,11},{8,4},{9,5},... | collective-permute-start | bytes 50696 | tf_op jit(solution)/shard_map/ppermute | solution.py:87
  (153 shorter events, 59.3 us)
Async XLA Ops:
  5.3 10.8 %collective-permute-start = (bf16[24,176]{1,0:T(8,128)(2,1)S(1)}, bf16[24,176]{1,0:T(8,128)(2,1)S(1)}, u32[]{:S(2)}, u32[]{:S(2)}) collective-permute-start(bf16[24,176]{1,0:T(8,128)(2,1)S(1)} %concatenate.21), channel_id=1, source_target_pairs={{0,1},{1,0},{2,3},{3,2},{4,5},{5,4},{6,7},{7,6},{8,9},{9,8},{10,11... | collective-permute-start | bytes 25352 | tf_op jit(solution)/shard_map/ppermute | solution.py:87
  16.1 16.3 %collective-permute-start.1 = (bf16[2,24,176]{2,1,0:T(8,128)(2,1)S(1)}, bf16[2,24,176]{2,1,0:T(8,128)(2,1)S(1)}, u32[]{:S(2)}, u32[]{:S(2)}) collective-permute-start(bf16[2,24,176]{2,1,0:T(8,128)(2,1)S(1)} %get-tuple-element.72), channel_id=1, source_target_pairs={{0,2},{1,3},{2,0},{3,1},{4,6},{5,7},{6,4},{7,5},{8,10},{9,11},{10,... | collective-permute-start | bytes 50696 | tf_op jit(solution)/shard_map/ppermute | solution.py:87
  32.5 6.0 %collective-permute-start.2 = (bf16[2,2,24,176]{3,2,1,0:T(8,128)(2,1)S(1)}, bf16[2,2,24,176]{3,2,1,0:T(8,128)(2,1)S(1)}, u32[]{:S(2)}, u32[]{:S(2)}) collective-permute-start(bf16[2,2,24,176]{3,2,1,0:T(8,128)(2,1)S(1)} %get-tuple-element.68), channel_id=1, source_target_pairs={{0,4},{1,5},{2,6},{3,7},{4,0},{5,1},{6,2},{7,3},{8,12},{9,13},{10,... | collective-permute-start | bytes 101384 | tf_op jit(solution)/shard_map/ppermute | solution.py:87
  38.5 8.0 %collective-permute-start.3 = (bf16[2,2,2,24,176]{4,3,2,1,0:T(8,128)(2,1)S(1)}, bf16[2,2,2,24,176]{4,3,2,1,0:T(8,128)(2,1)S(1)}, u32[]{:S(2)}, u32[]{:S(2)}) collective-permute-start(bf16[2,2,2,24,176]{4,3,2,1,0:T(8,128)(2,1)S(1)} %get-tuple-element.55), channel_id=1, source_target_pairs={{0,8},{1,9},{2,10},{3,11},{4,12},{5,13},{6,14},{7,15},{8,0},{9,1},... | collective-permute-start | bytes 202760 | tf_op jit(solution)/shard_map/ppermute | solution.py:87
  47.1 8.7 %collective-permute-start.4 = (bf16[11,16,256]{2,0,1:T(8,128)(2,1)S(1)}, bf16[11,16,256]{2,0,1:T(8,128)(2,1)S(1)}, u32[]{:S(2)}, u32[]{:S(2)}) collective-permute-start(bf16[11,16,256]{2,0,1:T(8,128)(2,1)S(1)} %bitcast.197), channel_id=1, source_target_pairs={{0,256},{16,272},{32,288},{48,304},{64,320},{80,336},{96,352},{112... | collective-permute-start | bytes 270344 | tf_op jit(solution)/shard_map/ppermute | solution.py:87
  55.9 8.3 %collective-permute-start.5 = (bf16[2,11,16,256]{3,1,2,0:T(8,128)(2,1)S(1)}, bf16[2,11,16,256]{3,1,2,0:T(8,128)(2,1)S(1)}, u32[]{:S(2)}, u32[]{:S(2)}) collective-permute-start(bf16[2,11,16,256]{3,1,2,0:T(8,128)(2,1)S(1)} %get-tuple-element.48), channel_id=1, source_target_pairs={{0,128},{16,144},{32,160},{48,176},{64,192},{80,208},{96,224},{112... | collective-permute-start | bytes 540680 | tf_op jit(solution)/shard_map/ppermute | solution.py:87
  64.6 15.1 %collective-permute-start.6 = (bf16[2,2,11,16,256]{4,3,2,0,1:T(8,128)(2,1)S(1)}, bf16[2,2,11,16,256]{4,3,2,0,1:T(8,128)(2,1)S(1)}, u32[]{:S(2)}, u32[]{:S(2)}) collective-permute-start(bf16[2,2,11,16,256]{4,3,2,0,1:T(8,128)(2,1)S(1)} %get-tuple-element.43), channel_id=1, source_target_pairs={{0,64},{16,80},{32,96},{48,112},{64,0},{80,16},{96,32},{112,48},{1... | collective-permute-start | bytes 1081352 | tf_op jit(solution)/shard_map/ppermute | solution.py:87
  80.1 17.1 %collective-permute-start.7 = (bf16[2,2,2,11,16,256]{5,4,3,1,0,2:T(8,128)(2,1)S(1)}, bf16[2,2,2,11,16,256]{5,4,3,1,0,2:T(8,128)(2,1)S(1)}, u32[]{:S(2)}, u32[]{:S(2)}) collective-permute-start(bf16[2,2,2,11,16,256]{5,4,3,1,0,2:T(8,128)(2,1)S(1)} %get-tuple-element.37), channel_id=1, source_target_pairs={{0,32},{16,48},{32,0},{48,16},{64,96},{80,112},{96,64},{112,80},{1... | collective-permute-start | bytes 2162696 | tf_op jit(solution)/shard_map/ppermute | solution.py:87
  82.8 21.5 %collective-permute-start.9 = (bf16[3,2816]{1,0:T(4,128)(2,1)S(1)}, bf16[3,2816]{1,0:T(4,128)(2,1)S(1)}, u32[]{:S(2)}, u32[]{:S(2)}) collective-permute-start(bf16[3,2816]{1,0:T(4,128)(2,1)S(1)} %slice_bitcast_fusion.2), channel_id=1, source_target_pairs={{0,1},{1,2},{2,3},{3,4},{4,5},{5,6},{6,7},{7,8},{8,9},{9,10},{10,1... | collective-permute-start | bytes 50696 | tf_op jit(solution)/shard_map/ppermute | solution.py:13
  97.9 6.4 %copy-start.18 = (bf16[1,128,2816]{2,1,0:T(8,128)(2,1)S(1)}, bf16[1,128,2816]{2,1,0:T(8,128)(2,1)}, u32[]{:S(2)}) copy-start(bf16[1,128,2816]{2,1,0:T(8,128)(2,1)} %param.9) | copy-start | bytes 2162692
  99.2 10.1 %collective-permute-start.8 = (bf16[2,2,2,2,11,16,256]{6,5,4,2,1,0,3:T(8,128)(2,1)}, bf16[2,2,2,2,11,16,256]{6,5,4,2,1,0,3:T(8,128)(2,1)}, u32[]{:S(2)}, u32[]{:S(2)}) collective-permute-start(bf16[2,2,2,2,11,16,256]{6,5,4,2,1,0,3:T(8,128)(2,1)} %get-tuple-element.30), channel_id=1, source_target_pairs={{0,16},{16,0},{32,48},{48,32},{64,80},{80,64},{96,112},{112,96},{1... | collective-permute-start | bytes 4325384 | tf_op jit(solution)/shard_map/ppermute | solution.py:87
  112.6 1.1 copy-start.8
  112.8 2.6 copy-start.2
  112.8 5.6 %copy-start = (bf16[11,32,8,256]{3,2,0,1:T(8,128)(2,1)}, bf16[11,32,8,256]{3,2,0,1:T(8,128)(2,1)S(1)}, u32[]{:S(2)}) copy-start(bf16[11,32,8,256]{3,2,0,1:T(8,128)(2,1)S(1)} %get-tuple-element.23) | copy-start | bytes 4325380
  121.2 3.0 copy-start.4
  124.2 1.4 copy-start.5
  124.2 1.5 copy-start.15
  125.5 3.0 copy-start.12
  125.5 5.3 %copy-start.17 = (f32[128,2816]{1,0:T(8,128)}, f32[128,2816]{1,0:T(8,128)S(1)}, u32[]{:S(2)}) copy-start(f32[128,2816]{1,0:T(8,128)S(1)} %get-tuple-element.76) | copy-start | bytes 4325380
  125.8 2.8 copy-start.19
  128.5 1.2 copy-start.16
  129.7 1.1 copy-start.10
  130.9 10.5 %collective-permute-start.10 = (f32[3,2816]{1,0:T(4,128)S(1)}, f32[3,2816]{1,0:T(4,128)S(1)}, u32[]{:S(2)}, u32[]{:S(2)}) collective-permute-start(f32[3,2816]{1,0:T(4,128)S(1)} %pad_maximum_fusion.10), channel_id=1, source_target_pairs={{0,1},{1,0},{2,3},{3,2},{4,5},{5,4},{6,7},{7,6},{8,9},{9,8},{10,11... | collective-permute-start | bytes 101384 | tf_op jit(solution)/shard_map/ppermute | solution.py:87
  142.5 15.0 %collective-permute-start.11 = (f32[3,2816]{1,0:T(4,128)S(1)}, f32[3,2816]{1,0:T(4,128)S(1)}, u32[]{:S(2)}, u32[]{:S(2)}) collective-permute-start(f32[3,2816]{1,0:T(4,128)S(1)} %pad_maximum_fusion.11), channel_id=1, source_target_pairs={{0,2},{1,3},{2,0},{3,1},{4,6},{5,7},{6,4},{7,5},{8,10},{9,11},{10,... | collective-permute-start | bytes 101384 | tf_op jit(solution)/shard_map/ppermute | solution.py:87
  157.6 5.9 %collective-permute-start.12 = (f32[3,2816]{1,0:T(4,128)S(1)}, f32[3,2816]{1,0:T(4,128)S(1)}, u32[]{:S(2)}, u32[]{:S(2)}) collective-permute-start(f32[3,2816]{1,0:T(4,128)S(1)} %pad_maximum_fusion.12), channel_id=1, source_target_pairs={{0,4},{1,5},{2,6},{3,7},{4,0},{5,1},{6,2},{7,3},{8,12},{9,13},{10,... | collective-permute-start | bytes 101384 | tf_op jit(solution)/shard_map/ppermute | solution.py:87
  163.6 7.4 %collective-permute-start.13 = (f32[3,2816]{1,0:T(4,128)S(1)}, f32[3,2816]{1,0:T(4,128)S(1)}, u32[]{:S(2)}, u32[]{:S(2)}) collective-permute-start(f32[3,2816]{1,0:T(4,128)S(1)} %pad_maximum_fusion.13), channel_id=1, source_target_pairs={{0,8},{1,9},{2,10},{3,11},{4,12},{5,13},{6,14},{7,15},{8,0},{9,1},... | collective-permute-start | bytes 101384 | tf_op jit(solution)/shard_map/ppermute | solution.py:87
  171.2 2.2 copy-start.6
  171.3 2.7 copy-start.11
  171.3 3.1 copy-start.13
  194.2 9.9 %collective-permute-start.15 = (f32[8,8,3168]{2,1,0:T(8,128)}, f32[8,8,3168]{2,1,0:T(8,128)}, u32[]{:S(2)}, u32[]{:S(2)}) collective-permute-start(f32[8,8,3168]{2,1,0:T(8,128)} %get-tuple-element.19), channel_id=1, source_target_pairs={{0,16},{16,0},{32,48},{48,32},{64,80},{80,64},{96,112},{112,96},{1... | collective-permute-start | bytes 2433032 | tf_op jit(solution)/shard_map/ppermute | solution.py:87
  196.1 23.3 %collective-permute-start.16 = (f32[8,8,3168]{2,1,0:T(8,128)}, f32[8,8,3168]{2,1,0:T(8,128)}, u32[]{:S(2)}, u32[]{:S(2)}) collective-permute-start(f32[8,8,3168]{2,1,0:T(8,128)} %get-tuple-element.21), channel_id=1, source_target_pairs={{0,32},{16,48},{32,0},{48,16},{64,96},{80,112},{96,64},{112,80},{1... | collective-permute-start | bytes 2433032 | tf_op jit(solution)/shard_map/ppermute | solution.py:87
  198.1 38.1 %collective-permute-start.17 = (f32[8,8,3168]{2,1,0:T(8,128)}, f32[8,8,3168]{2,1,0:T(8,128)}, u32[]{:S(2)}, u32[]{:S(2)}) collective-permute-start(f32[8,8,3168]{2,1,0:T(8,128)} %get-tuple-element.20), channel_id=1, source_target_pairs={{0,48},{16,32},{32,16},{48,0},{64,112},{80,96},{96,80},{112,64},{1... | collective-permute-start | bytes 2433032 | tf_op jit(solution)/shard_map/ppermute | solution.py:87
  236.2 12.4 %copy-start.3 = (bf16[11,32,8,256]{3,2,0,1:T(8,128)(2,1)S(1)}, bf16[11,32,8,256]{3,2,0,1:T(8,128)(2,1)}, u32[]{:S(2)}) copy-start(bf16[11,32,8,256]{3,2,0,1:T(8,128)(2,1)} %copy-done.2) | copy-start | bytes 4325380
  238.1 10.5 %copy-start.9 = (bf16[128,2816]{0,1:T(8,128)(2,1)S(1)}, bf16[128,2816]{0,1:T(8,128)(2,1)}, u32[]{:S(2)}) copy-start(bf16[128,2816]{0,1:T(8,128)(2,1)} %copy.132) | copy-start | bytes 2162692
  238.1 18.9 %collective-permute-start.18 = (f32[2,8,3168]{2,1,0:T(8,128)S(1)}, f32[2,8,3168]{2,1,0:T(8,128)S(1)}, u32[]{:S(2)}, u32[]{:S(2)}) collective-permute-start(f32[2,8,3168]{2,1,0:T(8,128)S(1)} %get-tuple-element.34), channel_id=1, source_target_pairs={{0,64},{16,80},{32,96},{48,112},{64,0},{80,16},{96,32},{112,48},{1... | collective-permute-start | bytes 608264 | tf_op jit(solution)/shard_map/ppermute | solution.py:87
  242.9 14.2 %collective-permute-start.19 = (f32[2,8,3168]{2,1,0:T(8,128)S(1)}, f32[2,8,3168]{2,1,0:T(8,128)S(1)}, u32[]{:S(2)}, u32[]{:S(2)}) collective-permute-start(f32[2,8,3168]{2,1,0:T(8,128)S(1)} %get-tuple-element.36), channel_id=1, source_target_pairs={{0,128},{16,144},{32,160},{48,176},{64,192},{80,208},{96,224},{112... | collective-permute-start | bytes 608264 | tf_op jit(solution)/shard_map/ppermute | solution.py:87
  246.6 16.0 %collective-permute-start.20 = (f32[2,8,3168]{2,1,0:T(8,128)S(1)}, f32[2,8,3168]{2,1,0:T(8,128)S(1)}, u32[]{:S(2)}, u32[]{:S(2)}) collective-permute-start(f32[2,8,3168]{2,1,0:T(8,128)S(1)} %get-tuple-element.35), channel_id=1, source_target_pairs={{0,192},{16,208},{32,224},{48,240},{64,128},{80,144},{96,160},{112... | collective-permute-start | bytes 608264 | tf_op jit(solution)/shard_map/ppermute | solution.py:87
  248.6 16.1 %copy-start.1 = (bf16[11,32,8,256]{3,2,0,1:T(8,128)(2,1)S(1)}, bf16[11,32,8,256]{3,2,0,1:T(8,128)(2,1)}, u32[]{:S(2)}) copy-start(bf16[11,32,8,256]{3,2,0,1:T(8,128)(2,1)} %copy-done) | copy-start | bytes 4325380
  249.1 15.5 %copy-start.14 = (bf16[128,2816]{0,1:T(8,128)(2,1)S(1)}, bf16[128,2816]{0,1:T(8,128)(2,1)}, u32[]{:S(2)}) copy-start(bf16[128,2816]{0,1:T(8,128)(2,1)} %copy.135) | copy-start | bytes 2162692
  262.7 8.2 %collective-permute-start.21 = (f32[1,8,3168]{2,1,0:T(8,128)S(1)}, f32[1,8,3168]{2,1,0:T(8,128)S(1)}, u32[]{:S(2)}, u32[]{:S(2)}) collective-permute-start(f32[1,8,3168]{2,1,0:T(8,128)S(1)} %constant_dynamic-slice_fusion.3), channel_id=1, source_target_pairs={{0,256},{16,272},{32,288},{48,304},{64,320},{80,336},{96,352},{112... | collective-permute-start | bytes 304136 | tf_op jit(solution)/shard_map/ppermute | solution.py:87
  268.3 20.1 %copy-start.7 = (f32[128,2816]{1,0:T(8,128)S(1)}, f32[128,2816]{1,0:T(8,128)}, u32[]{:S(2)}) copy-start(f32[128,2816]{1,0:T(8,128)} %copy.131) | copy-start | bytes 4325380
  271.4 27.4 %collective-permute-start.22 = (f32[4,8,528]{2,1,0:T(8,128)S(1)}, f32[4,8,528]{2,1,0:T(8,128)S(1)}, u32[]{:S(2)}, u32[]{:S(2)}) collective-permute-start(f32[4,8,528]{2,1,0:T(8,128)S(1)} %get-tuple-element.45), channel_id=1, source_target_pairs={{0,1},{1,0},{2,3},{3,2},{4,5},{5,4},{6,7},{7,6},{8,9},{9,8},{10,11... | collective-permute-start | bytes 202760 | tf_op jit(solution)/shard_map/ppermute | solution.py:87
  276.3 22.6 %collective-permute-start.23 = (f32[4,8,528]{2,1,0:T(8,128)S(1)}, f32[4,8,528]{2,1,0:T(8,128)S(1)}, u32[]{:S(2)}, u32[]{:S(2)}) collective-permute-start(f32[4,8,528]{2,1,0:T(8,128)S(1)} %get-tuple-element.47), channel_id=1, source_target_pairs={{0,2},{1,3},{2,0},{3,1},{4,6},{5,7},{6,4},{7,5},{8,10},{9,11},{10,... | collective-permute-start | bytes 202760 | tf_op jit(solution)/shard_map/ppermute | solution.py:87
  285.9 14.1 %collective-permute-start.24 = (f32[4,8,528]{2,1,0:T(8,128)S(1)}, f32[4,8,528]{2,1,0:T(8,128)S(1)}, u32[]{:S(2)}, u32[]{:S(2)}) collective-permute-start(f32[4,8,528]{2,1,0:T(8,128)S(1)} %get-tuple-element.46), channel_id=1, source_target_pairs={{0,3},{1,2},{2,1},{3,0},{4,7},{5,6},{6,5},{7,4},{8,11},{9,10},{10,... | collective-permute-start | bytes 202760 | tf_op jit(solution)/shard_map/ppermute | solution.py:87
  291.1 19.4 %collective-permute-start.14 = (f32[3,2816]{1,0:T(4,128)S(1)}, f32[3,2816]{1,0:T(4,128)S(1)}, u32[]{:S(2)}, u32[]{:S(2)}) collective-permute-start(f32[3,2816]{1,0:T(4,128)S(1)} %slice.215), channel_id=1, source_target_pairs={{1,0},{2,1},{3,2},{4,3},{5,4},{6,5},{7,6},{8,7},{9,8},{10,9},{11,1... | collective-permute-start | bytes 101384 | tf_op jit(solution)/shard_map/ppermute | solution.py:13
  300.1 12.0 %collective-permute-start.25 = (f32[1,8,528]{2,1,0:T(8,128)S(1)}, f32[1,8,528]{2,1,0:T(8,128)S(1)}, u32[]{:S(2)}, u32[]{:S(2)}) collective-permute-start(f32[1,8,528]{2,1,0:T(8,128)S(1)} %get-tuple-element.59), channel_id=1, source_target_pairs={{0,4},{1,5},{2,6},{3,7},{4,0},{5,1},{6,2},{7,3},{8,12},{9,13},{10,... | collective-permute-start | bytes 50696 | tf_op jit(solution)/shard_map/ppermute | solution.py:87
  302.7 9.4 %collective-permute-start.26 = (f32[1,8,528]{2,1,0:T(8,128)S(1)}, f32[1,8,528]{2,1,0:T(8,128)S(1)}, u32[]{:S(2)}, u32[]{:S(2)}) collective-permute-start(f32[1,8,528]{2,1,0:T(8,128)S(1)} %get-tuple-element.61), channel_id=1, source_target_pairs={{0,8},{1,9},{2,10},{3,11},{4,12},{5,13},{6,14},{7,15},{8,0},{9,1},... | collective-permute-start | bytes 50696 | tf_op jit(solution)/shard_map/ppermute | solution.py:87
  305.3 7.0 %collective-permute-start.27 = (f32[1,8,528]{2,1,0:T(8,128)S(1)}, f32[1,8,528]{2,1,0:T(8,128)S(1)}, u32[]{:S(2)}, u32[]{:S(2)}) collective-permute-start(f32[1,8,528]{2,1,0:T(8,128)S(1)} %get-tuple-element.60), channel_id=1, source_target_pairs={{0,12},{1,13},{2,14},{3,15},{4,8},{5,9},{6,10},{7,11},{8,4},{9,5},... | collective-permute-start | bytes 50696 | tf_op jit(solution)/shard_map/ppermute | solution.py:87
where the time goes:
time: 318 us; the launch traced here: 314 us
  starting transfers between devices  127 us (40%)
  waiting for transfers between devices  110 us (35%)
  local copies, waits for them, and re-layouts  37 us (12%)
  other arithmetic  24.7 us (8%)
  matrix products  12.6 us (4%)
    ppermute x26, starting transfers between devices, exchanged(): return lax.ppermute(array, axis, [(i, i ^ mask) for i in range(length)])  113 us
    ppermute x26, waiting for transfers between devices, exchanged(): return lax.ppermute(array, axis, [(i, i ^ mask) for i in range(length)])  107 us
    ppermute x2, starting transfers between devices, passed_along(): return lax.ppermute(array, axis, pairs)  14.9 us
  transfers between devices with their start and end apart: 28, of which 20 were waited for; matrix products, arithmetic and copies ran while one was open for 6% of the time, Pallas kernels for 0%

commit v1 on v0

--- a/solution.py
+++ b/solution.py
@@ -69,6 +69,11 @@
         stride *= 2
     return before[1], after[1]
 
+def core_first_steps(length):
+    bits = [stride for step in digit_steps(length) for stride in step]
+    return [bits[:1]] + [bits[i : i + 2] for i in range(1, len(bits), 2)]
+
+
 def bit_steps(length):
     return [[stride] for step in digit_steps(length) for stride in step]
 
@@ -248,7 +253,7 @@
     local_wgrad = grad_heads(conv_b, d_recur, head_width)
     local_rgrad = jnp.sum(d_log * (-8.0 * recur_gate), axis=0)
     by_row = local_wgrad.reshape(dp_size, rows, width)
-    row_sum, rgrad = summed_apart(by_row, local_rgrad, "dp", digit_steps(dp_size))
+    row_sum, rgrad = summed_apart(by_row, local_rgrad, "dp", core_first_steps(dp_size))
     by_channel = row_sum.reshape(rows, ctx_size, cols).transpose(1, 0, 2)
     wgrad, rgrad = summed_apart(by_channel, rgrad, "ctx", digit_steps(ctx_size))
     return (grad_in.astype(jnp.bfloat16)[None], wgrad, rgrad)

time: 318 us -> 310 us (0.975)
  the two profiles are of different devices: /device:TPU:6 before, /device:TPU:64 now
where the time goes in v1:
time: 310 us; the launch traced here: 309 us
  starting transfers between devices  145 us (47%)
  waiting for transfers between devices  81.4 us (26%)
  local copies, waits for them, and re-layouts  39.4 us (13%)
  other arithmetic  26.9 us (9%)
  matrix products  13.8 us (4%)
    ppermute x26, starting transfers between devices, exchanged(): return lax.ppermute(array, axis, [(i, i ^ mask) for i in range(length)])  137 us
    ppermute x26, waiting for transfers between devices, exchanged(): return lax.ppermute(array, axis, [(i, i ^ mask) for i in range(length)])  81.4 us
    ppermute x2, starting transfers between devices, passed_along(): return lax.ppermute(array, axis, pairs)  8.84 us
  transfers between devices with their start and end apart: 28, of which 18 were waited for; matrix products, arithmetic and copies ran while one was open for 6% of the time, Pallas kernels for 0%

profile of v1, /device:TPU:64, one launch (start us, length us, event | category | flops | bytes accessed | tf_op | source)
XLA Modules:
  0.0 308.8 jit_solution(1068888952646726007)
XLA Ops:
  3.3 2.1 concatenate.21
  5.3 9.1 %collective-permute-start = (bf16[24,176]{1,0:T(8,128)(2,1)S(1)}, bf16[24,176]{1,0:T(8,128)(2,1)S(1)}, u32[]{:S(2)}, u32[]{:S(2)}) collective-permute-start(bf16[24,176]{1,0:T(8,128)(2,1)S(1)} %concatenate.21), channel_id=1, source_target_pairs={{0,1},{1,0},{2,3},{3,2},{4,5},{5,4},{6,7},{7,6},{8,9},{9,8},{10,11... | collective-permute-start | bytes 25352 | tf_op jit(solution)/shard_map/ppermute | solution.py:92
  16.1 12.7 %collective-permute-start.1 = (bf16[2,24,176]{2,1,0:T(8,128)(2,1)S(1)}, bf16[2,24,176]{2,1,0:T(8,128)(2,1)S(1)}, u32[]{:S(2)}, u32[]{:S(2)}) collective-permute-start(bf16[2,24,176]{2,1,0:T(8,128)(2,1)S(1)} %get-tuple-element.72), channel_id=1, source_target_pairs={{0,2},{1,3},{2,0},{3,1},{4,6},{5,7},{6,4},{7,5},{8,10},{9,11},{10,... | collective-permute-start | bytes 50696 | tf_op jit(solution)/shard_map/ppermute | solution.py:92
  30.7 3.4 %collective-permute-start.2 = (bf16[2,2,24,176]{3,2,1,0:T(8,128)(2,1)S(1)}, bf16[2,2,24,176]{3,2,1,0:T(8,128)(2,1)S(1)}, u32[]{:S(2)}, u32[]{:S(2)}) collective-permute-start(bf16[2,2,24,176]{3,2,1,0:T(8,128)(2,1)S(1)} %get-tuple-element.68), channel_id=1, source_target_pairs={{0,4},{1,5},{2,6},{3,7},{4,0},{5,1},{6,2},{7,3},{8,12},{9,13},{10,... | collective-permute-start | bytes 101384 | tf_op jit(solution)/shard_map/ppermute | solution.py:92
  34.1 2.5 collective-permute-done.2
  36.7 4.9 %collective-permute-start.3 = (bf16[2,2,2,24,176]{4,3,2,1,0:T(8,128)(2,1)S(1)}, bf16[2,2,2,24,176]{4,3,2,1,0:T(8,128)(2,1)S(1)}, u32[]{:S(2)}, u32[]{:S(2)}) collective-permute-start(bf16[2,2,2,24,176]{4,3,2,1,0:T(8,128)(2,1)S(1)} %get-tuple-element.55), channel_id=1, source_target_pairs={{0,8},{1,9},{2,10},{3,11},{4,12},{5,13},{6,14},{7,15},{8,0},{9,1},... | collective-permute-start | bytes 202760 | tf_op jit(solution)/shard_map/ppermute | solution.py:92
  41.7 3.0 collective-permute-done.3
  45.3 5.1 %collective-permute-start.4 = (bf16[11,16,256]{2,0,1:T(8,128)(2,1)S(1)}, bf16[11,16,256]{2,0,1:T(8,128)(2,1)S(1)}, u32[]{:S(2)}, u32[]{:S(2)}) collective-permute-start(bf16[11,16,256]{2,0,1:T(8,128)(2,1)S(1)} %bitcast.189), channel_id=1, source_target_pairs={{0,256},{16,272},{32,288},{48,304},{64,320},{80,336},{96,352},{112... | collective-permute-start | bytes 270344 | tf_op jit(solution)/shard_map/ppermute | solution.py:92
  50.4 3.5 %collective-permute-done.4 = bf16[11,16,256]{2,0,1:T(8,128)(2,1)S(1)} collective-permute-done((bf16[11,16,256]{2,0,1:T(8,128)(2,1)S(1)}, bf16[11,16,256]{2,0,1:T(8,128)(2,1)S(1)}, u32[]{:S(2)}, u32[]{:S(2)}) %collective-permute-start.4) | collective-permute-done | bytes 90144 | tf_op jit(solution)/shard_map/ppermute | solution.py:92
  54.1 3.2 %collective-permute-start.5 = (bf16[2,11,16,256]{3,1,2,0:T(8,128)(2,1)S(1)}, bf16[2,11,16,256]{3,1,2,0:T(8,128)(2,1)S(1)}, u32[]{:S(2)}, u32[]{:S(2)}) collective-permute-start(bf16[2,11,16,256]{3,1,2,0:T(8,128)(2,1)S(1)} %get-tuple-element.48), channel_id=1, source_target_pairs={{0,128},{16,144},{32,160},{48,176},{64,192},{80,208},{96,224},{112... | collective-permute-start | bytes 540680 | tf_op jit(solution)/shard_map/ppermute | solution.py:92
  57.3 5.0 %collective-permute-done.5 = bf16[2,11,16,256]{3,1,2,0:T(8,128)(2,1)S(1)} collective-permute-done((bf16[2,11,16,256]{3,1,2,0:T(8,128)(2,1)S(1)}, bf16[2,11,16,256]{3,1,2,0:T(8,128)(2,1)S(1)}, u32[]{:S(2)}, u32[]{:S(2)}) %collective-permute-start.5) | collective-permute-done | bytes 180256 | tf_op jit(solution)/shard_map/ppermute | solution.py:92
  62.8 6.4 %collective-permute-start.6 = (bf16[2,2,11,16,256]{4,3,2,0,1:T(8,128)(2,1)S(1)}, bf16[2,2,11,16,256]{4,3,2,0,1:T(8,128)(2,1)S(1)}, u32[]{:S(2)}, u32[]{:S(2)}) collective-permute-start(bf16[2,2,11,16,256]{4,3,2,0,1:T(8,128)(2,1)S(1)} %get-tuple-element.43), channel_id=1, source_target_pairs={{0,64},{16,80},{32,96},{48,112},{64,0},{80,16},{96,32},{112,48},{1... | collective-permute-start | bytes 1081352 | tf_op jit(solution)/shard_map/ppermute | solution.py:92
  69.2 7.0 %collective-permute-done.6 = bf16[2,2,11,16,256]{4,3,2,0,1:T(8,128)(2,1)S(1)} collective-permute-done((bf16[2,2,11,16,256]{4,3,2,0,1:T(8,128)(2,1)S(1)}, bf16[2,2,11,16,256]{4,3,2,0,1:T(8,128)(2,1)S(1)}, u32[]{:S(2)}, u32[]{:S(2)}) %collective-permute-start.6) | collective-permute-done | bytes 360480 | tf_op jit(solution)/shard_map/ppermute | solution.py:92
  76.7 5.1 %collective-permute-start.7 = (bf16[2,2,2,11,16,256]{5,4,3,1,0,2:T(8,128)(2,1)S(1)}, bf16[2,2,2,11,16,256]{5,4,3,1,0,2:T(8,128)(2,1)S(1)}, u32[]{:S(2)}, u32[]{:S(2)}) collective-permute-start(bf16[2,2,2,11,16,256]{5,4,3,1,0,2:T(8,128)(2,1)S(1)} %get-tuple-element.34), channel_id=1, source_target_pairs={{0,32},{16,48},{32,0},{48,16},{64,96},{80,112},{96,64},{112,80},{1... | collective-permute-start | bytes 2162696 | tf_op jit(solution)/shard_map/ppermute | solution.py:92
  82.6 7.6 %collective-permute-start.9 = (bf16[3,2816]{1,0:T(4,128)(2,1)S(1)}, bf16[3,2816]{1,0:T(4,128)(2,1)S(1)}, u32[]{:S(2)}, u32[]{:S(2)}) collective-permute-start(bf16[3,2816]{1,0:T(4,128)(2,1)S(1)} %slice_bitcast_fusion.2), channel_id=1, source_target_pairs={{0,1},{1,2},{2,3},{3,4},{4,5},{5,6},{6,7},{7,8},{8,9},{9,10},{10,1... | collective-permute-start | bytes 50696 | tf_op jit(solution)/shard_map/ppermute | solution.py:13
  90.2 3.5 %collective-permute-done.7 = bf16[2,2,2,11,16,256]{5,4,3,1,0,2:T(8,128)(2,1)S(1)} collective-permute-done((bf16[2,2,2,11,16,256]{5,4,3,1,0,2:T(8,128)(2,1)S(1)}, bf16[2,2,2,11,16,256]{5,4,3,1,0,2:T(8,128)(2,1)S(1)}, u32[]{:S(2)}, u32[]{:S(2)}) %collective-permute-start.7) | collective-permute-done | bytes 720928 | tf_op jit(solution)/shard_map/ppermute | solution.py:92
  95.7 2.1 collective-permute-start.8
  100.4 2.3 copy.124
  102.9 2.4 fusion.17
  109.1 2.9 copy.127
  112.0 2.9 fusion.28
  114.8 3.1 %copy.131 = f32[128,2816]{1,0:T(8,128)} copy(f32[128,2816]{0,1:T(8,128)} %bitcast.174) | data formatting | bytes 2883584 | tf_op jit(solution)/shard_map/reshape | solution.py:21
  119.5 2.8 convolution_multiply_fusion
  124.6 9.5 %collective-permute-start.10 = (f32[3,2816]{1,0:T(4,128)S(1)}, f32[3,2816]{1,0:T(4,128)S(1)}, u32[]{:S(2)}, u32[]{:S(2)}) collective-permute-start(f32[3,2816]{1,0:T(4,128)S(1)} %pad_maximum_fusion.10), channel_id=1, source_target_pairs={{0,1},{1,0},{2,3},{3,2},{4,5},{5,4},{6,7},{7,6},{8,9},{9,8},{10,11... | collective-permute-start | bytes 101384 | tf_op jit(solution)/shard_map/ppermute | solution.py:92
  134.1 2.9 collective-permute-done.10
  138.1 11.2 %collective-permute-start.11 = (f32[3,2816]{1,0:T(4,128)S(1)}, f32[3,2816]{1,0:T(4,128)S(1)}, u32[]{:S(2)}, u32[]{:S(2)}) collective-permute-start(f32[3,2816]{1,0:T(4,128)S(1)} %pad_maximum_fusion.11), channel_id=1, source_target_pairs={{0,2},{1,3},{2,0},{3,1},{4,6},{5,7},{6,4},{7,5},{8,10},{9,11},{10,... | collective-permute-start | bytes 101384 | tf_op jit(solution)/shard_map/ppermute | solution.py:92
  149.4 3.9 %collective-permute-done.11 = f32[3,2816]{1,0:T(4,128)S(1)} collective-permute-done((f32[3,2816]{1,0:T(4,128)S(1)}, f32[3,2816]{1,0:T(4,128)S(1)}, u32[]{:S(2)}, u32[]{:S(2)}) %collective-permute-start.11) | collective-permute-done | bytes 33824 | tf_op jit(solution)/shard_map/ppermute | solution.py:92
  153.4 5.9 %collective-permute-start.12 = (f32[3,2816]{1,0:T(4,128)S(1)}, f32[3,2816]{1,0:T(4,128)S(1)}, u32[]{:S(2)}, u32[]{:S(2)}) collective-permute-start(f32[3,2816]{1,0:T(4,128)S(1)} %pad_maximum_fusion.12), channel_id=1, source_target_pairs={{0,4},{1,5},{2,6},{3,7},{4,0},{5,1},{6,2},{7,3},{8,12},{9,13},{10,... | collective-permute-start | bytes 101384 | tf_op jit(solution)/shard_map/ppermute | solution.py:92
  161.4 6.5 %collective-permute-start.13 = (f32[3,2816]{1,0:T(4,128)S(1)}, f32[3,2816]{1,0:T(4,128)S(1)}, u32[]{:S(2)}, u32[]{:S(2)}) collective-permute-start(f32[3,2816]{1,0:T(4,128)S(1)} %pad_maximum_fusion.13), channel_id=1, source_target_pairs={{0,8},{1,9},{2,10},{3,11},{4,12},{5,13},{6,14},{7,15},{8,0},{9,1},... | collective-permute-start | bytes 101384 | tf_op jit(solution)/shard_map/ppermute | solution.py:92
  169.9 2.1 slice_add_fusion
  173.0 4.6 %multiply_reduce_fusion = (f32[2816]{0:T(1024)S(1)}, f32[128,2816]{1,0:T(8,128)S(1)}, bf16[128,2816]{1,0:T(8,128)(2,1)}, f32[128,2816]{1,0:T(8,128)}) fusion(f32[128,2816]{1,0:T(8,128)S(1)} %copy-done.4, f32[2816]{0:T(1024)S(1)} %add.402, f32[128,2816]{1,0:T(8,128)S(1)} %copy-done.6, f32[2816]{0:T(1024)S(1)} %add.406, f32[2816]{0:T(1024)S(1)} %mul.339, ...), kind=kLoop, calls=%fused_computation.69 | loop fusion | flops 17659136 | bytes 16704512 | tf_op jit(solution)/shard_map/reduce_sum | solution.py:254
  181.1 3.4 %copy.139 = f32[256,11,256]{2,1,0:T(8,128)} copy(f32[256,11,256]{0,2,1:T(8,128)S(1)} %convolution_bitcast_fusion) | data formatting | bytes 5767168 | tf_op jit(solution)/shard_map/thk,thj->khj/transpose | solution.py:37
  184.5 4.7 %concatenate.25 = f32[2,2,2,2,2,8,2816]{6,5,4,3,2,1,0:T(8,128)} reshape(f32[256,11,256]{2,1,0:T(8,128)} %copy.139) | data formatting | bytes 5767168 | tf_op jit(solution)/shard_map/concatenate | solution.py:169
  194.6 3.8 %collective-permute-done.15 = f32[16,8,3168]{2,1,0:T(8,128)} collective-permute-done((f32[16,8,3168]{2,1,0:T(8,128)}, f32[16,8,3168]{2,1,0:T(8,128)}, u32[]{:S(2)}, u32[]{:S(2)}) %collective-permute-start.15) | collective-permute-done | bytes 1622048 | tf_op jit(solution)/shard_map/ppermute | solution.py:92
  204.1 2.9 collective-permute-start.17
  207.0 4.4 %collective-permute-start.18 = (f32[4,8,3168]{2,1,0:T(8,128)S(1)}, f32[4,8,3168]{2,1,0:T(8,128)}, u32[]{:S(2)}, u32[]{:S(2)}) collective-permute-start(f32[4,8,3168]{2,1,0:T(8,128)S(1)} %get-tuple-element.24), channel_id=1, source_target_pairs={{0,96},{16,112},{32,64},{48,80},{64,32},{80,48},{96,0},{112,16},{1... | collective-permute-start | bytes 1216520 | tf_op jit(solution)/shard_map/ppermute | solution.py:92
  214.3 4.4 %collective-permute-done.16 = f32[4,8,3168]{2,1,0:T(8,128)} collective-permute-done((f32[4,8,3168]{2,1,0:T(8,128)}, f32[4,8,3168]{2,1,0:T(8,128)}, u32[]{:S(2)}, u32[]{:S(2)}) %collective-permute-start.16) | collective-permute-done | bytes 405536 | tf_op jit(solution)/shard_map/ppermute | solution.py:92
  218.7 16.0 %collective-permute-done.17 = f32[4,8,3168]{2,1,0:T(8,128)} collective-permute-done((f32[4,8,3168]{2,1,0:T(8,128)}, f32[4,8,3168]{2,1,0:T(8,128)}, u32[]{:S(2)}, u32[]{:S(2)}) %collective-permute-start.17) | collective-permute-done | bytes 405536 | tf_op jit(solution)/shard_map/ppermute | solution.py:92
  234.7 10.7 %collective-permute-done.18 = f32[4,8,3168]{2,1,0:T(8,128)} collective-permute-done((f32[4,8,3168]{2,1,0:T(8,128)S(1)}, f32[4,8,3168]{2,1,0:T(8,128)}, u32[]{:S(2)}, u32[]{:S(2)}) %collective-permute-start.18) | collective-permute-done | bytes 405536 | tf_op jit(solution)/shard_map/ppermute | solution.py:92
  247.6 3.8 %collective-permute-start.19 = (f32[1,8,3168]{2,1,0:T(8,128)}, f32[1,8,3168]{2,1,0:T(8,128)}, u32[]{:S(2)}, u32[]{:S(2)}) collective-permute-start(f32[1,8,3168]{2,1,0:T(8,128)} %get-tuple-element.40), channel_id=1, source_target_pairs={{0,128},{16,144},{32,160},{48,176},{64,192},{80,208},{96,224},{112... | collective-permute-start | bytes 304136 | tf_op jit(solution)/shard_map/ppermute | solution.py:92
  253.3 4.7 %collective-permute-start.21 = (f32[1,8,3168]{2,1,0:T(8,128)S(1)}, f32[1,8,3168]{2,1,0:T(8,128)}, u32[]{:S(2)}, u32[]{:S(2)}) collective-permute-start(f32[1,8,3168]{2,1,0:T(8,128)S(1)} %get-tuple-element.41), channel_id=1, source_target_pairs={{0,384},{16,400},{32,416},{48,432},{64,448},{80,464},{96,480},{112... | collective-permute-start | bytes 304136 | tf_op jit(solution)/shard_map/ppermute | solution.py:92
  264.1 5.7 %collective-permute-start.22 = (f32[4,8,528]{2,1,0:T(8,128)S(1)}, f32[4,8,528]{2,1,0:T(8,128)S(1)}, u32[]{:S(2)}, u32[]{:S(2)}) collective-permute-start(f32[4,8,528]{2,1,0:T(8,128)S(1)} %get-tuple-element.45), channel_id=1, source_target_pairs={{0,1},{1,0},{2,3},{3,2},{4,5},{5,4},{6,7},{7,6},{8,9},{9,8},{10,11... | collective-permute-start | bytes 202760 | tf_op jit(solution)/shard_map/ppermute | solution.py:92
  269.8 10.2 %collective-permute-start.23 = (f32[4,8,528]{2,1,0:T(8,128)S(1)}, f32[4,8,528]{2,1,0:T(8,128)S(1)}, u32[]{:S(2)}, u32[]{:S(2)}) collective-permute-start(f32[4,8,528]{2,1,0:T(8,128)S(1)} %get-tuple-element.47), channel_id=1, source_target_pairs={{0,2},{1,3},{2,0},{3,1},{4,6},{5,7},{6,4},{7,5},{8,10},{9,11},{10,... | collective-permute-start | bytes 202760 | tf_op jit(solution)/shard_map/ppermute | solution.py:92
  281.9 2.6 add_add_fusion
  285.9 4.4 %collective-permute-done.24 = f32[4,8,528]{2,1,0:T(8,128)S(1)} collective-permute-done((f32[4,8,528]{2,1,0:T(8,128)S(1)}, f32[4,8,528]{2,1,0:T(8,128)S(1)}, u32[]{:S(2)}, u32[]{:S(2)}) %collective-permute-start.24) | collective-permute-done | bytes 67616 | tf_op jit(solution)/shard_map/ppermute | solution.py:92
  290.3 5.6 %collective-permute-start.25 = (f32[1,8,528]{2,1,0:T(8,128)S(1)}, f32[1,8,528]{2,1,0:T(8,128)S(1)}, u32[]{:S(2)}, u32[]{:S(2)}) collective-permute-start(f32[1,8,528]{2,1,0:T(8,128)S(1)} %get-tuple-element.59), channel_id=1, source_target_pairs={{0,4},{1,5},{2,6},{3,7},{4,0},{5,1},{6,2},{7,3},{8,12},{9,13},{10,... | collective-permute-start | bytes 50696 | tf_op jit(solution)/shard_map/ppermute | solution.py:92
  295.9 4.6 %collective-permute-start.26 = (f32[1,8,528]{2,1,0:T(8,128)S(1)}, f32[1,8,528]{2,1,0:T(8,128)S(1)}, u32[]{:S(2)}, u32[]{:S(2)}) collective-permute-start(f32[1,8,528]{2,1,0:T(8,128)S(1)} %get-tuple-element.61), channel_id=1, source_target_pairs={{0,8},{1,9},{2,10},{3,11},{4,12},{5,13},{6,14},{7,15},{8,0},{9,1},... | collective-permute-start | bytes 50696 | tf_op jit(solution)/shard_map/ppermute | solution.py:92
  304.0 3.4 %collective-permute-done.27 = f32[1,8,528]{2,1,0:T(8,128)S(1)} collective-permute-done((f32[1,8,528]{2,1,0:T(8,128)S(1)}, f32[1,8,528]{2,1,0:T(8,128)S(1)}, u32[]{:S(2)}, u32[]{:S(2)}) %collective-permute-start.27) | collective-permute-done | bytes 16928 | tf_op jit(solution)/shard_map/ppermute | solution.py:92
  (159 shorter events, 62.3 us)
Async XLA Ops:
  5.3 10.8 %collective-permute-start = (bf16[24,176]{1,0:T(8,128)(2,1)S(1)}, bf16[24,176]{1,0:T(8,128)(2,1)S(1)}, u32[]{:S(2)}, u32[]{:S(2)}) collective-permute-start(bf16[24,176]{1,0:T(8,128)(2,1)S(1)} %concatenate.21), channel_id=1, source_target_pairs={{0,1},{1,0},{2,3},{3,2},{4,5},{5,4},{6,7},{7,6},{8,9},{9,8},{10,11... | collective-permute-start | bytes 25352 | tf_op jit(solution)/shard_map/ppermute | solution.py:92
  16.1 14.5 %collective-permute-start.1 = (bf16[2,24,176]{2,1,0:T(8,128)(2,1)S(1)}, bf16[2,24,176]{2,1,0:T(8,128)(2,1)S(1)}, u32[]{:S(2)}, u32[]{:S(2)}) collective-permute-start(bf16[2,24,176]{2,1,0:T(8,128)(2,1)S(1)} %get-tuple-element.72), channel_id=1, source_target_pairs={{0,2},{1,3},{2,0},{3,1},{4,6},{5,7},{6,4},{7,5},{8,10},{9,11},{10,... | collective-permute-start | bytes 50696 | tf_op jit(solution)/shard_map/ppermute | solution.py:92
  30.7 6.0 %collective-permute-start.2 = (bf16[2,2,24,176]{3,2,1,0:T(8,128)(2,1)S(1)}, bf16[2,2,24,176]{3,2,1,0:T(8,128)(2,1)S(1)}, u32[]{:S(2)}, u32[]{:S(2)}) collective-permute-start(bf16[2,2,24,176]{3,2,1,0:T(8,128)(2,1)S(1)} %get-tuple-element.68), channel_id=1, source_target_pairs={{0,4},{1,5},{2,6},{3,7},{4,0},{5,1},{6,2},{7,3},{8,12},{9,13},{10,... | collective-permute-start | bytes 101384 | tf_op jit(solution)/shard_map/ppermute | solution.py:92
  36.7 8.0 %collective-permute-start.3 = (bf16[2,2,2,24,176]{4,3,2,1,0:T(8,128)(2,1)S(1)}, bf16[2,2,2,24,176]{4,3,2,1,0:T(8,128)(2,1)S(1)}, u32[]{:S(2)}, u32[]{:S(2)}) collective-permute-start(bf16[2,2,2,24,176]{4,3,2,1,0:T(8,128)(2,1)S(1)} %get-tuple-element.55), channel_id=1, source_target_pairs={{0,8},{1,9},{2,10},{3,11},{4,12},{5,13},{6,14},{7,15},{8,0},{9,1},... | collective-permute-start | bytes 202760 | tf_op jit(solution)/shard_map/ppermute | solution.py:92
  45.3 8.7 %collective-permute-start.4 = (bf16[11,16,256]{2,0,1:T(8,128)(2,1)S(1)}, bf16[11,16,256]{2,0,1:T(8,128)(2,1)S(1)}, u32[]{:S(2)}, u32[]{:S(2)}) collective-permute-start(bf16[11,16,256]{2,0,1:T(8,128)(2,1)S(1)} %bitcast.189), channel_id=1, source_target_pairs={{0,256},{16,272},{32,288},{48,304},{64,320},{80,336},{96,352},{112... | collective-permute-start | bytes 270344 | tf_op jit(solution)/shard_map/ppermute | solution.py:92
  54.1 8.3 %collective-permute-start.5 = (bf16[2,11,16,256]{3,1,2,0:T(8,128)(2,1)S(1)}, bf16[2,11,16,256]{3,1,2,0:T(8,128)(2,1)S(1)}, u32[]{:S(2)}, u32[]{:S(2)}) collective-permute-start(bf16[2,11,16,256]{3,1,2,0:T(8,128)(2,1)S(1)} %get-tuple-element.48), channel_id=1, source_target_pairs={{0,128},{16,144},{32,160},{48,176},{64,192},{80,208},{96,224},{112... | collective-permute-start | bytes 540680 | tf_op jit(solution)/shard_map/ppermute | solution.py:92
  62.8 13.4 %collective-permute-start.6 = (bf16[2,2,11,16,256]{4,3,2,0,1:T(8,128)(2,1)S(1)}, bf16[2,2,11,16,256]{4,3,2,0,1:T(8,128)(2,1)S(1)}, u32[]{:S(2)}, u32[]{:S(2)}) collective-permute-start(bf16[2,2,11,16,256]{4,3,2,0,1:T(8,128)(2,1)S(1)} %get-tuple-element.43), channel_id=1, source_target_pairs={{0,64},{16,80},{32,96},{48,112},{64,0},{80,16},{96,32},{112,48},{1... | collective-permute-start | bytes 1081352 | tf_op jit(solution)/shard_map/ppermute | solution.py:92
  76.7 17.1 %collective-permute-start.7 = (bf16[2,2,2,11,16,256]{5,4,3,1,0,2:T(8,128)(2,1)S(1)}, bf16[2,2,2,11,16,256]{5,4,3,1,0,2:T(8,128)(2,1)S(1)}, u32[]{:S(2)}, u32[]{:S(2)}) collective-permute-start(bf16[2,2,2,11,16,256]{5,4,3,1,0,2:T(8,128)(2,1)S(1)} %get-tuple-element.34), channel_id=1, source_target_pairs={{0,32},{16,48},{32,0},{48,16},{64,96},{80,112},{96,64},{112,80},{1... | collective-permute-start | bytes 2162696 | tf_op jit(solution)/shard_map/ppermute | solution.py:92
  82.6 15.3 %collective-permute-start.9 = (bf16[3,2816]{1,0:T(4,128)(2,1)S(1)}, bf16[3,2816]{1,0:T(4,128)(2,1)S(1)}, u32[]{:S(2)}, u32[]{:S(2)}) collective-permute-start(bf16[3,2816]{1,0:T(4,128)(2,1)S(1)} %slice_bitcast_fusion.2), channel_id=1, source_target_pairs={{0,1},{1,2},{2,3},{3,4},{4,5},{5,6},{6,7},{7,8},{8,9},{9,10},{10,1... | collective-permute-start | bytes 50696 | tf_op jit(solution)/shard_map/ppermute | solution.py:13
  94.4 3.4 %copy-start.21 = (bf16[1,128,2816]{2,1,0:T(8,128)(2,1)S(1)}, bf16[1,128,2816]{2,1,0:T(8,128)(2,1)}, u32[]{:S(2)}) copy-start(bf16[1,128,2816]{2,1,0:T(8,128)(2,1)} %param.9) | copy-start | bytes 2162692
  95.7 7.2 %collective-permute-start.8 = (bf16[2,2,2,2,11,16,256]{6,5,4,2,1,0,3:T(8,128)(2,1)}, bf16[2,2,2,2,11,16,256]{6,5,4,2,1,0,3:T(8,128)(2,1)}, u32[]{:S(2)}, u32[]{:S(2)}) collective-permute-start(bf16[2,2,2,2,11,16,256]{6,5,4,2,1,0,3:T(8,128)(2,1)} %get-tuple-element.30), channel_id=1, source_target_pairs={{0,16},{16,0},{32,48},{48,32},{64,80},{80,64},{96,112},{112,96},{1... | collective-permute-start | bytes 4325384 | tf_op jit(solution)/shard_map/ppermute | solution.py:92
  106.4 2.7 copy-start.2
  106.4 5.6 %copy-start = (bf16[11,32,8,256]{3,2,0,1:T(8,128)(2,1)}, bf16[11,32,8,256]{3,2,0,1:T(8,128)(2,1)S(1)}, u32[]{:S(2)}) copy-start(bf16[11,32,8,256]{3,2,0,1:T(8,128)(2,1)S(1)} %get-tuple-element.20) | copy-start | bytes 4325380
  114.8 3.1 %copy-start.4 = (f32[128,2816]{1,0:T(8,128)S(1)}, f32[128,2816]{1,0:T(8,128)}, u32[]{:S(2)}) copy-start(f32[128,2816]{1,0:T(8,128)} %copy.127) | copy-start | bytes 4325380
  117.9 1.4 copy-start.5
  117.9 1.5 copy-start.18
  119.2 3.0 copy-start.14
  119.3 5.3 %copy-start.20 = (f32[128,2816]{1,0:T(8,128)}, f32[128,2816]{1,0:T(8,128)S(1)}, u32[]{:S(2)}) copy-start(f32[128,2816]{1,0:T(8,128)S(1)} %get-tuple-element.76) | copy-start | bytes 4325380
  119.5 2.8 copy-start.22
  124.6 12.4 %collective-permute-start.10 = (f32[3,2816]{1,0:T(4,128)S(1)}, f32[3,2816]{1,0:T(4,128)S(1)}, u32[]{:S(2)}, u32[]{:S(2)}) collective-permute-start(f32[3,2816]{1,0:T(4,128)S(1)} %pad_maximum_fusion.10), channel_id=1, source_target_pairs={{0,1},{1,0},{2,3},{3,2},{4,5},{5,4},{6,7},{7,6},{8,9},{9,8},{10,11... | collective-permute-start | bytes 101384 | tf_op jit(solution)/shard_map/ppermute | solution.py:92
  138.1 15.1 %collective-permute-start.11 = (f32[3,2816]{1,0:T(4,128)S(1)}, f32[3,2816]{1,0:T(4,128)S(1)}, u32[]{:S(2)}, u32[]{:S(2)}) collective-permute-start(f32[3,2816]{1,0:T(4,128)S(1)} %pad_maximum_fusion.11), channel_id=1, source_target_pairs={{0,2},{1,3},{2,0},{3,1},{4,6},{5,7},{6,4},{7,5},{8,10},{9,11},{10,... | collective-permute-start | bytes 101384 | tf_op jit(solution)/shard_map/ppermute | solution.py:92
  153.4 7.9 %collective-permute-start.12 = (f32[3,2816]{1,0:T(4,128)S(1)}, f32[3,2816]{1,0:T(4,128)S(1)}, u32[]{:S(2)}, u32[]{:S(2)}) collective-permute-start(f32[3,2816]{1,0:T(4,128)S(1)} %pad_maximum_fusion.12), channel_id=1, source_target_pairs={{0,4},{1,5},{2,6},{3,7},{4,0},{5,1},{6,2},{7,3},{8,12},{9,13},{10,... | collective-permute-start | bytes 101384 | tf_op jit(solution)/shard_map/ppermute | solution.py:92
  161.4 8.3 %collective-permute-start.13 = (f32[3,2816]{1,0:T(4,128)S(1)}, f32[3,2816]{1,0:T(4,128)S(1)}, u32[]{:S(2)}, u32[]{:S(2)}) collective-permute-start(f32[3,2816]{1,0:T(4,128)S(1)} %pad_maximum_fusion.13), channel_id=1, source_target_pairs={{0,8},{1,9},{2,10},{3,11},{4,12},{5,13},{6,14},{7,15},{8,0},{9,1},... | collective-permute-start | bytes 101384 | tf_op jit(solution)/shard_map/ppermute | solution.py:92
  169.9 2.2 copy-start.6
  169.9 2.7 copy-start.12
  169.9 3.1 copy-start.15
  192.7 5.7 %collective-permute-start.15 = (f32[16,8,3168]{2,1,0:T(8,128)}, f32[16,8,3168]{2,1,0:T(8,128)}, u32[]{:S(2)}, u32[]{:S(2)}) collective-permute-start(f32[16,8,3168]{2,1,0:T(8,128)} %dynamic-slice_bitcast_fusion), channel_id=1, source_target_pairs={{0,16},{16,0},{32,48},{48,32},{64,80},{80,64},{96,112},{112,96},{1... | collective-permute-start | bytes 4866056 | tf_op jit(solution)/shard_map/ppermute | solution.py:92
  200.0 1.2 copy-start.9
  200.0 11.5 %copy-start.16 = (bf16[128,2816]{1,0:T(8,128)(2,1)S(1)}, bf16[128,2816]{1,0:T(8,128)(2,1)}, u32[]{:S(2)}) copy-start(bf16[128,2816]{1,0:T(8,128)(2,1)} %get-tuple-element.17) | copy-start | bytes 2162692
  201.2 11.5 %copy-start.3 = (bf16[11,32,8,256]{3,2,0,1:T(8,128)(2,1)S(1)}, bf16[11,32,8,256]{3,2,0,1:T(8,128)(2,1)}, u32[]{:S(2)}) copy-start(bf16[11,32,8,256]{3,2,0,1:T(8,128)(2,1)} %copy-done.2) | copy-start | bytes 4325380
  201.2 11.5 %copy-start.10 = (bf16[128,2816]{0,1:T(8,128)(2,1)S(1)}, bf16[128,2816]{0,1:T(8,128)(2,1)}, u32[]{:S(2)}) copy-start(bf16[128,2816]{0,1:T(8,128)(2,1)} %copy.132) | copy-start | bytes 2162692
  202.2 16.5 %collective-permute-start.16 = (f32[4,8,3168]{2,1,0:T(8,128)}, f32[4,8,3168]{2,1,0:T(8,128)}, u32[]{:S(2)}, u32[]{:S(2)}) collective-permute-start(f32[4,8,3168]{2,1,0:T(8,128)} %get-tuple-element.23), channel_id=1, source_target_pairs={{0,32},{16,48},{32,0},{48,16},{64,96},{80,112},{96,64},{112,80},{1... | collective-permute-start | bytes 1216520 | tf_op jit(solution)/shard_map/ppermute | solution.py:92
  204.1 30.6 %collective-permute-start.17 = (f32[4,8,3168]{2,1,0:T(8,128)}, f32[4,8,3168]{2,1,0:T(8,128)}, u32[]{:S(2)}, u32[]{:S(2)}) collective-permute-start(f32[4,8,3168]{2,1,0:T(8,128)} %get-tuple-element.25), channel_id=1, source_target_pairs={{0,64},{16,80},{32,96},{48,112},{64,0},{80,16},{96,32},{112,48},{1... | collective-permute-start | bytes 1216520 | tf_op jit(solution)/shard_map/ppermute | solution.py:92
  207.0 38.4 %collective-permute-start.18 = (f32[4,8,3168]{2,1,0:T(8,128)S(1)}, f32[4,8,3168]{2,1,0:T(8,128)}, u32[]{:S(2)}, u32[]{:S(2)}) collective-permute-start(f32[4,8,3168]{2,1,0:T(8,128)S(1)} %get-tuple-element.24), channel_id=1, source_target_pairs={{0,96},{16,112},{32,64},{48,80},{64,32},{80,48},{96,0},{112,16},{1... | collective-permute-start | bytes 1216520 | tf_op jit(solution)/shard_map/ppermute | solution.py:92
  214.3 43.7 %copy-start.1 = (bf16[11,32,8,256]{3,2,0,1:T(8,128)(2,1)S(1)}, bf16[11,32,8,256]{3,2,0,1:T(8,128)(2,1)}, u32[]{:S(2)}) copy-start(bf16[11,32,8,256]{3,2,0,1:T(8,128)(2,1)} %copy-done) | copy-start | bytes 4325380
  214.3 43.8 %copy-start.17 = (bf16[128,2816]{0,1:T(8,128)(2,1)S(1)}, bf16[128,2816]{0,1:T(8,128)(2,1)}, u32[]{:S(2)}) copy-start(bf16[128,2816]{0,1:T(8,128)(2,1)} %copy.135) | copy-start | bytes 2162692
  247.6 14.9 %collective-permute-start.19 = (f32[1,8,3168]{2,1,0:T(8,128)}, f32[1,8,3168]{2,1,0:T(8,128)}, u32[]{:S(2)}, u32[]{:S(2)}) collective-permute-start(f32[1,8,3168]{2,1,0:T(8,128)} %get-tuple-element.40), channel_id=1, source_target_pairs={{0,128},{16,144},{32,160},{48,176},{64,192},{80,208},{96,224},{112... | collective-permute-start | bytes 304136 | tf_op jit(solution)/shard_map/ppermute | solution.py:92
  251.3 11.2 %collective-permute-start.20 = (f32[1,8,3168]{2,1,0:T(8,128)}, f32[1,8,3168]{2,1,0:T(8,128)}, u32[]{:S(2)}, u32[]{:S(2)}) collective-permute-start(f32[1,8,3168]{2,1,0:T(8,128)} %get-tuple-element.42), channel_id=1, source_target_pairs={{0,256},{16,272},{32,288},{48,304},{64,320},{80,336},{96,352},{112... | collective-permute-start | bytes 304136 | tf_op jit(solution)/shard_map/ppermute | solution.py:92
  253.3 9.3 %collective-permute-start.21 = (f32[1,8,3168]{2,1,0:T(8,128)S(1)}, f32[1,8,3168]{2,1,0:T(8,128)}, u32[]{:S(2)}, u32[]{:S(2)}) collective-permute-start(f32[1,8,3168]{2,1,0:T(8,128)S(1)} %get-tuple-element.41), channel_id=1, source_target_pairs={{0,384},{16,400},{32,416},{48,432},{64,448},{80,464},{96,480},{112... | collective-permute-start | bytes 304136 | tf_op jit(solution)/shard_map/ppermute | solution.py:92
  258.0 1.4 copy-start.13
  262.5 19.4 %copy-start.7 = (f32[128,2816]{1,0:T(8,128)S(1)}, f32[128,2816]{1,0:T(8,128)}, u32[]{:S(2)}) copy-start(f32[128,2816]{1,0:T(8,128)} %copy.131) | copy-start | bytes 4325380
  264.1 21.8 %collective-permute-start.22 = (f32[4,8,528]{2,1,0:T(8,128)S(1)}, f32[4,8,528]{2,1,0:T(8,128)S(1)}, u32[]{:S(2)}, u32[]{:S(2)}) collective-permute-start(f32[4,8,528]{2,1,0:T(8,128)S(1)} %get-tuple-element.45), channel_id=1, source_target_pairs={{0,1},{1,0},{2,3},{3,2},{4,5},{5,4},{6,7},{7,6},{8,9},{9,8},{10,11... | collective-permute-start | bytes 202760 | tf_op jit(solution)/shard_map/ppermute | solution.py:92
  269.8 16.1 %collective-permute-start.23 = (f32[4,8,528]{2,1,0:T(8,128)S(1)}, f32[4,8,528]{2,1,0:T(8,128)S(1)}, u32[]{:S(2)}, u32[]{:S(2)}) collective-permute-start(f32[4,8,528]{2,1,0:T(8,128)S(1)} %get-tuple-element.47), channel_id=1, source_target_pairs={{0,2},{1,3},{2,0},{3,1},{4,6},{5,7},{6,4},{7,5},{8,10},{9,11},{10,... | collective-permute-start | bytes 202760 | tf_op jit(solution)/shard_map/ppermute | solution.py:92
  280.0 10.3 %collective-permute-start.24 = (f32[4,8,528]{2,1,0:T(8,128)S(1)}, f32[4,8,528]{2,1,0:T(8,128)S(1)}, u32[]{:S(2)}, u32[]{:S(2)}) collective-permute-start(f32[4,8,528]{2,1,0:T(8,128)S(1)} %get-tuple-element.46), channel_id=1, source_target_pairs={{0,3},{1,2},{2,1},{3,0},{4,7},{5,6},{6,5},{7,4},{8,11},{9,10},{10,... | collective-permute-start | bytes 202760 | tf_op jit(solution)/shard_map/ppermute | solution.py:92
  284.6 17.9 %collective-permute-start.14 = (f32[3,2816]{1,0:T(4,128)S(1)}, f32[3,2816]{1,0:T(4,128)S(1)}, u32[]{:S(2)}, u32[]{:S(2)}) collective-permute-start(f32[3,2816]{1,0:T(4,128)S(1)} %slice.215), channel_id=1, source_target_pairs={{1,0},{2,1},{3,2},{4,3},{5,4},{6,5},{7,6},{8,7},{9,8},{10,9},{11,1... | collective-permute-start | bytes 101384 | tf_op jit(solution)/shard_map/ppermute | solution.py:13
  290.3 13.7 %collective-permute-start.25 = (f32[1,8,528]{2,1,0:T(8,128)S(1)}, f32[1,8,528]{2,1,0:T(8,128)S(1)}, u32[]{:S(2)}, u32[]{:S(2)}) collective-permute-start(f32[1,8,528]{2,1,0:T(8,128)S(1)} %get-tuple-element.59), channel_id=1, source_target_pairs={{0,4},{1,5},{2,6},{3,7},{4,0},{5,1},{6,2},{7,3},{8,12},{9,13},{10,... | collective-permute-start | bytes 50696 | tf_op jit(solution)/shard_map/ppermute | solution.py:92
  295.9 8.1 %collective-permute-start.26 = (f32[1,8,528]{2,1,0:T(8,128)S(1)}, f32[1,8,528]{2,1,0:T(8,128)S(1)}, u32[]{:S(2)}, u32[]{:S(2)}) collective-permute-start(f32[1,8,528]{2,1,0:T(8,128)S(1)} %get-tuple-element.61), channel_id=1, source_target_pairs={{0,8},{1,9},{2,10},{3,11},{4,12},{5,13},{6,14},{7,15},{8,0},{9,1},... | collective-permute-start | bytes 50696 | tf_op jit(solution)/shard_map/ppermute | solution.py:92
  300.5 6.9 %collective-permute-start.27 = (f32[1,8,528]{2,1,0:T(8,128)S(1)}, f32[1,8,528]{2,1,0:T(8,128)S(1)}, u32[]{:S(2)}, u32[]{:S(2)}) collective-permute-start(f32[1,8,528]{2,1,0:T(8,128)S(1)} %get-tuple-element.60), channel_id=1, source_target_pairs={{0,12},{1,13},{2,14},{3,15},{4,8},{5,9},{6,10},{7,11},{8,4},{9,5},... | collective-permute-start | bytes 50696 | tf_op jit(solution)/shard_map/ppermute | solution.py:92
  (3 other events, 3.4 us)

commit v2 on v1

--- a/solution.py
+++ b/solution.py
@@ -74,6 +74,17 @@
     return [bits[:1]] + [bits[i : i + 2] for i in range(1, len(bits), 2)]
 
 
+def spread_steps(length, first):
+    bits = [stride for step in digit_steps(length) for stride in step]
+    head, rest = bits[:first], bits[first:]
+    half = (len(rest) + 1) // 2
+    low, high = rest[:half], rest[half:]
+    steps = [[b] for b in head]
+    for i, b in enumerate(low):
+        steps.append([b, high[i]] if i < len(high) else [b])
+    return steps
+
+
 def bit_steps(length):
     return [[stride] for step in digit_steps(length) for stride in step]
 
@@ -253,9 +264,9 @@
     local_wgrad = grad_heads(conv_b, d_recur, head_width)
     local_rgrad = jnp.sum(d_log * (-8.0 * recur_gate), axis=0)
     by_row = local_wgrad.reshape(dp_size, rows, width)
-    row_sum, rgrad = summed_apart(by_row, local_rgrad, "dp", core_first_steps(dp_size))
+    row_sum, rgrad = summed_apart(by_row, local_rgrad, "dp", spread_steps(dp_size, 1))
     by_channel = row_sum.reshape(rows, ctx_size, cols).transpose(1, 0, 2)
-    wgrad, rgrad = summed_apart(by_channel, rgrad, "ctx", digit_steps(ctx_size))
+    wgrad, rgrad = summed_apart(by_channel, rgrad, "ctx", spread_steps(ctx_size, 0))
     return (grad_in.astype(jnp.bfloat16)[None], wgrad, rgrad)
 
 

time: 310 us -> 307 us (level)
  the two profiles are of different devices: /device:TPU:64 before, /device:TPU:6 now
where the time goes in v2:
time: 307 us; the launch traced here: 303 us
  starting transfers between devices  135 us (44%)
  waiting for transfers between devices  85.4 us (28%)
  local copies, waits for them, and re-layouts  39.4 us (13%)
  other arithmetic  26.3 us (9%)
  matrix products  15 us (5%)
    ppermute x26, starting transfers between devices, exchanged(): return lax.ppermute(array, axis, [(i, i ^ mask) for i in range(length)])  120 us
    ppermute x26, waiting for transfers between devices, exchanged(): return lax.ppermute(array, axis, [(i, i ^ mask) for i in range(length)])  82.4 us
    ppermute x2, starting transfers between devices, passed_along(): return lax.ppermute(array, axis, pairs)  15.3 us
  transfers between devices with their start and end apart: 28, of which 18 were waited for; matrix products, arithmetic and copies ran while one was open for 7% of the time, Pallas kernels for 0%

profile of v2, /device:TPU:6, one launch (start us, length us, event | category | flops | bytes accessed | tf_op | source)
XLA Modules:
  0.0 303.4 jit_solution(15598115275828456425)
XLA Ops:
  5.3 9.1 %collective-permute-start = (bf16[24,176]{1,0:T(8,128)(2,1)S(1)}, bf16[24,176]{1,0:T(8,128)(2,1)S(1)}, u32[]{:S(2)}, u32[]{:S(2)}) collective-permute-start(bf16[24,176]{1,0:T(8,128)(2,1)S(1)} %concatenate.21), channel_id=1, source_target_pairs={{0,1},{1,0},{2,3},{3,2},{4,5},{5,4},{6,7},{7,6},{8,9},{9,8},{10,11... | collective-permute-start | bytes 25352 | tf_op jit(solution)/shard_map/ppermute | solution.py:103
  16.1 14.5 %collective-permute-start.1 = (bf16[2,24,176]{2,1,0:T(8,128)(2,1)S(1)}, bf16[2,24,176]{2,1,0:T(8,128)(2,1)S(1)}, u32[]{:S(2)}, u32[]{:S(2)}) collective-permute-start(bf16[2,24,176]{2,1,0:T(8,128)(2,1)S(1)} %get-tuple-element.72), channel_id=1, source_target_pairs={{0,2},{1,3},{2,0},{3,1},{4,6},{5,7},{6,4},{7,5},{8,10},{9,11},{10,... | collective-permute-start | bytes 50696 | tf_op jit(solution)/shard_map/ppermute | solution.py:103
  32.5 2.7 collective-permute-start.2
  35.2 3.2 %collective-permute-done.2 = bf16[2,2,24,176]{3,2,1,0:T(8,128)(2,1)S(1)} collective-permute-done((bf16[2,2,24,176]{3,2,1,0:T(8,128)(2,1)S(1)}, bf16[2,2,24,176]{3,2,1,0:T(8,128)(2,1)S(1)}, u32[]{:S(2)}, u32[]{:S(2)}) %collective-permute-start.2) | collective-permute-done | bytes 33824 | tf_op jit(solution)/shard_map/ppermute | solution.py:103
  38.5 4.2 %collective-permute-start.3 = (bf16[2,2,2,24,176]{4,3,2,1,0:T(8,128)(2,1)S(1)}, bf16[2,2,2,24,176]{4,3,2,1,0:T(8,128)(2,1)S(1)}, u32[]{:S(2)}, u32[]{:S(2)}) collective-permute-start(bf16[2,2,2,24,176]{4,3,2,1,0:T(8,128)(2,1)S(1)} %get-tuple-element.55), channel_id=1, source_target_pairs={{0,8},{1,9},{2,10},{3,11},{4,12},{5,13},{6,14},{7,15},{8,0},{9,1},... | collective-permute-start | bytes 202760 | tf_op jit(solution)/shard_map/ppermute | solution.py:103
  42.8 3.8 %collective-permute-done.3 = bf16[2,2,2,24,176]{4,3,2,1,0:T(8,128)(2,1)S(1)} collective-permute-done((bf16[2,2,2,24,176]{4,3,2,1,0:T(8,128)(2,1)S(1)}, bf16[2,2,2,24,176]{4,3,2,1,0:T(8,128)(2,1)S(1)}, u32[]{:S(2)}, u32[]{:S(2)}) %collective-permute-start.3) | collective-permute-done | bytes 67616 | tf_op jit(solution)/shard_map/ppermute | solution.py:103
  47.1 5.1 %collective-permute-start.4 = (bf16[11,16,256]{2,0,1:T(8,128)(2,1)S(1)}, bf16[11,16,256]{2,0,1:T(8,128)(2,1)S(1)}, u32[]{:S(2)}, u32[]{:S(2)}) collective-permute-start(bf16[11,16,256]{2,0,1:T(8,128)(2,1)S(1)} %bitcast.189), channel_id=1, source_target_pairs={{0,256},{16,272},{32,288},{48,304},{64,320},{80,336},{96,352},{112... | collective-permute-start | bytes 270344 | tf_op jit(solution)/shard_map/ppermute | solution.py:103
  52.2 3.5 %collective-permute-done.4 = bf16[11,16,256]{2,0,1:T(8,128)(2,1)S(1)} collective-permute-done((bf16[11,16,256]{2,0,1:T(8,128)(2,1)S(1)}, bf16[11,16,256]{2,0,1:T(8,128)(2,1)S(1)}, u32[]{:S(2)}, u32[]{:S(2)}) %collective-permute-start.4) | collective-permute-done | bytes 90144 | tf_op jit(solution)/shard_map/ppermute | solution.py:103
  55.9 3.2 %collective-permute-start.5 = (bf16[2,11,16,256]{3,1,2,0:T(8,128)(2,1)S(1)}, bf16[2,11,16,256]{3,1,2,0:T(8,128)(2,1)S(1)}, u32[]{:S(2)}, u32[]{:S(2)}) collective-permute-start(bf16[2,11,16,256]{3,1,2,0:T(8,128)(2,1)S(1)} %get-tuple-element.48), channel_id=1, source_target_pairs={{0,128},{16,144},{32,160},{48,176},{64,192},{80,208},{96,224},{112... | collective-permute-start | bytes 540680 | tf_op jit(solution)/shard_map/ppermute | solution.py:103
  59.1 5.0 %collective-permute-done.5 = bf16[2,11,16,256]{3,1,2,0:T(8,128)(2,1)S(1)} collective-permute-done((bf16[2,11,16,256]{3,1,2,0:T(8,128)(2,1)S(1)}, bf16[2,11,16,256]{3,1,2,0:T(8,128)(2,1)S(1)}, u32[]{:S(2)}, u32[]{:S(2)}) %collective-permute-start.5) | collective-permute-done | bytes 180256 | tf_op jit(solution)/shard_map/ppermute | solution.py:103
  64.6 3.4 %collective-permute-start.6 = (bf16[2,2,11,16,256]{4,3,2,0,1:T(8,128)(2,1)S(1)}, bf16[2,2,11,16,256]{4,3,2,0,1:T(8,128)(2,1)S(1)}, u32[]{:S(2)}, u32[]{:S(2)}) collective-permute-start(bf16[2,2,11,16,256]{4,3,2,0,1:T(8,128)(2,1)S(1)} %get-tuple-element.43), channel_id=1, source_target_pairs={{0,64},{16,80},{32,96},{48,112},{64,0},{80,16},{96,32},{112,48},{1... | collective-permute-start | bytes 1081352 | tf_op jit(solution)/shard_map/ppermute | solution.py:103
  68.0 11.7 %collective-permute-done.6 = bf16[2,2,11,16,256]{4,3,2,0,1:T(8,128)(2,1)S(1)} collective-permute-done((bf16[2,2,11,16,256]{4,3,2,0,1:T(8,128)(2,1)S(1)}, bf16[2,2,11,16,256]{4,3,2,0,1:T(8,128)(2,1)S(1)}, u32[]{:S(2)}, u32[]{:S(2)}) %collective-permute-start.6) | collective-permute-done | bytes 360480 | tf_op jit(solution)/shard_map/ppermute | solution.py:103
  82.8 7.2 %collective-permute-start.9 = (bf16[3,2816]{1,0:T(4,128)(2,1)S(1)}, bf16[3,2816]{1,0:T(4,128)(2,1)S(1)}, u32[]{:S(2)}, u32[]{:S(2)}) collective-permute-start(bf16[3,2816]{1,0:T(4,128)(2,1)S(1)} %slice_bitcast_fusion.2), channel_id=1, source_target_pairs={{0,1},{1,2},{2,3},{3,4},{4,5},{5,6},{6,7},{7,8},{8,9},{9,10},{10,1... | collective-permute-start | bytes 50696 | tf_op jit(solution)/shard_map/ppermute | solution.py:13
  90.1 7.1 %collective-permute-done.7 = bf16[2,2,2,11,16,256]{5,4,3,1,0,2:T(8,128)(2,1)S(1)} collective-permute-done((bf16[2,2,2,11,16,256]{5,4,3,1,0,2:T(8,128)(2,1)S(1)}, bf16[2,2,2,11,16,256]{5,4,3,1,0,2:T(8,128)(2,1)S(1)}, u32[]{:S(2)}, u32[]{:S(2)}) %collective-permute-start.7) | collective-permute-done | bytes 720928 | tf_op jit(solution)/shard_map/ppermute | solution.py:103
  101.3 3.0 collective-permute-done.9
  106.8 2.3 copy.127
  109.3 2.4 fusion.17
  115.5 2.9 copy.130
  118.4 2.9 fusion.28
  121.3 3.1 %copy.134 = f32[128,2816]{1,0:T(8,128)} copy(f32[128,2816]{0,1:T(8,128)} %bitcast.173) | data formatting | bytes 2883584 | tf_op jit(solution)/shard_map/reshape | solution.py:21
  126.0 2.8 convolution_multiply_fusion
  131.1 3.4 %collective-permute-start.10 = (f32[3,2816]{1,0:T(4,128)S(1)}, f32[3,2816]{1,0:T(4,128)S(1)}, u32[]{:S(2)}, u32[]{:S(2)}) collective-permute-start(f32[3,2816]{1,0:T(4,128)S(1)} %pad_maximum_fusion.10), channel_id=1, source_target_pairs={{0,1},{1,0},{2,3},{3,2},{4,5},{5,4},{6,7},{7,6},{8,9},{9,8},{10,11... | collective-permute-start | bytes 101384 | tf_op jit(solution)/shard_map/ppermute | solution.py:103
  134.5 7.1 %collective-permute-done.10 = f32[3,2816]{1,0:T(4,128)S(1)} collective-permute-done((f32[3,2816]{1,0:T(4,128)S(1)}, f32[3,2816]{1,0:T(4,128)S(1)}, u32[]{:S(2)}, u32[]{:S(2)}) %collective-permute-start.10) | collective-permute-done | bytes 33824 | tf_op jit(solution)/shard_map/ppermute | solution.py:103
  142.7 8.4 %collective-permute-start.11 = (f32[3,2816]{1,0:T(4,128)S(1)}, f32[3,2816]{1,0:T(4,128)S(1)}, u32[]{:S(2)}, u32[]{:S(2)}) collective-permute-start(f32[3,2816]{1,0:T(4,128)S(1)} %pad_maximum_fusion.11), channel_id=1, source_target_pairs={{0,2},{1,3},{2,0},{3,1},{4,6},{5,7},{6,4},{7,5},{8,10},{9,11},{10,... | collective-permute-start | bytes 101384 | tf_op jit(solution)/shard_map/ppermute | solution.py:103
  151.1 6.5 %collective-permute-done.11 = f32[3,2816]{1,0:T(4,128)S(1)} collective-permute-done((f32[3,2816]{1,0:T(4,128)S(1)}, f32[3,2816]{1,0:T(4,128)S(1)}, u32[]{:S(2)}, u32[]{:S(2)}) %collective-permute-start.11) | collective-permute-done | bytes 33824 | tf_op jit(solution)/shard_map/ppermute | solution.py:103
  157.7 2.5 collective-permute-start.12
  160.2 3.4 %collective-permute-done.12 = f32[3,2816]{1,0:T(4,128)S(1)} collective-permute-done((f32[3,2816]{1,0:T(4,128)S(1)}, f32[3,2816]{1,0:T(4,128)S(1)}, u32[]{:S(2)}, u32[]{:S(2)}) %collective-permute-start.12) | collective-permute-done | bytes 33824 | tf_op jit(solution)/shard_map/ppermute | solution.py:103
  163.8 4.1 %collective-permute-start.13 = (f32[3,2816]{1,0:T(4,128)S(1)}, f32[3,2816]{1,0:T(4,128)S(1)}, u32[]{:S(2)}, u32[]{:S(2)}) collective-permute-start(f32[3,2816]{1,0:T(4,128)S(1)} %pad_maximum_fusion.13), channel_id=1, source_target_pairs={{0,8},{1,9},{2,10},{3,11},{4,12},{5,13},{6,14},{7,15},{8,0},{9,1},... | collective-permute-start | bytes 101384 | tf_op jit(solution)/shard_map/ppermute | solution.py:103
  167.9 3.3 %collective-permute-done.13 = f32[3,2816]{1,0:T(4,128)S(1)} collective-permute-done((f32[3,2816]{1,0:T(4,128)S(1)}, f32[3,2816]{1,0:T(4,128)S(1)}, u32[]{:S(2)}, u32[]{:S(2)}) %collective-permute-start.13) | collective-permute-done | bytes 33824 | tf_op jit(solution)/shard_map/ppermute | solution.py:103
  174.5 4.6 %multiply_reduce_fusion = (f32[2816]{0:T(1024)S(1)}, f32[128,2816]{1,0:T(8,128)S(1)}, bf16[128,2816]{1,0:T(8,128)(2,1)}, f32[128,2816]{1,0:T(8,128)}) fusion(f32[128,2816]{1,0:T(8,128)S(1)} %copy-done.4, f32[2816]{0:T(1024)S(1)} %add.402, f32[128,2816]{1,0:T(8,128)S(1)} %copy-done.6, f32[2816]{0:T(1024)S(1)} %add.406, f32[2816]{0:T(1024)S(1)} %mul.339, ...), kind=kLoop, calls=%fused_computation.69 | loop fusion | flops 17659136 | bytes 16704512 | tf_op jit(solution)/shard_map/reduce_sum | solution.py:265
  182.6 3.4 %copy.142 = f32[256,11,256]{2,1,0:T(8,128)} copy(f32[256,11,256]{0,2,1:T(8,128)S(1)} %convolution_bitcast_fusion) | data formatting | bytes 5767168 | tf_op jit(solution)/shard_map/thk,thj->khj/transpose | solution.py:37
  186.0 4.7 %concatenate.25 = f32[2,2,2,2,2,8,2816]{6,5,4,3,2,1,0:T(8,128)} reshape(f32[256,11,256]{2,1,0:T(8,128)} %copy.142) | data formatting | bytes 5767168 | tf_op jit(solution)/shard_map/concatenate | solution.py:180
  196.1 3.8 %collective-permute-done.15 = f32[16,8,3168]{2,1,0:T(8,128)} collective-permute-done((f32[16,8,3168]{2,1,0:T(8,128)}, f32[16,8,3168]{2,1,0:T(8,128)}, u32[]{:S(2)}, u32[]{:S(2)}) %collective-permute-start.15) | collective-permute-done | bytes 1622048 | tf_op jit(solution)/shard_map/ppermute | solution.py:103
  204.5 3.8 %collective-permute-start.17 = (f32[4,8,3168]{2,1,0:T(8,128)}, f32[4,8,3168]{2,1,0:T(8,128)}, u32[]{:S(2)}, u32[]{:S(2)}) collective-permute-start(f32[4,8,3168]{2,1,0:T(8,128)} %get-tuple-element.25), channel_id=1, source_target_pairs={{0,128},{16,144},{32,160},{48,176},{64,192},{80,208},{96,224},{112... | collective-permute-start | bytes 1216520 | tf_op jit(solution)/shard_map/ppermute | solution.py:103
  208.3 3.5 %collective-permute-start.18 = (f32[4,8,3168]{2,1,0:T(8,128)S(1)}, f32[4,8,3168]{2,1,0:T(8,128)}, u32[]{:S(2)}, u32[]{:S(2)}) collective-permute-start(f32[4,8,3168]{2,1,0:T(8,128)S(1)} %get-tuple-element.24), channel_id=1, source_target_pairs={{0,160},{16,176},{32,128},{48,144},{64,224},{80,240},{96,192},{112... | collective-permute-start | bytes 1216520 | tf_op jit(solution)/shard_map/ppermute | solution.py:103
  211.9 2.3 copy.138
  214.2 2.8 fusion.30
  217.1 10.1 %collective-permute-done.17 = f32[4,8,3168]{2,1,0:T(8,128)} collective-permute-done((f32[4,8,3168]{2,1,0:T(8,128)}, f32[4,8,3168]{2,1,0:T(8,128)}, u32[]{:S(2)}, u32[]{:S(2)}) %collective-permute-start.17) | collective-permute-done | bytes 405536 | tf_op jit(solution)/shard_map/ppermute | solution.py:103
  229.2 4.6 %collective-permute-start.19 = (f32[1,8,3168]{2,1,0:T(8,128)}, f32[1,8,3168]{2,1,0:T(8,128)}, u32[]{:S(2)}, u32[]{:S(2)}) collective-permute-start(f32[1,8,3168]{2,1,0:T(8,128)} %get-tuple-element.40), channel_id=1, source_target_pairs={{0,64},{16,80},{32,96},{48,112},{64,0},{80,16},{96,32},{112,48},{1... | collective-permute-start | bytes 304136 | tf_op jit(solution)/shard_map/ppermute | solution.py:103
  235.8 5.1 %collective-permute-start.21 = (f32[1,8,3168]{2,1,0:T(8,128)S(1)}, f32[1,8,3168]{2,1,0:T(8,128)}, u32[]{:S(2)}, u32[]{:S(2)}) collective-permute-start(f32[1,8,3168]{2,1,0:T(8,128)S(1)} %get-tuple-element.41), channel_id=1, source_target_pairs={{0,320},{16,336},{32,352},{48,368},{64,256},{80,272},{96,288},{112... | collective-permute-start | bytes 304136 | tf_op jit(solution)/shard_map/ppermute | solution.py:103
  248.9 5.5 %collective-permute-start.22 = (f32[4,8,528]{2,1,0:T(8,128)S(1)}, f32[4,8,528]{2,1,0:T(8,128)S(1)}, u32[]{:S(2)}, u32[]{:S(2)}) collective-permute-start(f32[4,8,528]{2,1,0:T(8,128)S(1)} %get-tuple-element.45), channel_id=1, source_target_pairs={{0,1},{1,0},{2,3},{3,2},{4,5},{5,4},{6,7},{7,6},{8,9},{9,8},{10,11... | collective-permute-start | bytes 202760 | tf_op jit(solution)/shard_map/ppermute | solution.py:103
  254.3 2.7 collective-permute-start.23
  257.1 4.9 %collective-permute-start.24 = (f32[4,8,528]{2,1,0:T(8,128)S(1)}, f32[4,8,528]{2,1,0:T(8,128)S(1)}, u32[]{:S(2)}, u32[]{:S(2)}) collective-permute-start(f32[4,8,528]{2,1,0:T(8,128)S(1)} %get-tuple-element.46), channel_id=1, source_target_pairs={{0,5},{1,4},{2,7},{3,6},{4,1},{5,0},{6,3},{7,2},{8,13},{9,12},{10,... | collective-permute-start | bytes 202760 | tf_op jit(solution)/shard_map/ppermute | solution.py:103
  264.2 8.1 %collective-permute-start.14 = (f32[3,2816]{1,0:T(4,128)S(1)}, f32[3,2816]{1,0:T(4,128)S(1)}, u32[]{:S(2)}, u32[]{:S(2)}) collective-permute-start(f32[3,2816]{1,0:T(4,128)S(1)} %slice.215), channel_id=1, source_target_pairs={{1,0},{2,1},{3,2},{4,3},{5,4},{6,5},{7,6},{8,7},{9,8},{10,9},{11,1... | collective-permute-start | bytes 101384 | tf_op jit(solution)/shard_map/ppermute | solution.py:13
  272.5 8.0 %collective-permute-start.25 = (f32[1,8,528]{2,1,0:T(8,128)S(1)}, f32[1,8,528]{2,1,0:T(8,128)S(1)}, u32[]{:S(2)}, u32[]{:S(2)}) collective-permute-start(f32[1,8,528]{2,1,0:T(8,128)S(1)} %get-tuple-element.59), channel_id=1, source_target_pairs={{0,2},{1,3},{2,0},{3,1},{4,6},{5,7},{6,4},{7,5},{8,10},{9,11},{10,... | collective-permute-start | bytes 50696 | tf_op jit(solution)/shard_map/ppermute | solution.py:103
  280.4 4.8 %collective-permute-start.26 = (f32[1,8,528]{2,1,0:T(8,128)S(1)}, f32[1,8,528]{2,1,0:T(8,128)S(1)}, u32[]{:S(2)}, u32[]{:S(2)}) collective-permute-start(f32[1,8,528]{2,1,0:T(8,128)S(1)} %get-tuple-element.61), channel_id=1, source_target_pairs={{0,8},{1,9},{2,10},{3,11},{4,12},{5,13},{6,14},{7,15},{8,0},{9,1},... | collective-permute-start | bytes 50696 | tf_op jit(solution)/shard_map/ppermute | solution.py:103
  285.2 6.7 %collective-permute-start.27 = (f32[1,8,528]{2,1,0:T(8,128)S(1)}, f32[1,8,528]{2,1,0:T(8,128)S(1)}, u32[]{:S(2)}, u32[]{:S(2)}) collective-permute-start(f32[1,8,528]{2,1,0:T(8,128)S(1)} %get-tuple-element.60), channel_id=1, source_target_pairs={{0,10},{1,11},{2,8},{3,9},{4,14},{5,15},{6,12},{7,13},{8,2},{9,3},... | collective-permute-start | bytes 50696 | tf_op jit(solution)/shard_map/ppermute | solution.py:103
  293.5 8.5 %collective-permute-done.27 = f32[1,8,528]{2,1,0:T(8,128)S(1)} collective-permute-done((f32[1,8,528]{2,1,0:T(8,128)S(1)}, f32[1,8,528]{2,1,0:T(8,128)S(1)}, u32[]{:S(2)}, u32[]{:S(2)}) %collective-permute-start.27) | collective-permute-done | bytes 16928 | tf_op jit(solution)/shard_map/ppermute | solution.py:103
  (157 shorter events, 61.9 us)
Async XLA Ops:
  5.3 10.8 %collective-permute-start = (bf16[24,176]{1,0:T(8,128)(2,1)S(1)}, bf16[24,176]{1,0:T(8,128)(2,1)S(1)}, u32[]{:S(2)}, u32[]{:S(2)}) collective-permute-start(bf16[24,176]{1,0:T(8,128)(2,1)S(1)} %concatenate.21), channel_id=1, source_target_pairs={{0,1},{1,0},{2,3},{3,2},{4,5},{5,4},{6,7},{7,6},{8,9},{9,8},{10,11... | collective-permute-start | bytes 25352 | tf_op jit(solution)/shard_map/ppermute | solution.py:103
  16.1 16.3 %collective-permute-start.1 = (bf16[2,24,176]{2,1,0:T(8,128)(2,1)S(1)}, bf16[2,24,176]{2,1,0:T(8,128)(2,1)S(1)}, u32[]{:S(2)}, u32[]{:S(2)}) collective-permute-start(bf16[2,24,176]{2,1,0:T(8,128)(2,1)S(1)} %get-tuple-element.72), channel_id=1, source_target_pairs={{0,2},{1,3},{2,0},{3,1},{4,6},{5,7},{6,4},{7,5},{8,10},{9,11},{10,... | collective-permute-start | bytes 50696 | tf_op jit(solution)/shard_map/ppermute | solution.py:103
  32.5 6.0 %collective-permute-start.2 = (bf16[2,2,24,176]{3,2,1,0:T(8,128)(2,1)S(1)}, bf16[2,2,24,176]{3,2,1,0:T(8,128)(2,1)S(1)}, u32[]{:S(2)}, u32[]{:S(2)}) collective-permute-start(bf16[2,2,24,176]{3,2,1,0:T(8,128)(2,1)S(1)} %get-tuple-element.68), channel_id=1, source_target_pairs={{0,4},{1,5},{2,6},{3,7},{4,0},{5,1},{6,2},{7,3},{8,12},{9,13},{10,... | collective-permute-start | bytes 101384 | tf_op jit(solution)/shard_map/ppermute | solution.py:103
  38.5 8.0 %collective-permute-start.3 = (bf16[2,2,2,24,176]{4,3,2,1,0:T(8,128)(2,1)S(1)}, bf16[2,2,2,24,176]{4,3,2,1,0:T(8,128)(2,1)S(1)}, u32[]{:S(2)}, u32[]{:S(2)}) collective-permute-start(bf16[2,2,2,24,176]{4,3,2,1,0:T(8,128)(2,1)S(1)} %get-tuple-element.55), channel_id=1, source_target_pairs={{0,8},{1,9},{2,10},{3,11},{4,12},{5,13},{6,14},{7,15},{8,0},{9,1},... | collective-permute-start | bytes 202760 | tf_op jit(solution)/shard_map/ppermute | solution.py:103
  47.1 8.7 %collective-permute-start.4 = (bf16[11,16,256]{2,0,1:T(8,128)(2,1)S(1)}, bf16[11,16,256]{2,0,1:T(8,128)(2,1)S(1)}, u32[]{:S(2)}, u32[]{:S(2)}) collective-permute-start(bf16[11,16,256]{2,0,1:T(8,128)(2,1)S(1)} %bitcast.189), channel_id=1, source_target_pairs={{0,256},{16,272},{32,288},{48,304},{64,320},{80,336},{96,352},{112... | collective-permute-start | bytes 270344 | tf_op jit(solution)/shard_map/ppermute | solution.py:103
  55.9 8.3 %collective-permute-start.5 = (bf16[2,11,16,256]{3,1,2,0:T(8,128)(2,1)S(1)}, bf16[2,11,16,256]{3,1,2,0:T(8,128)(2,1)S(1)}, u32[]{:S(2)}, u32[]{:S(2)}) collective-permute-start(bf16[2,11,16,256]{3,1,2,0:T(8,128)(2,1)S(1)} %get-tuple-element.48), channel_id=1, source_target_pairs={{0,128},{16,144},{32,160},{48,176},{64,192},{80,208},{96,224},{112... | collective-permute-start | bytes 540680 | tf_op jit(solution)/shard_map/ppermute | solution.py:103
  64.6 15.1 %collective-permute-start.6 = (bf16[2,2,11,16,256]{4,3,2,0,1:T(8,128)(2,1)S(1)}, bf16[2,2,11,16,256]{4,3,2,0,1:T(8,128)(2,1)S(1)}, u32[]{:S(2)}, u32[]{:S(2)}) collective-permute-start(bf16[2,2,11,16,256]{4,3,2,0,1:T(8,128)(2,1)S(1)} %get-tuple-element.43), channel_id=1, source_target_pairs={{0,64},{16,80},{32,96},{48,112},{64,0},{80,16},{96,32},{112,48},{1... | collective-permute-start | bytes 1081352 | tf_op jit(solution)/shard_map/ppermute | solution.py:103
  80.1 17.1 %collective-permute-start.7 = (bf16[2,2,2,11,16,256]{5,4,3,1,0,2:T(8,128)(2,1)S(1)}, bf16[2,2,2,11,16,256]{5,4,3,1,0,2:T(8,128)(2,1)S(1)}, u32[]{:S(2)}, u32[]{:S(2)}) collective-permute-start(bf16[2,2,2,11,16,256]{5,4,3,1,0,2:T(8,128)(2,1)S(1)} %get-tuple-element.34), channel_id=1, source_target_pairs={{0,32},{16,48},{32,0},{48,16},{64,96},{80,112},{96,64},{112,80},{1... | collective-permute-start | bytes 2162696 | tf_op jit(solution)/shard_map/ppermute | solution.py:103
  82.8 21.5 %collective-permute-start.9 = (bf16[3,2816]{1,0:T(4,128)(2,1)S(1)}, bf16[3,2816]{1,0:T(4,128)(2,1)S(1)}, u32[]{:S(2)}, u32[]{:S(2)}) collective-permute-start(bf16[3,2816]{1,0:T(4,128)(2,1)S(1)} %slice_bitcast_fusion.2), channel_id=1, source_target_pairs={{0,1},{1,2},{2,3},{3,4},{4,5},{5,6},{6,7},{7,8},{8,9},{9,10},{10,1... | collective-permute-start | bytes 50696 | tf_op jit(solution)/shard_map/ppermute | solution.py:13
  97.9 6.4 %copy-start.19 = (bf16[1,128,2816]{2,1,0:T(8,128)(2,1)S(1)}, bf16[1,128,2816]{2,1,0:T(8,128)(2,1)}, u32[]{:S(2)}) copy-start(bf16[1,128,2816]{2,1,0:T(8,128)(2,1)} %param.9) | copy-start | bytes 2162692
  99.2 10.1 %collective-permute-start.8 = (bf16[2,2,2,2,11,16,256]{6,5,4,2,1,0,3:T(8,128)(2,1)}, bf16[2,2,2,2,11,16,256]{6,5,4,2,1,0,3:T(8,128)(2,1)}, u32[]{:S(2)}, u32[]{:S(2)}) collective-permute-start(bf16[2,2,2,2,11,16,256]{6,5,4,2,1,0,3:T(8,128)(2,1)} %get-tuple-element.30), channel_id=1, source_target_pairs={{0,16},{16,0},{32,48},{48,32},{64,80},{80,64},{96,112},{112,96},{1... | collective-permute-start | bytes 4325384 | tf_op jit(solution)/shard_map/ppermute | solution.py:103
  112.6 1.1 copy-start.8
  112.8 2.7 copy-start.2
  112.8 5.6 %copy-start = (bf16[11,32,8,256]{3,2,0,1:T(8,128)(2,1)}, bf16[11,32,8,256]{3,2,0,1:T(8,128)(2,1)S(1)}, u32[]{:S(2)}) copy-start(bf16[11,32,8,256]{3,2,0,1:T(8,128)(2,1)S(1)} %get-tuple-element.20) | copy-start | bytes 4325380
  121.3 3.1 %copy-start.4 = (f32[128,2816]{1,0:T(8,128)S(1)}, f32[128,2816]{1,0:T(8,128)}, u32[]{:S(2)}) copy-start(f32[128,2816]{1,0:T(8,128)} %copy.130) | copy-start | bytes 4325380
  124.4 1.4 copy-start.5
  124.4 1.5 copy-start.16
  125.7 3.0 %copy-start.12 = (f32[128,2816]{1,0:T(8,128)}, f32[128,2816]{1,0:T(8,128)S(1)}, u32[]{:S(2)}) copy-start(f32[128,2816]{1,0:T(8,128)S(1)} %get-tuple-element.77) | copy-start | bytes 4325380
  125.7 5.3 %copy-start.18 = (f32[128,2816]{1,0:T(8,128)}, f32[128,2816]{1,0:T(8,128)S(1)}, u32[]{:S(2)}) copy-start(f32[128,2816]{1,0:T(8,128)S(1)} %get-tuple-element.76) | copy-start | bytes 4325380
  125.9 2.8 copy-start.20
  128.7 1.2 copy-start.17
  131.1 10.5 %collective-permute-start.10 = (f32[3,2816]{1,0:T(4,128)S(1)}, f32[3,2816]{1,0:T(4,128)S(1)}, u32[]{:S(2)}, u32[]{:S(2)}) collective-permute-start(f32[3,2816]{1,0:T(4,128)S(1)} %pad_maximum_fusion.10), channel_id=1, source_target_pairs={{0,1},{1,0},{2,3},{3,2},{4,5},{5,4},{6,7},{7,6},{8,9},{9,8},{10,11... | collective-permute-start | bytes 101384 | tf_op jit(solution)/shard_map/ppermute | solution.py:103
  142.7 15.0 %collective-permute-start.11 = (f32[3,2816]{1,0:T(4,128)S(1)}, f32[3,2816]{1,0:T(4,128)S(1)}, u32[]{:S(2)}, u32[]{:S(2)}) collective-permute-start(f32[3,2816]{1,0:T(4,128)S(1)} %pad_maximum_fusion.11), channel_id=1, source_target_pairs={{0,2},{1,3},{2,0},{3,1},{4,6},{5,7},{6,4},{7,5},{8,10},{9,11},{10,... | collective-permute-start | bytes 101384 | tf_op jit(solution)/shard_map/ppermute | solution.py:103
  157.7 5.9 %collective-permute-start.12 = (f32[3,2816]{1,0:T(4,128)S(1)}, f32[3,2816]{1,0:T(4,128)S(1)}, u32[]{:S(2)}, u32[]{:S(2)}) collective-permute-start(f32[3,2816]{1,0:T(4,128)S(1)} %pad_maximum_fusion.12), channel_id=1, source_target_pairs={{0,4},{1,5},{2,6},{3,7},{4,0},{5,1},{6,2},{7,3},{8,12},{9,13},{10,... | collective-permute-start | bytes 101384 | tf_op jit(solution)/shard_map/ppermute | solution.py:103
  163.8 7.4 %collective-permute-start.13 = (f32[3,2816]{1,0:T(4,128)S(1)}, f32[3,2816]{1,0:T(4,128)S(1)}, u32[]{:S(2)}, u32[]{:S(2)}) collective-permute-start(f32[3,2816]{1,0:T(4,128)S(1)} %pad_maximum_fusion.13), channel_id=1, source_target_pairs={{0,8},{1,9},{2,10},{3,11},{4,12},{5,13},{6,14},{7,15},{8,0},{9,1},... | collective-permute-start | bytes 101384 | tf_op jit(solution)/shard_map/ppermute | solution.py:103
  171.4 2.2 copy-start.6
  171.4 2.7 copy-start.10
  171.4 3.1 %copy-start.13 = (f32[128,2816]{1,0:T(8,128)S(1)}, f32[128,2816]{1,0:T(8,128)}, u32[]{:S(2)}) copy-start(f32[128,2816]{1,0:T(8,128)} %copy-done.12) | copy-start | bytes 4325380
  194.2 5.7 %collective-permute-start.15 = (f32[16,8,3168]{2,1,0:T(8,128)}, f32[16,8,3168]{2,1,0:T(8,128)}, u32[]{:S(2)}, u32[]{:S(2)}) collective-permute-start(f32[16,8,3168]{2,1,0:T(8,128)} %dynamic-slice_bitcast_fusion), channel_id=1, source_target_pairs={{0,16},{16,0},{32,48},{48,32},{64,80},{80,64},{96,112},{112,96},{1... | collective-permute-start | bytes 4866056 | tf_op jit(solution)/shard_map/ppermute | solution.py:103
  201.6 12.6 %copy-start.3 = (bf16[11,32,8,256]{3,2,0,1:T(8,128)(2,1)S(1)}, bf16[11,32,8,256]{3,2,0,1:T(8,128)(2,1)}, u32[]{:S(2)}) copy-start(bf16[11,32,8,256]{3,2,0,1:T(8,128)(2,1)} %copy-done.2) | copy-start | bytes 4325380
  202.6 14.5 %collective-permute-start.16 = (f32[4,8,3168]{2,1,0:T(8,128)}, f32[4,8,3168]{2,1,0:T(8,128)}, u32[]{:S(2)}, u32[]{:S(2)}) collective-permute-start(f32[4,8,3168]{2,1,0:T(8,128)} %get-tuple-element.23), channel_id=1, source_target_pairs={{0,32},{16,48},{32,0},{48,16},{64,96},{80,112},{96,64},{112,80},{1... | collective-permute-start | bytes 1216520 | tf_op jit(solution)/shard_map/ppermute | solution.py:103
  204.5 22.7 %collective-permute-start.17 = (f32[4,8,3168]{2,1,0:T(8,128)}, f32[4,8,3168]{2,1,0:T(8,128)}, u32[]{:S(2)}, u32[]{:S(2)}) collective-permute-start(f32[4,8,3168]{2,1,0:T(8,128)} %get-tuple-element.25), channel_id=1, source_target_pairs={{0,128},{16,144},{32,160},{48,176},{64,192},{80,208},{96,224},{112... | collective-permute-start | bytes 1216520 | tf_op jit(solution)/shard_map/ppermute | solution.py:103
  208.3 18.9 %collective-permute-start.18 = (f32[4,8,3168]{2,1,0:T(8,128)S(1)}, f32[4,8,3168]{2,1,0:T(8,128)}, u32[]{:S(2)}, u32[]{:S(2)}) collective-permute-start(f32[4,8,3168]{2,1,0:T(8,128)S(1)} %get-tuple-element.24), channel_id=1, source_target_pairs={{0,160},{16,176},{32,128},{48,144},{64,224},{80,240},{96,192},{112... | collective-permute-start | bytes 1216520 | tf_op jit(solution)/shard_map/ppermute | solution.py:103
  217.0 23.9 %copy-start.1 = (bf16[11,32,8,256]{3,2,0,1:T(8,128)(2,1)S(1)}, bf16[11,32,8,256]{3,2,0,1:T(8,128)(2,1)}, u32[]{:S(2)}) copy-start(bf16[11,32,8,256]{3,2,0,1:T(8,128)(2,1)} %copy-done) | copy-start | bytes 4325380
  217.0 23.9 %copy-start.15 = (bf16[128,2816]{0,1:T(8,128)(2,1)S(1)}, bf16[128,2816]{0,1:T(8,128)(2,1)}, u32[]{:S(2)}) copy-start(bf16[128,2816]{0,1:T(8,128)(2,1)} %copy.138) | copy-start | bytes 2162692
  229.2 16.1 %collective-permute-start.19 = (f32[1,8,3168]{2,1,0:T(8,128)}, f32[1,8,3168]{2,1,0:T(8,128)}, u32[]{:S(2)}, u32[]{:S(2)}) collective-permute-start(f32[1,8,3168]{2,1,0:T(8,128)} %get-tuple-element.40), channel_id=1, source_target_pairs={{0,64},{16,80},{32,96},{48,112},{64,0},{80,16},{96,32},{112,48},{1... | collective-permute-start | bytes 304136 | tf_op jit(solution)/shard_map/ppermute | solution.py:103
  233.8 11.5 %collective-permute-start.20 = (f32[1,8,3168]{2,1,0:T(8,128)}, f32[1,8,3168]{2,1,0:T(8,128)}, u32[]{:S(2)}, u32[]{:S(2)}) collective-permute-start(f32[1,8,3168]{2,1,0:T(8,128)} %get-tuple-element.42), channel_id=1, source_target_pairs={{0,256},{16,272},{32,288},{48,304},{64,320},{80,336},{96,352},{112... | collective-permute-start | bytes 304136 | tf_op jit(solution)/shard_map/ppermute | solution.py:103
  235.8 11.5 %collective-permute-start.21 = (f32[1,8,3168]{2,1,0:T(8,128)S(1)}, f32[1,8,3168]{2,1,0:T(8,128)}, u32[]{:S(2)}, u32[]{:S(2)}) collective-permute-start(f32[1,8,3168]{2,1,0:T(8,128)S(1)} %get-tuple-element.41), channel_id=1, source_target_pairs={{0,320},{16,336},{32,352},{48,368},{64,256},{80,272},{96,288},{112... | collective-permute-start | bytes 304136 | tf_op jit(solution)/shard_map/ppermute | solution.py:103
  240.9 1.4 copy-start.11
  247.2 14.8 %copy-start.14 = (f32[128,2816]{1,0:T(8,128)S(1)}, f32[128,2816]{1,0:T(8,128)}, u32[]{:S(2)}) copy-start(f32[128,2816]{1,0:T(8,128)} %copy.137) | copy-start | bytes 4325380
  248.4 13.6 %copy-start.7 = (f32[128,2816]{1,0:T(8,128)S(1)}, f32[128,2816]{1,0:T(8,128)}, u32[]{:S(2)}) copy-start(f32[128,2816]{1,0:T(8,128)} %copy.134) | copy-start | bytes 4325380
  248.9 23.5 %collective-permute-start.22 = (f32[4,8,528]{2,1,0:T(8,128)S(1)}, f32[4,8,528]{2,1,0:T(8,128)S(1)}, u32[]{:S(2)}, u32[]{:S(2)}) collective-permute-start(f32[4,8,528]{2,1,0:T(8,128)S(1)} %get-tuple-element.45), channel_id=1, source_target_pairs={{0,1},{1,0},{2,3},{3,2},{4,5},{5,4},{6,7},{7,6},{8,9},{9,8},{10,11... | collective-permute-start | bytes 202760 | tf_op jit(solution)/shard_map/ppermute | solution.py:103
  254.3 18.1 %collective-permute-start.23 = (f32[4,8,528]{2,1,0:T(8,128)S(1)}, f32[4,8,528]{2,1,0:T(8,128)S(1)}, u32[]{:S(2)}, u32[]{:S(2)}) collective-permute-start(f32[4,8,528]{2,1,0:T(8,128)S(1)} %get-tuple-element.47), channel_id=1, source_target_pairs={{0,4},{1,5},{2,6},{3,7},{4,0},{5,1},{6,2},{7,3},{8,12},{9,13},{10,... | collective-permute-start | bytes 202760 | tf_op jit(solution)/shard_map/ppermute | solution.py:103
  257.1 15.3 %collective-permute-start.24 = (f32[4,8,528]{2,1,0:T(8,128)S(1)}, f32[4,8,528]{2,1,0:T(8,128)S(1)}, u32[]{:S(2)}, u32[]{:S(2)}) collective-permute-start(f32[4,8,528]{2,1,0:T(8,128)S(1)} %get-tuple-element.46), channel_id=1, source_target_pairs={{0,5},{1,4},{2,7},{3,6},{4,1},{5,0},{6,3},{7,2},{8,13},{9,12},{10,... | collective-permute-start | bytes 202760 | tf_op jit(solution)/shard_map/ppermute | solution.py:103
  264.2 27.7 %collective-permute-start.14 = (f32[3,2816]{1,0:T(4,128)S(1)}, f32[3,2816]{1,0:T(4,128)S(1)}, u32[]{:S(2)}, u32[]{:S(2)}) collective-permute-start(f32[3,2816]{1,0:T(4,128)S(1)} %slice.215), channel_id=1, source_target_pairs={{1,0},{2,1},{3,2},{4,3},{5,4},{6,5},{7,6},{8,7},{9,8},{10,9},{11,1... | collective-permute-start | bytes 101384 | tf_op jit(solution)/shard_map/ppermute | solution.py:13
  272.5 21.0 %collective-permute-start.25 = (f32[1,8,528]{2,1,0:T(8,128)S(1)}, f32[1,8,528]{2,1,0:T(8,128)S(1)}, u32[]{:S(2)}, u32[]{:S(2)}) collective-permute-start(f32[1,8,528]{2,1,0:T(8,128)S(1)} %get-tuple-element.59), channel_id=1, source_target_pairs={{0,2},{1,3},{2,0},{3,1},{4,6},{5,7},{6,4},{7,5},{8,10},{9,11},{10,... | collective-permute-start | bytes 50696 | tf_op jit(solution)/shard_map/ppermute | solution.py:103
  280.4 13.0 %collective-permute-start.26 = (f32[1,8,528]{2,1,0:T(8,128)S(1)}, f32[1,8,528]{2,1,0:T(8,128)S(1)}, u32[]{:S(2)}, u32[]{:S(2)}) collective-permute-start(f32[1,8,528]{2,1,0:T(8,128)S(1)} %get-tuple-element.61), channel_id=1, source_target_pairs={{0,8},{1,9},{2,10},{3,11},{4,12},{5,13},{6,14},{7,15},{8,0},{9,1},... | collective-permute-start | bytes 50696 | tf_op jit(solution)/shard_map/ppermute | solution.py:103
  285.2 16.8 %collective-permute-start.27 = (f32[1,8,528]{2,1,0:T(8,128)S(1)}, f32[1,8,528]{2,1,0:T(8,128)S(1)}, u32[]{:S(2)}, u32[]{:S(2)}) collective-permute-start(f32[1,8,528]{2,1,0:T(8,128)S(1)} %get-tuple-element.60), channel_id=1, source_target_pairs={{0,10},{1,11},{2,8},{3,9},{4,14},{5,15},{6,12},{7,13},{8,2},{9,3},... | collective-permute-start | bytes 50696 | tf_op jit(solution)/shard_map/ppermute | solution.py:103
  (1 other events, 1.1 us)

commit v3 on v2

--- a/solution.py
+++ b/solution.py
@@ -85,6 +85,11 @@
     return steps
 
 
+def near_last(length):
+    single = [[b] for b in [stride for step in spread_steps(length, 1) for stride in step]]
+    return single[::-1]
+
+
 def bit_steps(length):
     return [[stride] for step in digit_steps(length) for stride in step]
 
@@ -203,7 +208,7 @@
     by_ctx = by_ctx.transpose(1, 0, 2).reshape(joined.shape[0], width)
     params = by_ctx[2 * rows :]
     heads = by_ctx[: 2 * rows].reshape(2 * rows, -1, head_width).transpose(1, 0, 2)
-    by_dp = gathered_by_doubling(heads, "dp", bit_steps(dp_size)[::-1])
+    by_dp = gathered_by_doubling(heads, "dp", near_last(dp_size))
     head_count = heads.shape[0]
 
     def head_major(part):
@@ -266,7 +271,7 @@
     by_row = local_wgrad.reshape(dp_size, rows, width)
     row_sum, rgrad = summed_apart(by_row, local_rgrad, "dp", spread_steps(dp_size, 1))
     by_channel = row_sum.reshape(rows, ctx_size, cols).transpose(1, 0, 2)
-    wgrad, rgrad = summed_apart(by_channel, rgrad, "ctx", spread_steps(ctx_size, 0))
+    wgrad, rgrad = summed_apart(by_channel, rgrad, "ctx", digit_steps(ctx_size))
     return (grad_in.astype(jnp.bfloat16)[None], wgrad, rgrad)
 
 

time: 307 us -> 290 us (0.945)
  waiting for transfers between devices: 85.4 us -> 67.1 us
    ppermute x26, waiting for transfers between devices: 82.4 us -> 64.1 us  [exchanged(): return lax.ppermute(array, axis, [(i, i ^ mask) for i in range(length)])]
where the time goes in v3:
time: 290 us; the launch traced here: 286 us
  starting transfers between devices  136 us (47%)
  waiting for transfers between devices  67.1 us (23%)
  local copies, waits for them, and re-layouts  39.4 us (14%)
  other arithmetic  26.7 us (9%)
  matrix products  15 us (5%)
    ppermute x26, starting transfers between devices, exchanged(): return lax.ppermute(array, axis, [(i, i ^ mask) for i in range(length)])  121 us
    ppermute x26, waiting for transfers between devices, exchanged(): return lax.ppermute(array, axis, [(i, i ^ mask) for i in range(length)])  64.1 us
    ppermute x2, starting transfers between devices, passed_along(): return lax.ppermute(array, axis, pairs)  15.6 us
    reshape x2, local copies, waits for them, and re-layouts, mix_heads(): return result.reshape(tokens, head_count * head_width)  6.01 us
  transfers between devices with their start and end apart: 28, of which 18 were waited for; matrix products, arithmetic and copies ran while one was open for 7% of the time, Pallas kernels for 0%

profile of v3, /device:TPU:6, one launch (start us, length us, event | category | flops | bytes accessed | tf_op | source)
XLA Modules:
  0.0 286.4 jit_solution(12607498597056998131)
XLA Ops:
  5.3 9.1 %collective-permute-start = (bf16[24,176]{1,0:T(8,128)(2,1)S(1)}, bf16[24,176]{1,0:T(8,128)(2,1)S(1)}, u32[]{:S(2)}, u32[]{:S(2)}) collective-permute-start(bf16[24,176]{1,0:T(8,128)(2,1)S(1)} %concatenate.21), channel_id=1, source_target_pairs={{0,1},{1,0},{2,3},{3,2},{4,5},{5,4},{6,7},{7,6},{8,9},{9,8},{10,11... | collective-permute-start | bytes 25352 | tf_op jit(solution)/shard_map/ppermute | solution.py:108
  16.1 14.5 %collective-permute-start.1 = (bf16[2,24,176]{2,1,0:T(8,128)(2,1)S(1)}, bf16[2,24,176]{2,1,0:T(8,128)(2,1)S(1)}, u32[]{:S(2)}, u32[]{:S(2)}) collective-permute-start(bf16[2,24,176]{2,1,0:T(8,128)(2,1)S(1)} %get-tuple-element.72), channel_id=1, source_target_pairs={{0,2},{1,3},{2,0},{3,1},{4,6},{5,7},{6,4},{7,5},{8,10},{9,11},{10,... | collective-permute-start | bytes 50696 | tf_op jit(solution)/shard_map/ppermute | solution.py:108
  32.5 2.7 collective-permute-start.2
  35.2 3.2 %collective-permute-done.2 = bf16[2,2,24,176]{3,2,1,0:T(8,128)(2,1)S(1)} collective-permute-done((bf16[2,2,24,176]{3,2,1,0:T(8,128)(2,1)S(1)}, bf16[2,2,24,176]{3,2,1,0:T(8,128)(2,1)S(1)}, u32[]{:S(2)}, u32[]{:S(2)}) %collective-permute-start.2) | collective-permute-done | bytes 33824 | tf_op jit(solution)/shard_map/ppermute | solution.py:108
  38.5 4.2 %collective-permute-start.3 = (bf16[2,2,2,24,176]{4,3,2,1,0:T(8,128)(2,1)S(1)}, bf16[2,2,2,24,176]{4,3,2,1,0:T(8,128)(2,1)S(1)}, u32[]{:S(2)}, u32[]{:S(2)}) collective-permute-start(bf16[2,2,2,24,176]{4,3,2,1,0:T(8,128)(2,1)S(1)} %get-tuple-element.55), channel_id=1, source_target_pairs={{0,8},{1,9},{2,10},{3,11},{4,12},{5,13},{6,14},{7,15},{8,0},{9,1},... | collective-permute-start | bytes 202760 | tf_op jit(solution)/shard_map/ppermute | solution.py:108
  42.8 3.8 %collective-permute-done.3 = bf16[2,2,2,24,176]{4,3,2,1,0:T(8,128)(2,1)S(1)} collective-permute-done((bf16[2,2,2,24,176]{4,3,2,1,0:T(8,128)(2,1)S(1)}, bf16[2,2,2,24,176]{4,3,2,1,0:T(8,128)(2,1)S(1)}, u32[]{:S(2)}, u32[]{:S(2)}) %collective-permute-start.3) | collective-permute-done | bytes 67616 | tf_op jit(solution)/shard_map/ppermute | solution.py:108
  47.1 5.1 %collective-permute-start.4 = (bf16[11,16,256]{2,0,1:T(8,128)(2,1)S(1)}, bf16[11,16,256]{2,0,1:T(8,128)(2,1)S(1)}, u32[]{:S(2)}, u32[]{:S(2)}) collective-permute-start(bf16[11,16,256]{2,0,1:T(8,128)(2,1)S(1)} %bitcast.191), channel_id=1, source_target_pairs={{0,256},{16,272},{32,288},{48,304},{64,320},{80,336},{96,352},{112... | collective-permute-start | bytes 270344 | tf_op jit(solution)/shard_map/ppermute | solution.py:108
  52.2 3.2 %collective-permute-done.4 = bf16[11,16,256]{2,0,1:T(8,128)(2,1)S(1)} collective-permute-done((bf16[11,16,256]{2,0,1:T(8,128)(2,1)S(1)}, bf16[11,16,256]{2,0,1:T(8,128)(2,1)S(1)}, u32[]{:S(2)}, u32[]{:S(2)}) %collective-permute-start.4) | collective-permute-done | bytes 90144 | tf_op jit(solution)/shard_map/ppermute | solution.py:108
  55.6 3.4 %collective-permute-start.5 = (bf16[2,11,16,256]{3,1,2,0:T(8,128)(2,1)S(1)}, bf16[2,11,16,256]{3,1,2,0:T(8,128)(2,1)S(1)}, u32[]{:S(2)}, u32[]{:S(2)}) collective-permute-start(bf16[2,11,16,256]{3,1,2,0:T(8,128)(2,1)S(1)} %get-tuple-element.48), channel_id=1, source_target_pairs={{0,64},{16,80},{32,96},{48,112},{64,0},{80,16},{96,32},{112,48},{1... | collective-permute-start | bytes 540680 | tf_op jit(solution)/shard_map/ppermute | solution.py:108
  59.0 8.5 %collective-permute-done.5 = bf16[2,11,16,256]{3,1,2,0:T(8,128)(2,1)S(1)} collective-permute-done((bf16[2,11,16,256]{3,1,2,0:T(8,128)(2,1)S(1)}, bf16[2,11,16,256]{3,1,2,0:T(8,128)(2,1)S(1)}, u32[]{:S(2)}, u32[]{:S(2)}) %collective-permute-start.5) | collective-permute-done | bytes 180256 | tf_op jit(solution)/shard_map/ppermute | solution.py:108
  68.0 3.5 %collective-permute-start.6 = (bf16[2,2,11,16,256]{4,3,2,0,1:T(8,128)(2,1)S(1)}, bf16[2,2,11,16,256]{4,3,2,0,1:T(8,128)(2,1)S(1)}, u32[]{:S(2)}, u32[]{:S(2)}) collective-permute-start(bf16[2,2,11,16,256]{4,3,2,0,1:T(8,128)(2,1)S(1)} %get-tuple-element.43), channel_id=1, source_target_pairs={{0,128},{16,144},{32,160},{48,176},{64,192},{80,208},{96,224},{112... | collective-permute-start | bytes 1081352 | tf_op jit(solution)/shard_map/ppermute | solution.py:108
  71.5 5.8 %collective-permute-done.6 = bf16[2,2,11,16,256]{4,3,2,0,1:T(8,128)(2,1)S(1)} collective-permute-done((bf16[2,2,11,16,256]{4,3,2,0,1:T(8,128)(2,1)S(1)}, bf16[2,2,11,16,256]{4,3,2,0,1:T(8,128)(2,1)S(1)}, u32[]{:S(2)}, u32[]{:S(2)}) %collective-permute-start.6) | collective-permute-done | bytes 360480 | tf_op jit(solution)/shard_map/ppermute | solution.py:108
  80.5 7.4 %collective-permute-start.9 = (bf16[3,2816]{1,0:T(4,128)(2,1)S(1)}, bf16[3,2816]{1,0:T(4,128)(2,1)S(1)}, u32[]{:S(2)}, u32[]{:S(2)}) collective-permute-start(bf16[3,2816]{1,0:T(4,128)(2,1)S(1)} %slice_bitcast_fusion.2), channel_id=1, source_target_pairs={{0,1},{1,2},{2,3},{3,4},{4,5},{5,6},{6,7},{7,8},{8,9},{9,10},{10,1... | collective-permute-start | bytes 50696 | tf_op jit(solution)/shard_map/ppermute | solution.py:13
  87.9 3.0 %collective-permute-done.7 = bf16[2,2,2,11,16,256]{5,4,3,1,0,2:T(8,128)(2,1)S(1)} collective-permute-done((bf16[2,2,2,11,16,256]{5,4,3,1,0,2:T(8,128)(2,1)S(1)}, bf16[2,2,2,11,16,256]{5,4,3,1,0,2:T(8,128)(2,1)S(1)}, u32[]{:S(2)}, u32[]{:S(2)}) %collective-permute-start.7) | collective-permute-done | bytes 720928 | tf_op jit(solution)/shard_map/ppermute | solution.py:108
  95.0 3.0 %collective-permute-done.9 = bf16[3,2816]{1,0:T(4,128)(2,1)S(1)} collective-permute-done((bf16[3,2816]{1,0:T(4,128)(2,1)S(1)}, bf16[3,2816]{1,0:T(4,128)(2,1)S(1)}, u32[]{:S(2)}, u32[]{:S(2)}) %collective-permute-start.9) | collective-permute-done | bytes 16928 | tf_op jit(solution)/shard_map/ppermute | solution.py:13
  103.0 2.4 fusion.17
  109.2 2.9 %copy.124 = f32[128,2816]{1,0:T(8,128)} copy(f32[128,2816]{0,1:T(8,128)} %bitcast.175) | data formatting | bytes 2883584 | tf_op jit(solution)/shard_map/reshape | solution.py:21
  112.1 2.9 %fusion.28 = f32[11,256,128]{2,1,0:T(8,128)} fusion(bf16[128,11,256]{0,2,1:T(8,128)(2,1)} %bitcast.165, bf16[11,32,8,256]{3,2,0,1:T(8,128)(2,1)S(1)} %get-tuple-element.20), kind=kOutput, calls=%fused_computation.61 | convolution fusion | flops 184549376 | bytes 3604480 | tf_op jit(solution)/shard_map/thk,hkj->thj/dot_general | solution.py:20
  115.0 3.1 %copy.128 = f32[128,2816]{1,0:T(8,128)} copy(f32[128,2816]{0,1:T(8,128)} %bitcast.176) | data formatting | bytes 2883584 | tf_op jit(solution)/shard_map/reshape | solution.py:21
  119.7 2.8 convolution_multiply_fusion
  124.8 3.5 %collective-permute-start.10 = (f32[3,2816]{1,0:T(4,128)S(1)}, f32[3,2816]{1,0:T(4,128)S(1)}, u32[]{:S(2)}, u32[]{:S(2)}) collective-permute-start(f32[3,2816]{1,0:T(4,128)S(1)} %pad_maximum_fusion.9), channel_id=1, source_target_pairs={{0,1},{1,0},{2,3},{3,2},{4,5},{5,4},{6,7},{7,6},{8,9},{9,8},{10,11... | collective-permute-start | bytes 101384 | tf_op jit(solution)/shard_map/ppermute | solution.py:108
  128.3 6.6 %collective-permute-done.10 = f32[3,2816]{1,0:T(4,128)S(1)} collective-permute-done((f32[3,2816]{1,0:T(4,128)S(1)}, f32[3,2816]{1,0:T(4,128)S(1)}, u32[]{:S(2)}, u32[]{:S(2)}) %collective-permute-start.10) | collective-permute-done | bytes 33824 | tf_op jit(solution)/shard_map/ppermute | solution.py:108
  136.0 12.1 %collective-permute-start.11 = (f32[3,2816]{1,0:T(4,128)S(1)}, f32[3,2816]{1,0:T(4,128)S(1)}, u32[]{:S(2)}, u32[]{:S(2)}) collective-permute-start(f32[3,2816]{1,0:T(4,128)S(1)} %pad_maximum_fusion.10), channel_id=1, source_target_pairs={{0,2},{1,3},{2,0},{3,1},{4,6},{5,7},{6,4},{7,5},{8,10},{9,11},{10,... | collective-permute-start | bytes 101384 | tf_op jit(solution)/shard_map/ppermute | solution.py:108
  148.1 2.5 collective-permute-done.11
  150.8 2.7 collective-permute-start.12
  153.5 3.2 %collective-permute-done.12 = f32[3,2816]{1,0:T(4,128)S(1)} collective-permute-done((f32[3,2816]{1,0:T(4,128)S(1)}, f32[3,2816]{1,0:T(4,128)S(1)}, u32[]{:S(2)}, u32[]{:S(2)}) %collective-permute-start.12) | collective-permute-done | bytes 33824 | tf_op jit(solution)/shard_map/ppermute | solution.py:108
  156.8 3.5 %collective-permute-start.13 = (f32[3,2816]{1,0:T(4,128)S(1)}, f32[3,2816]{1,0:T(4,128)S(1)}, u32[]{:S(2)}, u32[]{:S(2)}) collective-permute-start(f32[3,2816]{1,0:T(4,128)S(1)} %pad_maximum_fusion.12), channel_id=1, source_target_pairs={{0,8},{1,9},{2,10},{3,11},{4,12},{5,13},{6,14},{7,15},{8,0},{9,1},... | collective-permute-start | bytes 101384 | tf_op jit(solution)/shard_map/ppermute | solution.py:108
  160.3 3.9 %collective-permute-done.13 = f32[3,2816]{1,0:T(4,128)S(1)} collective-permute-done((f32[3,2816]{1,0:T(4,128)S(1)}, f32[3,2816]{1,0:T(4,128)S(1)}, u32[]{:S(2)}, u32[]{:S(2)}) %collective-permute-start.13) | collective-permute-done | bytes 33824 | tf_op jit(solution)/shard_map/ppermute | solution.py:108
  167.5 4.6 %multiply_reduce_fusion = (f32[2816]{0:T(1024)S(1)}, f32[128,2816]{1,0:T(8,128)S(1)}, bf16[128,2816]{1,0:T(8,128)(2,1)}, f32[128,2816]{1,0:T(8,128)}) fusion(f32[128,2816]{1,0:T(8,128)S(1)} %copy-done.4, f32[2816]{0:T(1024)S(1)} %add.402, f32[128,2816]{1,0:T(8,128)S(1)} %copy-done.6, f32[2816]{0:T(1024)S(1)} %add.406, f32[2816]{0:T(1024)S(1)} %mul.339, ...), kind=kLoop, calls=%fused_computation.69 | loop fusion | flops 17659136 | bytes 16704512 | tf_op jit(solution)/shard_map/reduce_sum | solution.py:270
  175.6 3.4 %copy.136 = f32[256,11,256]{2,1,0:T(8,128)} copy(f32[256,11,256]{0,2,1:T(8,128)S(1)} %convolution_bitcast_fusion) | data formatting | bytes 5767168 | tf_op jit(solution)/shard_map/thk,thj->khj/transpose | solution.py:37
  179.0 4.7 %concatenate.25 = f32[2,2,2,2,2,8,2816]{6,5,4,3,2,1,0:T(8,128)} reshape(f32[256,11,256]{2,1,0:T(8,128)} %copy.136) | data formatting | bytes 5767168 | tf_op jit(solution)/shard_map/concatenate | solution.py:185
  189.1 3.8 %collective-permute-done.15 = f32[16,8,3168]{2,1,0:T(8,128)} collective-permute-done((f32[16,8,3168]{2,1,0:T(8,128)}, f32[16,8,3168]{2,1,0:T(8,128)}, u32[]{:S(2)}, u32[]{:S(2)}) %collective-permute-start.15) | collective-permute-done | bytes 1622048 | tf_op jit(solution)/shard_map/ppermute | solution.py:108
  197.5 3.5 %collective-permute-start.17 = (f32[4,8,3168]{2,1,0:T(8,128)}, f32[4,8,3168]{2,1,0:T(8,128)}, u32[]{:S(2)}, u32[]{:S(2)}) collective-permute-start(f32[4,8,3168]{2,1,0:T(8,128)} %get-tuple-element.25), channel_id=1, source_target_pairs={{0,128},{16,144},{32,160},{48,176},{64,192},{80,208},{96,224},{112... | collective-permute-start | bytes 1216520 | tf_op jit(solution)/shard_map/ppermute | solution.py:108
  201.0 3.8 %collective-permute-start.18 = (f32[4,8,3168]{2,1,0:T(8,128)S(1)}, f32[4,8,3168]{2,1,0:T(8,128)}, u32[]{:S(2)}, u32[]{:S(2)}) collective-permute-start(f32[4,8,3168]{2,1,0:T(8,128)S(1)} %get-tuple-element.24), channel_id=1, source_target_pairs={{0,160},{16,176},{32,128},{48,144},{64,224},{80,240},{96,192},{112... | collective-permute-start | bytes 1216520 | tf_op jit(solution)/shard_map/ppermute | solution.py:108
  204.9 2.3 copy.132
  207.2 2.8 fusion.30
  210.1 9.9 %collective-permute-done.17 = f32[4,8,3168]{2,1,0:T(8,128)} collective-permute-done((f32[4,8,3168]{2,1,0:T(8,128)}, f32[4,8,3168]{2,1,0:T(8,128)}, u32[]{:S(2)}, u32[]{:S(2)}) %collective-permute-start.17) | collective-permute-done | bytes 405536 | tf_op jit(solution)/shard_map/ppermute | solution.py:108
  222.1 3.9 %collective-permute-start.19 = (f32[1,8,3168]{2,1,0:T(8,128)}, f32[1,8,3168]{2,1,0:T(8,128)}, u32[]{:S(2)}, u32[]{:S(2)}) collective-permute-start(f32[1,8,3168]{2,1,0:T(8,128)} %get-tuple-element.40), channel_id=1, source_target_pairs={{0,64},{16,80},{32,96},{48,112},{64,0},{80,16},{96,32},{112,48},{1... | collective-permute-start | bytes 304136 | tf_op jit(solution)/shard_map/ppermute | solution.py:108
  226.0 5.1 %collective-permute-start.20 = (f32[1,8,3168]{2,1,0:T(8,128)}, f32[1,8,3168]{2,1,0:T(8,128)}, u32[]{:S(2)}, u32[]{:S(2)}) collective-permute-start(f32[1,8,3168]{2,1,0:T(8,128)} %get-tuple-element.42), channel_id=1, source_target_pairs={{0,256},{16,272},{32,288},{48,304},{64,320},{80,336},{96,352},{112... | collective-permute-start | bytes 304136 | tf_op jit(solution)/shard_map/ppermute | solution.py:108
  231.1 2.6 collective-permute-start.21
  238.2 2.8 collective-permute-done.21
  242.5 8.0 %collective-permute-start.22 = (f32[4,8,528]{2,1,0:T(8,128)S(1)}, f32[4,8,528]{2,1,0:T(8,128)S(1)}, u32[]{:S(2)}, u32[]{:S(2)}) collective-permute-start(f32[4,8,528]{2,1,0:T(8,128)S(1)} %get-tuple-element.45), channel_id=1, source_target_pairs={{0,1},{1,0},{2,3},{3,2},{4,5},{5,4},{6,7},{7,6},{8,9},{9,8},{10,11... | collective-permute-start | bytes 202760 | tf_op jit(solution)/shard_map/ppermute | solution.py:108
  250.6 9.4 %collective-permute-start.23 = (f32[4,8,528]{2,1,0:T(8,128)S(1)}, f32[4,8,528]{2,1,0:T(8,128)S(1)}, u32[]{:S(2)}, u32[]{:S(2)}) collective-permute-start(f32[4,8,528]{2,1,0:T(8,128)S(1)} %get-tuple-element.47), channel_id=1, source_target_pairs={{0,2},{1,3},{2,0},{3,1},{4,6},{5,7},{6,4},{7,5},{8,10},{9,11},{10,... | collective-permute-start | bytes 202760 | tf_op jit(solution)/shard_map/ppermute | solution.py:108
  261.9 2.6 add_add_fusion
  264.5 8.2 %collective-permute-start.14 = (f32[3,2816]{1,0:T(4,128)S(1)}, f32[3,2816]{1,0:T(4,128)S(1)}, u32[]{:S(2)}, u32[]{:S(2)}) collective-permute-start(f32[3,2816]{1,0:T(4,128)S(1)} %slice.215), channel_id=1, source_target_pairs={{1,0},{2,1},{3,2},{4,3},{5,4},{6,5},{7,6},{8,7},{9,8},{10,9},{11,1... | collective-permute-start | bytes 101384 | tf_op jit(solution)/shard_map/ppermute | solution.py:13
  272.8 2.4 collective-permute-start.25
  275.3 2.5 collective-permute-start.26
  277.8 5.5 %collective-permute-start.27 = (f32[1,8,528]{2,1,0:T(8,128)S(1)}, f32[1,8,528]{2,1,0:T(8,128)S(1)}, u32[]{:S(2)}, u32[]{:S(2)}) collective-permute-start(f32[1,8,528]{2,1,0:T(8,128)S(1)} %get-tuple-element.60), channel_id=1, source_target_pairs={{0,12},{1,13},{2,14},{3,15},{4,8},{5,9},{6,10},{7,11},{8,4},{9,5},... | collective-permute-start | bytes 50696 | tf_op jit(solution)/shard_map/ppermute | solution.py:108
  (154 shorter events, 60.1 us)
Async XLA Ops:
  5.3 10.8 %collective-permute-start = (bf16[24,176]{1,0:T(8,128)(2,1)S(1)}, bf16[24,176]{1,0:T(8,128)(2,1)S(1)}, u32[]{:S(2)}, u32[]{:S(2)}) collective-permute-start(bf16[24,176]{1,0:T(8,128)(2,1)S(1)} %concatenate.21), channel_id=1, source_target_pairs={{0,1},{1,0},{2,3},{3,2},{4,5},{5,4},{6,7},{7,6},{8,9},{9,8},{10,11... | collective-permute-start | bytes 25352 | tf_op jit(solution)/shard_map/ppermute | solution.py:108
  16.1 16.3 %collective-permute-start.1 = (bf16[2,24,176]{2,1,0:T(8,128)(2,1)S(1)}, bf16[2,24,176]{2,1,0:T(8,128)(2,1)S(1)}, u32[]{:S(2)}, u32[]{:S(2)}) collective-permute-start(bf16[2,24,176]{2,1,0:T(8,128)(2,1)S(1)} %get-tuple-element.72), channel_id=1, source_target_pairs={{0,2},{1,3},{2,0},{3,1},{4,6},{5,7},{6,4},{7,5},{8,10},{9,11},{10,... | collective-permute-start | bytes 50696 | tf_op jit(solution)/shard_map/ppermute | solution.py:108
  32.5 6.0 %collective-permute-start.2 = (bf16[2,2,24,176]{3,2,1,0:T(8,128)(2,1)S(1)}, bf16[2,2,24,176]{3,2,1,0:T(8,128)(2,1)S(1)}, u32[]{:S(2)}, u32[]{:S(2)}) collective-permute-start(bf16[2,2,24,176]{3,2,1,0:T(8,128)(2,1)S(1)} %get-tuple-element.68), channel_id=1, source_target_pairs={{0,4},{1,5},{2,6},{3,7},{4,0},{5,1},{6,2},{7,3},{8,12},{9,13},{10,... | collective-permute-start | bytes 101384 | tf_op jit(solution)/shard_map/ppermute | solution.py:108
  38.5 8.0 %collective-permute-start.3 = (bf16[2,2,2,24,176]{4,3,2,1,0:T(8,128)(2,1)S(1)}, bf16[2,2,2,24,176]{4,3,2,1,0:T(8,128)(2,1)S(1)}, u32[]{:S(2)}, u32[]{:S(2)}) collective-permute-start(bf16[2,2,2,24,176]{4,3,2,1,0:T(8,128)(2,1)S(1)} %get-tuple-element.55), channel_id=1, source_target_pairs={{0,8},{1,9},{2,10},{3,11},{4,12},{5,13},{6,14},{7,15},{8,0},{9,1},... | collective-permute-start | bytes 202760 | tf_op jit(solution)/shard_map/ppermute | solution.py:108
  47.1 8.4 %collective-permute-start.4 = (bf16[11,16,256]{2,0,1:T(8,128)(2,1)S(1)}, bf16[11,16,256]{2,0,1:T(8,128)(2,1)S(1)}, u32[]{:S(2)}, u32[]{:S(2)}) collective-permute-start(bf16[11,16,256]{2,0,1:T(8,128)(2,1)S(1)} %bitcast.191), channel_id=1, source_target_pairs={{0,256},{16,272},{32,288},{48,304},{64,320},{80,336},{96,352},{112... | collective-permute-start | bytes 270344 | tf_op jit(solution)/shard_map/ppermute | solution.py:108
  55.6 12.0 %collective-permute-start.5 = (bf16[2,11,16,256]{3,1,2,0:T(8,128)(2,1)S(1)}, bf16[2,11,16,256]{3,1,2,0:T(8,128)(2,1)S(1)}, u32[]{:S(2)}, u32[]{:S(2)}) collective-permute-start(bf16[2,11,16,256]{3,1,2,0:T(8,128)(2,1)S(1)} %get-tuple-element.48), channel_id=1, source_target_pairs={{0,64},{16,80},{32,96},{48,112},{64,0},{80,16},{96,32},{112,48},{1... | collective-permute-start | bytes 540680 | tf_op jit(solution)/shard_map/ppermute | solution.py:108
  68.0 9.3 %collective-permute-start.6 = (bf16[2,2,11,16,256]{4,3,2,0,1:T(8,128)(2,1)S(1)}, bf16[2,2,11,16,256]{4,3,2,0,1:T(8,128)(2,1)S(1)}, u32[]{:S(2)}, u32[]{:S(2)}) collective-permute-start(bf16[2,2,11,16,256]{4,3,2,0,1:T(8,128)(2,1)S(1)} %get-tuple-element.43), channel_id=1, source_target_pairs={{0,128},{16,144},{32,160},{48,176},{64,192},{80,208},{96,224},{112... | collective-permute-start | bytes 1081352 | tf_op jit(solution)/shard_map/ppermute | solution.py:108
  77.7 13.2 %collective-permute-start.7 = (bf16[2,2,2,11,16,256]{5,4,3,1,0,2:T(8,128)(2,1)S(1)}, bf16[2,2,2,11,16,256]{5,4,3,1,0,2:T(8,128)(2,1)S(1)}, u32[]{:S(2)}, u32[]{:S(2)}) collective-permute-start(bf16[2,2,2,11,16,256]{5,4,3,1,0,2:T(8,128)(2,1)S(1)} %get-tuple-element.34), channel_id=1, source_target_pairs={{0,32},{16,48},{32,0},{48,16},{64,96},{80,112},{96,64},{112,80},{1... | collective-permute-start | bytes 2162696 | tf_op jit(solution)/shard_map/ppermute | solution.py:108
  80.5 17.5 %collective-permute-start.9 = (bf16[3,2816]{1,0:T(4,128)(2,1)S(1)}, bf16[3,2816]{1,0:T(4,128)(2,1)S(1)}, u32[]{:S(2)}, u32[]{:S(2)}) collective-permute-start(bf16[3,2816]{1,0:T(4,128)(2,1)S(1)} %slice_bitcast_fusion.2), channel_id=1, source_target_pairs={{0,1},{1,2},{2,3},{3,4},{4,5},{5,6},{6,7},{7,8},{8,9},{9,10},{10,1... | collective-permute-start | bytes 50696 | tf_op jit(solution)/shard_map/ppermute | solution.py:13
  91.6 6.4 %copy-start.18 = (bf16[1,128,2816]{2,1,0:T(8,128)(2,1)S(1)}, bf16[1,128,2816]{2,1,0:T(8,128)(2,1)}, u32[]{:S(2)}) copy-start(bf16[1,128,2816]{2,1,0:T(8,128)(2,1)} %param.9) | copy-start | bytes 2162692
  92.9 10.1 %collective-permute-start.8 = (bf16[2,2,2,2,11,16,256]{6,5,4,2,1,0,3:T(8,128)(2,1)}, bf16[2,2,2,2,11,16,256]{6,5,4,2,1,0,3:T(8,128)(2,1)}, u32[]{:S(2)}, u32[]{:S(2)}) collective-permute-start(bf16[2,2,2,2,11,16,256]{6,5,4,2,1,0,3:T(8,128)(2,1)} %get-tuple-element.30), channel_id=1, source_target_pairs={{0,16},{16,0},{32,48},{48,32},{64,80},{80,64},{96,112},{112,96},{1... | collective-permute-start | bytes 4325384 | tf_op jit(solution)/shard_map/ppermute | solution.py:108
  106.4 1.1 copy-start.8
  106.6 2.7 copy-start.2
  106.6 5.6 %copy-start = (bf16[11,32,8,256]{3,2,0,1:T(8,128)(2,1)}, bf16[11,32,8,256]{3,2,0,1:T(8,128)(2,1)S(1)}, u32[]{:S(2)}) copy-start(bf16[11,32,8,256]{3,2,0,1:T(8,128)(2,1)S(1)} %get-tuple-element.20) | copy-start | bytes 4325380
  115.0 3.1 %copy-start.4 = (f32[128,2816]{1,0:T(8,128)S(1)}, f32[128,2816]{1,0:T(8,128)}, u32[]{:S(2)}) copy-start(f32[128,2816]{1,0:T(8,128)} %copy.124) | copy-start | bytes 4325380
  118.1 1.4 copy-start.5
  118.1 1.5 copy-start.15
  119.4 3.0 %copy-start.12 = (f32[128,2816]{1,0:T(8,128)}, f32[128,2816]{1,0:T(8,128)S(1)}, u32[]{:S(2)}) copy-start(f32[128,2816]{1,0:T(8,128)S(1)} %get-tuple-element.77) | copy-start | bytes 4325380
  119.4 5.3 %copy-start.17 = (f32[128,2816]{1,0:T(8,128)}, f32[128,2816]{1,0:T(8,128)S(1)}, u32[]{:S(2)}) copy-start(f32[128,2816]{1,0:T(8,128)S(1)} %get-tuple-element.76) | copy-start | bytes 4325380
  119.7 2.8 copy-start.19
  122.4 1.2 copy-start.16
  123.6 1.1 copy-start.9
  124.8 10.1 %collective-permute-start.10 = (f32[3,2816]{1,0:T(4,128)S(1)}, f32[3,2816]{1,0:T(4,128)S(1)}, u32[]{:S(2)}, u32[]{:S(2)}) collective-permute-start(f32[3,2816]{1,0:T(4,128)S(1)} %pad_maximum_fusion.9), channel_id=1, source_target_pairs={{0,1},{1,0},{2,3},{3,2},{4,5},{5,4},{6,7},{7,6},{8,9},{9,8},{10,11... | collective-permute-start | bytes 101384 | tf_op jit(solution)/shard_map/ppermute | solution.py:108
  136.0 14.7 %collective-permute-start.11 = (f32[3,2816]{1,0:T(4,128)S(1)}, f32[3,2816]{1,0:T(4,128)S(1)}, u32[]{:S(2)}, u32[]{:S(2)}) collective-permute-start(f32[3,2816]{1,0:T(4,128)S(1)} %pad_maximum_fusion.10), channel_id=1, source_target_pairs={{0,2},{1,3},{2,0},{3,1},{4,6},{5,7},{6,4},{7,5},{8,10},{9,11},{10,... | collective-permute-start | bytes 101384 | tf_op jit(solution)/shard_map/ppermute | solution.py:108
  150.8 5.9 %collective-permute-start.12 = (f32[3,2816]{1,0:T(4,128)S(1)}, f32[3,2816]{1,0:T(4,128)S(1)}, u32[]{:S(2)}, u32[]{:S(2)}) collective-permute-start(f32[3,2816]{1,0:T(4,128)S(1)} %pad_maximum_fusion.11), channel_id=1, source_target_pairs={{0,4},{1,5},{2,6},{3,7},{4,0},{5,1},{6,2},{7,3},{8,12},{9,13},{10,... | collective-permute-start | bytes 101384 | tf_op jit(solution)/shard_map/ppermute | solution.py:108
  156.8 7.4 %collective-permute-start.13 = (f32[3,2816]{1,0:T(4,128)S(1)}, f32[3,2816]{1,0:T(4,128)S(1)}, u32[]{:S(2)}, u32[]{:S(2)}) collective-permute-start(f32[3,2816]{1,0:T(4,128)S(1)} %pad_maximum_fusion.12), channel_id=1, source_target_pairs={{0,8},{1,9},{2,10},{3,11},{4,12},{5,13},{6,14},{7,15},{8,0},{9,1},... | collective-permute-start | bytes 101384 | tf_op jit(solution)/shard_map/ppermute | solution.py:108
  164.4 2.2 copy-start.6
  164.4 2.7 copy-start.10
  164.4 3.1 %copy-start.13 = (f32[128,2816]{1,0:T(8,128)S(1)}, f32[128,2816]{1,0:T(8,128)}, u32[]{:S(2)}) copy-start(f32[128,2816]{1,0:T(8,128)} %copy-done.12) | copy-start | bytes 4325380
  187.2 5.7 %collective-permute-start.15 = (f32[16,8,3168]{2,1,0:T(8,128)}, f32[16,8,3168]{2,1,0:T(8,128)}, u32[]{:S(2)}, u32[]{:S(2)}) collective-permute-start(f32[16,8,3168]{2,1,0:T(8,128)} %dynamic-slice_bitcast_fusion), channel_id=1, source_target_pairs={{0,16},{16,0},{32,48},{48,32},{64,80},{80,64},{96,112},{112,96},{1... | collective-permute-start | bytes 4866056 | tf_op jit(solution)/shard_map/ppermute | solution.py:108
  194.6 12.6 %copy-start.3 = (bf16[11,32,8,256]{3,2,0,1:T(8,128)(2,1)S(1)}, bf16[11,32,8,256]{3,2,0,1:T(8,128)(2,1)}, u32[]{:S(2)}) copy-start(bf16[11,32,8,256]{3,2,0,1:T(8,128)(2,1)} %copy-done.2) | copy-start | bytes 4325380
  195.6 14.5 %collective-permute-start.16 = (f32[4,8,3168]{2,1,0:T(8,128)}, f32[4,8,3168]{2,1,0:T(8,128)}, u32[]{:S(2)}, u32[]{:S(2)}) collective-permute-start(f32[4,8,3168]{2,1,0:T(8,128)} %get-tuple-element.23), channel_id=1, source_target_pairs={{0,32},{16,48},{32,0},{48,16},{64,96},{80,112},{96,64},{112,80},{1... | collective-permute-start | bytes 1216520 | tf_op jit(solution)/shard_map/ppermute | solution.py:108
  197.5 22.5 %collective-permute-start.17 = (f32[4,8,3168]{2,1,0:T(8,128)}, f32[4,8,3168]{2,1,0:T(8,128)}, u32[]{:S(2)}, u32[]{:S(2)}) collective-permute-start(f32[4,8,3168]{2,1,0:T(8,128)} %get-tuple-element.25), channel_id=1, source_target_pairs={{0,128},{16,144},{32,160},{48,176},{64,192},{80,208},{96,224},{112... | collective-permute-start | bytes 1216520 | tf_op jit(solution)/shard_map/ppermute | solution.py:108
  201.0 19.0 %collective-permute-start.18 = (f32[4,8,3168]{2,1,0:T(8,128)S(1)}, f32[4,8,3168]{2,1,0:T(8,128)}, u32[]{:S(2)}, u32[]{:S(2)}) collective-permute-start(f32[4,8,3168]{2,1,0:T(8,128)S(1)} %get-tuple-element.24), channel_id=1, source_target_pairs={{0,160},{16,176},{32,128},{48,144},{64,224},{80,240},{96,192},{112... | collective-permute-start | bytes 1216520 | tf_op jit(solution)/shard_map/ppermute | solution.py:108
  210.0 23.8 %copy-start.1 = (bf16[11,32,8,256]{3,2,0,1:T(8,128)(2,1)S(1)}, bf16[11,32,8,256]{3,2,0,1:T(8,128)(2,1)}, u32[]{:S(2)}) copy-start(bf16[11,32,8,256]{3,2,0,1:T(8,128)(2,1)} %copy-done) | copy-start | bytes 4325380
  210.0 23.8 %copy-start.14 = (bf16[128,2816]{0,1:T(8,128)(2,1)S(1)}, bf16[128,2816]{0,1:T(8,128)(2,1)}, u32[]{:S(2)}) copy-start(bf16[128,2816]{0,1:T(8,128)(2,1)} %copy.132) | copy-start | bytes 2162692
  222.1 16.1 %collective-permute-start.19 = (f32[1,8,3168]{2,1,0:T(8,128)}, f32[1,8,3168]{2,1,0:T(8,128)}, u32[]{:S(2)}, u32[]{:S(2)}) collective-permute-start(f32[1,8,3168]{2,1,0:T(8,128)} %get-tuple-element.40), channel_id=1, source_target_pairs={{0,64},{16,80},{32,96},{48,112},{64,0},{80,16},{96,32},{112,48},{1... | collective-permute-start | bytes 304136 | tf_op jit(solution)/shard_map/ppermute | solution.py:108
  226.0 12.2 %collective-permute-start.20 = (f32[1,8,3168]{2,1,0:T(8,128)}, f32[1,8,3168]{2,1,0:T(8,128)}, u32[]{:S(2)}, u32[]{:S(2)}) collective-permute-start(f32[1,8,3168]{2,1,0:T(8,128)} %get-tuple-element.42), channel_id=1, source_target_pairs={{0,256},{16,272},{32,288},{48,304},{64,320},{80,336},{96,352},{112... | collective-permute-start | bytes 304136 | tf_op jit(solution)/shard_map/ppermute | solution.py:108
  231.1 10.0 %collective-permute-start.21 = (f32[1,8,3168]{2,1,0:T(8,128)S(1)}, f32[1,8,3168]{2,1,0:T(8,128)}, u32[]{:S(2)}, u32[]{:S(2)}) collective-permute-start(f32[1,8,3168]{2,1,0:T(8,128)S(1)} %get-tuple-element.41), channel_id=1, source_target_pairs={{0,320},{16,336},{32,352},{48,368},{64,256},{80,272},{96,288},{112... | collective-permute-start | bytes 304136 | tf_op jit(solution)/shard_map/ppermute | solution.py:108
  233.7 1.4 copy-start.11
  238.2 23.7 %copy-start.7 = (f32[128,2816]{1,0:T(8,128)S(1)}, f32[128,2816]{1,0:T(8,128)}, u32[]{:S(2)}) copy-start(f32[128,2816]{1,0:T(8,128)} %copy.128) | copy-start | bytes 4325380
  242.5 30.2 %collective-permute-start.22 = (f32[4,8,528]{2,1,0:T(8,128)S(1)}, f32[4,8,528]{2,1,0:T(8,128)S(1)}, u32[]{:S(2)}, u32[]{:S(2)}) collective-permute-start(f32[4,8,528]{2,1,0:T(8,128)S(1)} %get-tuple-element.45), channel_id=1, source_target_pairs={{0,1},{1,0},{2,3},{3,2},{4,5},{5,4},{6,7},{7,6},{8,9},{9,8},{10,11... | collective-permute-start | bytes 202760 | tf_op jit(solution)/shard_map/ppermute | solution.py:108
  250.6 22.2 %collective-permute-start.23 = (f32[4,8,528]{2,1,0:T(8,128)S(1)}, f32[4,8,528]{2,1,0:T(8,128)S(1)}, u32[]{:S(2)}, u32[]{:S(2)}) collective-permute-start(f32[4,8,528]{2,1,0:T(8,128)S(1)} %get-tuple-element.47), channel_id=1, source_target_pairs={{0,2},{1,3},{2,0},{3,1},{4,6},{5,7},{6,4},{7,5},{8,10},{9,11},{10,... | collective-permute-start | bytes 202760 | tf_op jit(solution)/shard_map/ppermute | solution.py:108
  260.0 12.8 %collective-permute-start.24 = (f32[4,8,528]{2,1,0:T(8,128)S(1)}, f32[4,8,528]{2,1,0:T(8,128)S(1)}, u32[]{:S(2)}, u32[]{:S(2)}) collective-permute-start(f32[4,8,528]{2,1,0:T(8,128)S(1)} %get-tuple-element.46), channel_id=1, source_target_pairs={{0,3},{1,2},{2,1},{3,0},{4,7},{5,6},{6,5},{7,4},{8,11},{9,10},{10,... | collective-permute-start | bytes 202760 | tf_op jit(solution)/shard_map/ppermute | solution.py:108
  264.5 18.8 %collective-permute-start.14 = (f32[3,2816]{1,0:T(4,128)S(1)}, f32[3,2816]{1,0:T(4,128)S(1)}, u32[]{:S(2)}, u32[]{:S(2)}) collective-permute-start(f32[3,2816]{1,0:T(4,128)S(1)} %slice.215), channel_id=1, source_target_pairs={{1,0},{2,1},{3,2},{4,3},{5,4},{6,5},{7,6},{8,7},{9,8},{10,9},{11,1... | collective-permute-start | bytes 101384 | tf_op jit(solution)/shard_map/ppermute | solution.py:13
  272.8 12.0 %collective-permute-start.25 = (f32[1,8,528]{2,1,0:T(8,128)S(1)}, f32[1,8,528]{2,1,0:T(8,128)S(1)}, u32[]{:S(2)}, u32[]{:S(2)}) collective-permute-start(f32[1,8,528]{2,1,0:T(8,128)S(1)} %get-tuple-element.59), channel_id=1, source_target_pairs={{0,4},{1,5},{2,6},{3,7},{4,0},{5,1},{6,2},{7,3},{8,12},{9,13},{10,... | collective-permute-start | bytes 50696 | tf_op jit(solution)/shard_map/ppermute | solution.py:108
  275.3 9.5 %collective-permute-start.26 = (f32[1,8,528]{2,1,0:T(8,128)S(1)}, f32[1,8,528]{2,1,0:T(8,128)S(1)}, u32[]{:S(2)}, u32[]{:S(2)}) collective-permute-start(f32[1,8,528]{2,1,0:T(8,128)S(1)} %get-tuple-element.61), channel_id=1, source_target_pairs={{0,8},{1,9},{2,10},{3,11},{4,12},{5,13},{6,14},{7,15},{8,0},{9,1},... | collective-permute-start | bytes 50696 | tf_op jit(solution)/shard_map/ppermute | solution.py:108
  277.8 7.2 %collective-permute-start.27 = (f32[1,8,528]{2,1,0:T(8,128)S(1)}, f32[1,8,528]{2,1,0:T(8,128)S(1)}, u32[]{:S(2)}, u32[]{:S(2)}) collective-permute-start(f32[1,8,528]{2,1,0:T(8,128)S(1)} %get-tuple-element.60), channel_id=1, source_target_pairs={{0,12},{1,13},{2,14},{3,15},{4,8},{5,9},{6,10},{7,11},{8,4},{9,5},... | collective-permute-start | bytes 50696 | tf_op jit(solution)/shard_map/ppermute | solution.py:108

commit v4 on v3

--- a/solution.py
+++ b/solution.py
@@ -90,6 +90,12 @@
     return single[::-1]
 
 
+def high_first(length):
+    single = bit_steps(length)
+    half = len(single) // 2
+    return single[half:] + single[:half]
+
+
 def bit_steps(length):
     return [[stride] for step in digit_steps(length) for stride in step]
 
@@ -204,7 +210,7 @@
     width = ctx_size * cols
     head_width = dp_size * rows
     joined = jnp.concatenate([weight_a, weight_x, packed], 0)
-    by_ctx = gathered_by_doubling(joined, "ctx", bit_steps(ctx_size))
+    by_ctx = gathered_by_doubling(joined, "ctx", high_first(ctx_size))
     by_ctx = by_ctx.transpose(1, 0, 2).reshape(joined.shape[0], width)
     params = by_ctx[2 * rows :]
     heads = by_ctx[: 2 * rows].reshape(2 * rows, -1, head_width).transpose(1, 0, 2)
@@ -271,7 +277,7 @@
     by_row = local_wgrad.reshape(dp_size, rows, width)
     row_sum, rgrad = summed_apart(by_row, local_rgrad, "dp", spread_steps(dp_size, 1))
     by_channel = row_sum.reshape(rows, ctx_size, cols).transpose(1, 0, 2)
-    wgrad, rgrad = summed_apart(by_channel, rgrad, "ctx", digit_steps(ctx_size))
+    wgrad, rgrad = summed_apart(by_channel, rgrad, "ctx", digit_steps(ctx_size)[::-1])
     return (grad_in.astype(jnp.bfloat16)[None], wgrad, rgrad)
 
 

time: 290 us -> 291 us (level)
  starting transfers between devices: 136 us -> 141 us
    ppermute x26, starting transfers between devices: 121 us -> 125 us  [exchanged(): return lax.ppermute(array, axis, [(i, i ^ mask) for i in range(length)])]
    ppermute x26, waiting for transfers between devices: 64.1 us -> 60.9 us  [exchanged(): return lax.ppermute(array, axis, [(i, i ^ mask) for i in range(length)])]
where the time goes in v4:
time: 291 us; the launch traced here: 289 us
  starting transfers between devices  141 us (48%)
  waiting for transfers between devices  65.1 us (22%)
  local copies, waits for them, and re-layouts  39.4 us (14%)
  other arithmetic  26.7 us (9%)
  matrix products  14.9 us (5%)
    ppermute x26, starting transfers between devices, exchanged(): return lax.ppermute(array, axis, [(i, i ^ mask) for i in range(length)])  125 us
    ppermute x26, waiting for transfers between devices, exchanged(): return lax.ppermute(array, axis, [(i, i ^ mask) for i in range(length)])  60.9 us
    ppermute x2, starting transfers between devices, passed_along(): return lax.ppermute(array, axis, pairs)  16.2 us
    reshape x2, local copies, waits for them, and re-layouts, mix_heads(): return result.reshape(tokens, head_count * head_width)  6.01 us
  transfers between devices with their start and end apart: 28, of which 18 were waited for; matrix products, arithmetic and copies ran while one was open for 7% of the time, Pallas kernels for 0%

profile of v4, /device:TPU:6, one launch (start us, length us, event | category | flops | bytes accessed | tf_op | source)
XLA Modules:
  0.0 289.1 jit_solution(2495539224707541510)
XLA Ops:
  5.3 2.7 collective-permute-start
  8.1 2.8 collective-permute-done
  11.0 7.2 %collective-permute-start.1 = (bf16[2,24,176]{2,1,0:T(8,128)(2,1)S(1)}, bf16[2,24,176]{2,1,0:T(8,128)(2,1)S(1)}, u32[]{:S(2)}, u32[]{:S(2)}) collective-permute-start(bf16[2,24,176]{2,1,0:T(8,128)(2,1)S(1)} %get-tuple-element.72), channel_id=1, source_target_pairs={{0,8},{1,9},{2,10},{3,11},{4,12},{5,13},{6,14},{7,15},{8,0},{9,1},... | collective-permute-start | bytes 50696 | tf_op jit(solution)/shard_map/ppermute | solution.py:114
  20.0 7.3 %collective-permute-start.2 = (bf16[2,2,24,176]{3,2,0,1:T(8,128)(2,1)S(1)}, bf16[2,2,24,176]{3,2,0,1:T(8,128)(2,1)S(1)}, u32[]{:S(2)}, u32[]{:S(2)}) collective-permute-start(bf16[2,2,24,176]{3,2,0,1:T(8,128)(2,1)S(1)} %get-tuple-element.68), channel_id=1, source_target_pairs={{0,1},{1,0},{2,3},{3,2},{4,5},{5,4},{6,7},{7,6},{8,9},{9,8},{10,11... | collective-permute-start | bytes 101384 | tf_op jit(solution)/shard_map/ppermute | solution.py:114
  27.4 3.6 %collective-permute-done.2 = bf16[2,2,24,176]{3,2,0,1:T(8,128)(2,1)S(1)} collective-permute-done((bf16[2,2,24,176]{3,2,0,1:T(8,128)(2,1)S(1)}, bf16[2,2,24,176]{3,2,0,1:T(8,128)(2,1)S(1)}, u32[]{:S(2)}, u32[]{:S(2)}) %collective-permute-start.2) | collective-permute-done | bytes 33824 | tf_op jit(solution)/shard_map/ppermute | solution.py:114
  31.1 12.9 %collective-permute-start.3 = (bf16[2,2,2,24,176]{4,3,2,0,1:T(8,128)(2,1)S(1)}, bf16[2,2,2,24,176]{4,3,2,0,1:T(8,128)(2,1)S(1)}, u32[]{:S(2)}, u32[]{:S(2)}) collective-permute-start(bf16[2,2,2,24,176]{4,3,2,0,1:T(8,128)(2,1)S(1)} %get-tuple-element.55), channel_id=1, source_target_pairs={{0,2},{1,3},{2,0},{3,1},{4,6},{5,7},{6,4},{7,5},{8,10},{9,11},{10,... | collective-permute-start | bytes 202760 | tf_op jit(solution)/shard_map/ppermute | solution.py:114
  44.0 2.8 collective-permute-done.3
  47.3 5.1 %collective-permute-start.4 = (bf16[11,16,256]{2,0,1:T(8,128)(2,1)S(1)}, bf16[11,16,256]{2,0,1:T(8,128)(2,1)S(1)}, u32[]{:S(2)}, u32[]{:S(2)}) collective-permute-start(bf16[11,16,256]{2,0,1:T(8,128)(2,1)S(1)} %bitcast.187), channel_id=1, source_target_pairs={{0,256},{16,272},{32,288},{48,304},{64,320},{80,336},{96,352},{112... | collective-permute-start | bytes 270344 | tf_op jit(solution)/shard_map/ppermute | solution.py:114
  52.5 3.2 %collective-permute-done.4 = bf16[11,16,256]{2,0,1:T(8,128)(2,1)S(1)} collective-permute-done((bf16[11,16,256]{2,0,1:T(8,128)(2,1)S(1)}, bf16[11,16,256]{2,0,1:T(8,128)(2,1)S(1)}, u32[]{:S(2)}, u32[]{:S(2)}) %collective-permute-start.4) | collective-permute-done | bytes 90144 | tf_op jit(solution)/shard_map/ppermute | solution.py:114
  55.9 4.6 %collective-permute-start.5 = (bf16[2,11,16,256]{3,1,2,0:T(8,128)(2,1)S(1)}, bf16[2,11,16,256]{3,1,2,0:T(8,128)(2,1)S(1)}, u32[]{:S(2)}, u32[]{:S(2)}) collective-permute-start(bf16[2,11,16,256]{3,1,2,0:T(8,128)(2,1)S(1)} %get-tuple-element.48), channel_id=1, source_target_pairs={{0,64},{16,80},{32,96},{48,112},{64,0},{80,16},{96,32},{112,48},{1... | collective-permute-start | bytes 540680 | tf_op jit(solution)/shard_map/ppermute | solution.py:114
  60.5 4.5 %collective-permute-done.5 = bf16[2,11,16,256]{3,1,2,0:T(8,128)(2,1)S(1)} collective-permute-done((bf16[2,11,16,256]{3,1,2,0:T(8,128)(2,1)S(1)}, bf16[2,11,16,256]{3,1,2,0:T(8,128)(2,1)S(1)}, u32[]{:S(2)}, u32[]{:S(2)}) %collective-permute-start.5) | collective-permute-done | bytes 180256 | tf_op jit(solution)/shard_map/ppermute | solution.py:114
  65.5 3.5 %collective-permute-start.6 = (bf16[2,2,11,16,256]{4,3,2,0,1:T(8,128)(2,1)S(1)}, bf16[2,2,11,16,256]{4,3,2,0,1:T(8,128)(2,1)S(1)}, u32[]{:S(2)}, u32[]{:S(2)}) collective-permute-start(bf16[2,2,11,16,256]{4,3,2,0,1:T(8,128)(2,1)S(1)} %get-tuple-element.43), channel_id=1, source_target_pairs={{0,128},{16,144},{32,160},{48,176},{64,192},{80,208},{96,224},{112... | collective-permute-start | bytes 1081352 | tf_op jit(solution)/shard_map/ppermute | solution.py:114
  69.0 5.8 %collective-permute-done.6 = bf16[2,2,11,16,256]{4,3,2,0,1:T(8,128)(2,1)S(1)} collective-permute-done((bf16[2,2,11,16,256]{4,3,2,0,1:T(8,128)(2,1)S(1)}, bf16[2,2,11,16,256]{4,3,2,0,1:T(8,128)(2,1)S(1)}, u32[]{:S(2)}, u32[]{:S(2)}) %collective-permute-start.6) | collective-permute-done | bytes 360480 | tf_op jit(solution)/shard_map/ppermute | solution.py:114
  75.2 5.8 %collective-permute-start.7 = (bf16[2,2,2,11,16,256]{5,4,3,1,0,2:T(8,128)(2,1)S(1)}, bf16[2,2,2,11,16,256]{5,4,3,1,0,2:T(8,128)(2,1)S(1)}, u32[]{:S(2)}, u32[]{:S(2)}) collective-permute-start(bf16[2,2,2,11,16,256]{5,4,3,1,0,2:T(8,128)(2,1)S(1)} %get-tuple-element.34), channel_id=1, source_target_pairs={{0,32},{16,48},{32,0},{48,16},{64,96},{80,112},{96,64},{112,80},{1... | collective-permute-start | bytes 2162696 | tf_op jit(solution)/shard_map/ppermute | solution.py:114
  81.9 7.1 %collective-permute-start.9 = (bf16[3,2816]{1,0:T(4,128)(2,1)S(1)}, bf16[3,2816]{1,0:T(4,128)(2,1)S(1)}, u32[]{:S(2)}, u32[]{:S(2)}) collective-permute-start(bf16[3,2816]{1,0:T(4,128)(2,1)S(1)} %slice_bitcast_fusion.2), channel_id=1, source_target_pairs={{0,1},{1,2},{2,3},{3,4},{4,5},{5,6},{6,7},{7,8},{8,9},{9,10},{10,1... | collective-permute-start | bytes 50696 | tf_op jit(solution)/shard_map/ppermute | solution.py:13
  94.4 4.2 %collective-permute-done.9 = bf16[3,2816]{1,0:T(4,128)(2,1)S(1)} collective-permute-done((bf16[3,2816]{1,0:T(4,128)(2,1)S(1)}, bf16[3,2816]{1,0:T(4,128)(2,1)S(1)}, u32[]{:S(2)}, u32[]{:S(2)}) %collective-permute-start.9) | collective-permute-done | bytes 16928 | tf_op jit(solution)/shard_map/ppermute | solution.py:13
  109.8 2.9 %copy.59 = f32[128,2816]{1,0:T(8,128)} copy(f32[128,2816]{0,1:T(8,128)} %bitcast.171) | data formatting | bytes 2883584 | tf_op jit(solution)/shard_map/reshape | solution.py:21
  112.7 2.9 fusion.28
  115.6 3.1 %copy.63 = f32[128,2816]{1,0:T(8,128)} copy(f32[128,2816]{0,1:T(8,128)} %bitcast.172) | data formatting | bytes 2883584 | tf_op jit(solution)/shard_map/reshape | solution.py:21
  120.3 2.8 convolution_multiply_fusion
  125.4 4.9 %collective-permute-start.10 = (f32[3,2816]{1,0:T(4,128)S(1)}, f32[3,2816]{1,0:T(4,128)S(1)}, u32[]{:S(2)}, u32[]{:S(2)}) collective-permute-start(f32[3,2816]{1,0:T(4,128)S(1)} %pad_maximum_fusion.10), channel_id=1, source_target_pairs={{0,1},{1,0},{2,3},{3,2},{4,5},{5,4},{6,7},{7,6},{8,9},{9,8},{10,11... | collective-permute-start | bytes 101384 | tf_op jit(solution)/shard_map/ppermute | solution.py:114
  130.3 6.3 %collective-permute-done.10 = f32[3,2816]{1,0:T(4,128)S(1)} collective-permute-done((f32[3,2816]{1,0:T(4,128)S(1)}, f32[3,2816]{1,0:T(4,128)S(1)}, u32[]{:S(2)}, u32[]{:S(2)}) %collective-permute-start.10) | collective-permute-done | bytes 33824 | tf_op jit(solution)/shard_map/ppermute | solution.py:114
  137.7 11.2 %collective-permute-start.11 = (f32[3,2816]{1,0:T(4,128)S(1)}, f32[3,2816]{1,0:T(4,128)S(1)}, u32[]{:S(2)}, u32[]{:S(2)}) collective-permute-start(f32[3,2816]{1,0:T(4,128)S(1)} %pad_maximum_fusion.11), channel_id=1, source_target_pairs={{0,2},{1,3},{2,0},{3,1},{4,6},{5,7},{6,4},{7,5},{8,10},{9,11},{10,... | collective-permute-start | bytes 101384 | tf_op jit(solution)/shard_map/ppermute | solution.py:114
  148.9 3.5 %collective-permute-done.11 = f32[3,2816]{1,0:T(4,128)S(1)} collective-permute-done((f32[3,2816]{1,0:T(4,128)S(1)}, f32[3,2816]{1,0:T(4,128)S(1)}, u32[]{:S(2)}, u32[]{:S(2)}) %collective-permute-start.11) | collective-permute-done | bytes 33824 | tf_op jit(solution)/shard_map/ppermute | solution.py:114
  152.5 2.5 collective-permute-start.12
  155.0 3.4 %collective-permute-done.12 = f32[3,2816]{1,0:T(4,128)S(1)} collective-permute-done((f32[3,2816]{1,0:T(4,128)S(1)}, f32[3,2816]{1,0:T(4,128)S(1)}, u32[]{:S(2)}, u32[]{:S(2)}) %collective-permute-start.12) | collective-permute-done | bytes 33824 | tf_op jit(solution)/shard_map/ppermute | solution.py:114
  158.5 4.9 %collective-permute-start.13 = (f32[3,2816]{1,0:T(4,128)S(1)}, f32[3,2816]{1,0:T(4,128)S(1)}, u32[]{:S(2)}, u32[]{:S(2)}) collective-permute-start(f32[3,2816]{1,0:T(4,128)S(1)} %pad_maximum_fusion.13), channel_id=1, source_target_pairs={{0,8},{1,9},{2,10},{3,11},{4,12},{5,13},{6,14},{7,15},{8,0},{9,1},... | collective-permute-start | bytes 101384 | tf_op jit(solution)/shard_map/ppermute | solution.py:114
  163.5 2.5 collective-permute-done.13
  169.3 4.6 %multiply_reduce_fusion = (f32[2816]{0:T(1024)S(1)}, f32[128,2816]{1,0:T(8,128)S(1)}, bf16[128,2816]{1,0:T(8,128)(2,1)}, f32[128,2816]{1,0:T(8,128)}) fusion(f32[128,2816]{1,0:T(8,128)S(1)} %copy-done.4, f32[2816]{0:T(1024)S(1)} %add.402, f32[128,2816]{1,0:T(8,128)S(1)} %copy-done.6, f32[2816]{0:T(1024)S(1)} %add.406, f32[2816]{0:T(1024)S(1)} %mul.339, ...), kind=kLoop, calls=%fused_computation.69 | loop fusion | flops 17659136 | bytes 16704512 | tf_op jit(solution)/shard_map/reduce_sum | solution.py:276
  177.3 3.4 %copy.71 = f32[256,11,256]{2,1,0:T(8,128)} copy(f32[256,11,256]{0,2,1:T(8,128)S(1)} %convolution_bitcast_fusion) | data formatting | bytes 5767168 | tf_op jit(solution)/shard_map/thk,thj->khj/transpose | solution.py:37
  180.7 4.7 %concatenate.25 = f32[2,2,2,2,2,8,2816]{6,5,4,3,2,1,0:T(8,128)} reshape(f32[256,11,256]{2,1,0:T(8,128)} %copy.71) | data formatting | bytes 5767168 | tf_op jit(solution)/shard_map/concatenate | solution.py:191
  190.9 3.8 %collective-permute-done.15 = f32[16,8,3168]{2,1,0:T(8,128)} collective-permute-done((f32[16,8,3168]{2,1,0:T(8,128)}, f32[16,8,3168]{2,1,0:T(8,128)}, u32[]{:S(2)}, u32[]{:S(2)}) %collective-permute-start.15) | collective-permute-done | bytes 1622048 | tf_op jit(solution)/shard_map/ppermute | solution.py:114
  199.3 3.5 %collective-permute-start.17 = (f32[4,8,3168]{2,1,0:T(8,128)}, f32[4,8,3168]{2,1,0:T(8,128)}, u32[]{:S(2)}, u32[]{:S(2)}) collective-permute-start(f32[4,8,3168]{2,1,0:T(8,128)} %get-tuple-element.25), channel_id=1, source_target_pairs={{0,128},{16,144},{32,160},{48,176},{64,192},{80,208},{96,224},{112... | collective-permute-start | bytes 1216520 | tf_op jit(solution)/shard_map/ppermute | solution.py:114
  202.8 3.8 %collective-permute-start.18 = (f32[4,8,3168]{2,1,0:T(8,128)S(1)}, f32[4,8,3168]{2,1,0:T(8,128)}, u32[]{:S(2)}, u32[]{:S(2)}) collective-permute-start(f32[4,8,3168]{2,1,0:T(8,128)S(1)} %get-tuple-element.24), channel_id=1, source_target_pairs={{0,160},{16,176},{32,128},{48,144},{64,224},{80,240},{96,192},{112... | collective-permute-start | bytes 1216520 | tf_op jit(solution)/shard_map/ppermute | solution.py:114
  208.9 2.8 fusion.30
  211.9 9.9 %collective-permute-done.17 = f32[4,8,3168]{2,1,0:T(8,128)} collective-permute-done((f32[4,8,3168]{2,1,0:T(8,128)}, f32[4,8,3168]{2,1,0:T(8,128)}, u32[]{:S(2)}, u32[]{:S(2)}) %collective-permute-start.17) | collective-permute-done | bytes 405536 | tf_op jit(solution)/shard_map/ppermute | solution.py:114
  223.8 2.8 collective-permute-start.19
  226.6 5.1 %collective-permute-start.20 = (f32[1,8,3168]{2,1,0:T(8,128)}, f32[1,8,3168]{2,1,0:T(8,128)}, u32[]{:S(2)}, u32[]{:S(2)}) collective-permute-start(f32[1,8,3168]{2,1,0:T(8,128)} %get-tuple-element.42), channel_id=1, source_target_pairs={{0,256},{16,272},{32,288},{48,304},{64,320},{80,336},{96,352},{112... | collective-permute-start | bytes 304136 | tf_op jit(solution)/shard_map/ppermute | solution.py:114
  231.7 3.8 %collective-permute-start.21 = (f32[1,8,3168]{2,1,0:T(8,128)S(1)}, f32[1,8,3168]{2,1,0:T(8,128)}, u32[]{:S(2)}, u32[]{:S(2)}) collective-permute-start(f32[1,8,3168]{2,1,0:T(8,128)S(1)} %get-tuple-element.41), channel_id=1, source_target_pairs={{0,320},{16,336},{32,352},{48,368},{64,256},{80,272},{96,288},{112... | collective-permute-start | bytes 304136 | tf_op jit(solution)/shard_map/ppermute | solution.py:114
  243.1 2.9 %collective-permute-start.22 = (f32[4,8,528]{2,1,0:T(8,128)S(1)}, f32[4,8,528]{2,1,0:T(8,128)S(1)}, u32[]{:S(2)}, u32[]{:S(2)}) collective-permute-start(f32[4,8,528]{2,1,0:T(8,128)S(1)} %get-tuple-element.45), channel_id=1, source_target_pairs={{0,4},{1,5},{2,6},{3,7},{4,0},{5,1},{6,2},{7,3},{8,12},{9,13},{10,... | collective-permute-start | bytes 202760 | tf_op jit(solution)/shard_map/ppermute | solution.py:114
  246.0 3.8 %collective-permute-start.23 = (f32[4,8,528]{2,1,0:T(8,128)S(1)}, f32[4,8,528]{2,1,0:T(8,128)S(1)}, u32[]{:S(2)}, u32[]{:S(2)}) collective-permute-start(f32[4,8,528]{2,1,0:T(8,128)S(1)} %get-tuple-element.47), channel_id=1, source_target_pairs={{0,8},{1,9},{2,10},{3,11},{4,12},{5,13},{6,14},{7,15},{8,0},{9,1},... | collective-permute-start | bytes 202760 | tf_op jit(solution)/shard_map/ppermute | solution.py:114
  249.8 3.7 %collective-permute-start.24 = (f32[4,8,528]{2,1,0:T(8,128)S(1)}, f32[4,8,528]{2,1,0:T(8,128)S(1)}, u32[]{:S(2)}, u32[]{:S(2)}) collective-permute-start(f32[4,8,528]{2,1,0:T(8,128)S(1)} %get-tuple-element.46), channel_id=1, source_target_pairs={{0,12},{1,13},{2,14},{3,15},{4,8},{5,9},{6,10},{7,11},{8,4},{9,5},... | collective-permute-start | bytes 202760 | tf_op jit(solution)/shard_map/ppermute | solution.py:114
  253.5 2.6 add_add_fusion
  256.2 9.1 %collective-permute-start.14 = (f32[3,2816]{1,0:T(4,128)S(1)}, f32[3,2816]{1,0:T(4,128)S(1)}, u32[]{:S(2)}, u32[]{:S(2)}) collective-permute-start(f32[3,2816]{1,0:T(4,128)S(1)} %slice.215), channel_id=1, source_target_pairs={{1,0},{2,1},{3,2},{4,3},{5,4},{6,5},{7,6},{8,7},{9,8},{10,9},{11,1... | collective-permute-start | bytes 101384 | tf_op jit(solution)/shard_map/ppermute | solution.py:13
  265.4 2.9 %collective-permute-start.25 = (f32[1,8,528]{2,1,0:T(8,128)S(1)}, f32[1,8,528]{2,1,0:T(8,128)S(1)}, u32[]{:S(2)}, u32[]{:S(2)}) collective-permute-start(f32[1,8,528]{2,1,0:T(8,128)S(1)} %get-tuple-element.59), channel_id=1, source_target_pairs={{0,1},{1,0},{2,3},{3,2},{4,5},{5,4},{6,7},{7,6},{8,9},{9,8},{10,11... | collective-permute-start | bytes 50696 | tf_op jit(solution)/shard_map/ppermute | solution.py:114
  268.3 9.9 %collective-permute-start.26 = (f32[1,8,528]{2,1,0:T(8,128)S(1)}, f32[1,8,528]{2,1,0:T(8,128)S(1)}, u32[]{:S(2)}, u32[]{:S(2)}) collective-permute-start(f32[1,8,528]{2,1,0:T(8,128)S(1)} %get-tuple-element.61), channel_id=1, source_target_pairs={{0,2},{1,3},{2,0},{3,1},{4,6},{5,7},{6,4},{7,5},{8,10},{9,11},{10,... | collective-permute-start | bytes 50696 | tf_op jit(solution)/shard_map/ppermute | solution.py:114
  278.2 4.2 %collective-permute-start.27 = (f32[1,8,528]{2,1,0:T(8,128)S(1)}, f32[1,8,528]{2,1,0:T(8,128)S(1)}, u32[]{:S(2)}, u32[]{:S(2)}) collective-permute-start(f32[1,8,528]{2,1,0:T(8,128)S(1)} %get-tuple-element.60), channel_id=1, source_target_pairs={{0,3},{1,2},{2,1},{3,0},{4,7},{5,6},{6,5},{7,4},{8,11},{9,10},{10,... | collective-permute-start | bytes 50696 | tf_op jit(solution)/shard_map/ppermute | solution.py:114
  284.0 3.8 %collective-permute-done.27 = f32[1,8,528]{2,1,0:T(8,128)S(1)} collective-permute-done((f32[1,8,528]{2,1,0:T(8,128)S(1)}, f32[1,8,528]{2,1,0:T(8,128)S(1)}, u32[]{:S(2)}, u32[]{:S(2)}) %collective-permute-start.27) | collective-permute-done | bytes 16928 | tf_op jit(solution)/shard_map/ppermute | solution.py:114
  (153 shorter events, 62.0 us)
Async XLA Ops:
  5.3 5.6 %collective-permute-start = (bf16[24,176]{1,0:T(8,128)(2,1)S(1)}, bf16[24,176]{1,0:T(8,128)(2,1)S(1)}, u32[]{:S(2)}, u32[]{:S(2)}) collective-permute-start(bf16[24,176]{1,0:T(8,128)(2,1)S(1)} %concatenate.21), channel_id=1, source_target_pairs={{0,4},{1,5},{2,6},{3,7},{4,0},{5,1},{6,2},{7,3},{8,12},{9,13},{10,... | collective-permute-start | bytes 25352 | tf_op jit(solution)/shard_map/ppermute | solution.py:114
  11.0 9.0 %collective-permute-start.1 = (bf16[2,24,176]{2,1,0:T(8,128)(2,1)S(1)}, bf16[2,24,176]{2,1,0:T(8,128)(2,1)S(1)}, u32[]{:S(2)}, u32[]{:S(2)}) collective-permute-start(bf16[2,24,176]{2,1,0:T(8,128)(2,1)S(1)} %get-tuple-element.72), channel_id=1, source_target_pairs={{0,8},{1,9},{2,10},{3,11},{4,12},{5,13},{6,14},{7,15},{8,0},{9,1},... | collective-permute-start | bytes 50696 | tf_op jit(solution)/shard_map/ppermute | solution.py:114
  20.0 10.9 %collective-permute-start.2 = (bf16[2,2,24,176]{3,2,0,1:T(8,128)(2,1)S(1)}, bf16[2,2,24,176]{3,2,0,1:T(8,128)(2,1)S(1)}, u32[]{:S(2)}, u32[]{:S(2)}) collective-permute-start(bf16[2,2,24,176]{3,2,0,1:T(8,128)(2,1)S(1)} %get-tuple-element.68), channel_id=1, source_target_pairs={{0,1},{1,0},{2,3},{3,2},{4,5},{5,4},{6,7},{7,6},{8,9},{9,8},{10,11... | collective-permute-start | bytes 101384 | tf_op jit(solution)/shard_map/ppermute | solution.py:114
  31.1 15.8 %collective-permute-start.3 = (bf16[2,2,2,24,176]{4,3,2,0,1:T(8,128)(2,1)S(1)}, bf16[2,2,2,24,176]{4,3,2,0,1:T(8,128)(2,1)S(1)}, u32[]{:S(2)}, u32[]{:S(2)}) collective-permute-start(bf16[2,2,2,24,176]{4,3,2,0,1:T(8,128)(2,1)S(1)} %get-tuple-element.55), channel_id=1, source_target_pairs={{0,2},{1,3},{2,0},{3,1},{4,6},{5,7},{6,4},{7,5},{8,10},{9,11},{10,... | collective-permute-start | bytes 202760 | tf_op jit(solution)/shard_map/ppermute | solution.py:114
  47.3 8.4 %collective-permute-start.4 = (bf16[11,16,256]{2,0,1:T(8,128)(2,1)S(1)}, bf16[11,16,256]{2,0,1:T(8,128)(2,1)S(1)}, u32[]{:S(2)}, u32[]{:S(2)}) collective-permute-start(bf16[11,16,256]{2,0,1:T(8,128)(2,1)S(1)} %bitcast.187), channel_id=1, source_target_pairs={{0,256},{16,272},{32,288},{48,304},{64,320},{80,336},{96,352},{112... | collective-permute-start | bytes 270344 | tf_op jit(solution)/shard_map/ppermute | solution.py:114
  55.9 9.2 %collective-permute-start.5 = (bf16[2,11,16,256]{3,1,2,0:T(8,128)(2,1)S(1)}, bf16[2,11,16,256]{3,1,2,0:T(8,128)(2,1)S(1)}, u32[]{:S(2)}, u32[]{:S(2)}) collective-permute-start(bf16[2,11,16,256]{3,1,2,0:T(8,128)(2,1)S(1)} %get-tuple-element.48), channel_id=1, source_target_pairs={{0,64},{16,80},{32,96},{48,112},{64,0},{80,16},{96,32},{112,48},{1... | collective-permute-start | bytes 540680 | tf_op jit(solution)/shard_map/ppermute | solution.py:114
  65.5 9.3 %collective-permute-start.6 = (bf16[2,2,11,16,256]{4,3,2,0,1:T(8,128)(2,1)S(1)}, bf16[2,2,11,16,256]{4,3,2,0,1:T(8,128)(2,1)S(1)}, u32[]{:S(2)}, u32[]{:S(2)}) collective-permute-start(bf16[2,2,11,16,256]{4,3,2,0,1:T(8,128)(2,1)S(1)} %get-tuple-element.43), channel_id=1, source_target_pairs={{0,128},{16,144},{32,160},{48,176},{64,192},{80,208},{96,224},{112... | collective-permute-start | bytes 1081352 | tf_op jit(solution)/shard_map/ppermute | solution.py:114
  75.2 15.1 %collective-permute-start.7 = (bf16[2,2,2,11,16,256]{5,4,3,1,0,2:T(8,128)(2,1)S(1)}, bf16[2,2,2,11,16,256]{5,4,3,1,0,2:T(8,128)(2,1)S(1)}, u32[]{:S(2)}, u32[]{:S(2)}) collective-permute-start(bf16[2,2,2,11,16,256]{5,4,3,1,0,2:T(8,128)(2,1)S(1)} %get-tuple-element.34), channel_id=1, source_target_pairs={{0,32},{16,48},{32,0},{48,16},{64,96},{80,112},{96,64},{112,80},{1... | collective-permute-start | bytes 2162696 | tf_op jit(solution)/shard_map/ppermute | solution.py:114
  81.9 16.7 %collective-permute-start.9 = (bf16[3,2816]{1,0:T(4,128)(2,1)S(1)}, bf16[3,2816]{1,0:T(4,128)(2,1)S(1)}, u32[]{:S(2)}, u32[]{:S(2)}) collective-permute-start(bf16[3,2816]{1,0:T(4,128)(2,1)S(1)} %slice_bitcast_fusion.2), channel_id=1, source_target_pairs={{0,1},{1,2},{2,3},{3,4},{4,5},{5,6},{6,7},{7,8},{8,9},{9,10},{10,1... | collective-permute-start | bytes 50696 | tf_op jit(solution)/shard_map/ppermute | solution.py:13
  91.0 7.6 %copy-start.18 = (bf16[1,128,2816]{2,1,0:T(8,128)(2,1)S(1)}, bf16[1,128,2816]{2,1,0:T(8,128)(2,1)}, u32[]{:S(2)}) copy-start(bf16[1,128,2816]{2,1,0:T(8,128)(2,1)} %param.9) | copy-start | bytes 2162692
  92.3 11.3 %collective-permute-start.8 = (bf16[2,2,2,2,11,16,256]{6,5,4,2,1,0,3:T(8,128)(2,1)}, bf16[2,2,2,2,11,16,256]{6,5,4,2,1,0,3:T(8,128)(2,1)}, u32[]{:S(2)}, u32[]{:S(2)}) collective-permute-start(bf16[2,2,2,2,11,16,256]{6,5,4,2,1,0,3:T(8,128)(2,1)} %get-tuple-element.30), channel_id=1, source_target_pairs={{0,16},{16,0},{32,48},{48,32},{64,80},{80,64},{96,112},{112,96},{1... | collective-permute-start | bytes 4325384 | tf_op jit(solution)/shard_map/ppermute | solution.py:114
  106.9 1.1 copy-start.8
  107.2 2.7 copy-start.2
  107.2 5.6 %copy-start = (bf16[11,32,8,256]{3,2,0,1:T(8,128)(2,1)}, bf16[11,32,8,256]{3,2,0,1:T(8,128)(2,1)S(1)}, u32[]{:S(2)}) copy-start(bf16[11,32,8,256]{3,2,0,1:T(8,128)(2,1)S(1)} %get-tuple-element.20) | copy-start | bytes 4325380
  115.6 3.1 %copy-start.4 = (f32[128,2816]{1,0:T(8,128)S(1)}, f32[128,2816]{1,0:T(8,128)}, u32[]{:S(2)}) copy-start(f32[128,2816]{1,0:T(8,128)} %copy.59) | copy-start | bytes 4325380
  118.7 1.4 copy-start.5
  118.7 1.5 copy-start.15
  120.0 3.0 %copy-start.12 = (f32[128,2816]{1,0:T(8,128)}, f32[128,2816]{1,0:T(8,128)S(1)}, u32[]{:S(2)}) copy-start(f32[128,2816]{1,0:T(8,128)S(1)} %get-tuple-element.77) | copy-start | bytes 4325380
  120.0 5.3 %copy-start.17 = (f32[128,2816]{1,0:T(8,128)}, f32[128,2816]{1,0:T(8,128)S(1)}, u32[]{:S(2)}) copy-start(f32[128,2816]{1,0:T(8,128)S(1)} %get-tuple-element.76) | copy-start | bytes 4325380
  120.3 2.8 copy-start.19
  123.0 1.2 copy-start.16
  124.2 1.1 copy-start.9
  125.4 11.2 %collective-permute-start.10 = (f32[3,2816]{1,0:T(4,128)S(1)}, f32[3,2816]{1,0:T(4,128)S(1)}, u32[]{:S(2)}, u32[]{:S(2)}) collective-permute-start(f32[3,2816]{1,0:T(4,128)S(1)} %pad_maximum_fusion.10), channel_id=1, source_target_pairs={{0,1},{1,0},{2,3},{3,2},{4,5},{5,4},{6,7},{7,6},{8,9},{9,8},{10,11... | collective-permute-start | bytes 101384 | tf_op jit(solution)/shard_map/ppermute | solution.py:114
  137.7 14.7 %collective-permute-start.11 = (f32[3,2816]{1,0:T(4,128)S(1)}, f32[3,2816]{1,0:T(4,128)S(1)}, u32[]{:S(2)}, u32[]{:S(2)}) collective-permute-start(f32[3,2816]{1,0:T(4,128)S(1)} %pad_maximum_fusion.11), channel_id=1, source_target_pairs={{0,2},{1,3},{2,0},{3,1},{4,6},{5,7},{6,4},{7,5},{8,10},{9,11},{10,... | collective-permute-start | bytes 101384 | tf_op jit(solution)/shard_map/ppermute | solution.py:114
  152.5 5.9 %collective-permute-start.12 = (f32[3,2816]{1,0:T(4,128)S(1)}, f32[3,2816]{1,0:T(4,128)S(1)}, u32[]{:S(2)}, u32[]{:S(2)}) collective-permute-start(f32[3,2816]{1,0:T(4,128)S(1)} %pad_maximum_fusion.12), channel_id=1, source_target_pairs={{0,4},{1,5},{2,6},{3,7},{4,0},{5,1},{6,2},{7,3},{8,12},{9,13},{10,... | collective-permute-start | bytes 101384 | tf_op jit(solution)/shard_map/ppermute | solution.py:114
  158.5 7.4 %collective-permute-start.13 = (f32[3,2816]{1,0:T(4,128)S(1)}, f32[3,2816]{1,0:T(4,128)S(1)}, u32[]{:S(2)}, u32[]{:S(2)}) collective-permute-start(f32[3,2816]{1,0:T(4,128)S(1)} %pad_maximum_fusion.13), channel_id=1, source_target_pairs={{0,8},{1,9},{2,10},{3,11},{4,12},{5,13},{6,14},{7,15},{8,0},{9,1},... | collective-permute-start | bytes 101384 | tf_op jit(solution)/shard_map/ppermute | solution.py:114
  166.2 2.2 copy-start.6
  166.2 2.7 copy-start.10
  166.2 3.1 %copy-start.13 = (f32[128,2816]{1,0:T(8,128)S(1)}, f32[128,2816]{1,0:T(8,128)}, u32[]{:S(2)}) copy-start(f32[128,2816]{1,0:T(8,128)} %copy-done.12) | copy-start | bytes 4325380
  188.9 5.7 %collective-permute-start.15 = (f32[16,8,3168]{2,1,0:T(8,128)}, f32[16,8,3168]{2,1,0:T(8,128)}, u32[]{:S(2)}, u32[]{:S(2)}) collective-permute-start(f32[16,8,3168]{2,1,0:T(8,128)} %dynamic-slice_bitcast_fusion), channel_id=1, source_target_pairs={{0,16},{16,0},{32,48},{48,32},{64,80},{80,64},{96,112},{112,96},{1... | collective-permute-start | bytes 4866056 | tf_op jit(solution)/shard_map/ppermute | solution.py:114
  196.4 12.6 %copy-start.3 = (bf16[11,32,8,256]{3,2,0,1:T(8,128)(2,1)S(1)}, bf16[11,32,8,256]{3,2,0,1:T(8,128)(2,1)}, u32[]{:S(2)}) copy-start(bf16[11,32,8,256]{3,2,0,1:T(8,128)(2,1)} %copy-done.2) | copy-start | bytes 4325380
  197.3 14.5 %collective-permute-start.16 = (f32[4,8,3168]{2,1,0:T(8,128)}, f32[4,8,3168]{2,1,0:T(8,128)}, u32[]{:S(2)}, u32[]{:S(2)}) collective-permute-start(f32[4,8,3168]{2,1,0:T(8,128)} %get-tuple-element.23), channel_id=1, source_target_pairs={{0,32},{16,48},{32,0},{48,16},{64,96},{80,112},{96,64},{112,80},{1... | collective-permute-start | bytes 1216520 | tf_op jit(solution)/shard_map/ppermute | solution.py:114
  199.3 22.5 %collective-permute-start.17 = (f32[4,8,3168]{2,1,0:T(8,128)}, f32[4,8,3168]{2,1,0:T(8,128)}, u32[]{:S(2)}, u32[]{:S(2)}) collective-permute-start(f32[4,8,3168]{2,1,0:T(8,128)} %get-tuple-element.25), channel_id=1, source_target_pairs={{0,128},{16,144},{32,160},{48,176},{64,192},{80,208},{96,224},{112... | collective-permute-start | bytes 1216520 | tf_op jit(solution)/shard_map/ppermute | solution.py:114
  202.8 19.0 %collective-permute-start.18 = (f32[4,8,3168]{2,1,0:T(8,128)S(1)}, f32[4,8,3168]{2,1,0:T(8,128)}, u32[]{:S(2)}, u32[]{:S(2)}) collective-permute-start(f32[4,8,3168]{2,1,0:T(8,128)S(1)} %get-tuple-element.24), channel_id=1, source_target_pairs={{0,160},{16,176},{32,128},{48,144},{64,224},{80,240},{96,192},{112... | collective-permute-start | bytes 1216520 | tf_op jit(solution)/shard_map/ppermute | solution.py:114
  211.7 23.8 %copy-start.1 = (bf16[11,32,8,256]{3,2,0,1:T(8,128)(2,1)S(1)}, bf16[11,32,8,256]{3,2,0,1:T(8,128)(2,1)}, u32[]{:S(2)}) copy-start(bf16[11,32,8,256]{3,2,0,1:T(8,128)(2,1)} %copy-done) | copy-start | bytes 4325380
  211.7 23.8 %copy-start.14 = (bf16[128,2816]{0,1:T(8,128)(2,1)S(1)}, bf16[128,2816]{0,1:T(8,128)(2,1)}, u32[]{:S(2)}) copy-start(bf16[128,2816]{0,1:T(8,128)(2,1)} %copy.67) | copy-start | bytes 2162692
  223.8 16.1 %collective-permute-start.19 = (f32[1,8,3168]{2,1,0:T(8,128)}, f32[1,8,3168]{2,1,0:T(8,128)}, u32[]{:S(2)}, u32[]{:S(2)}) collective-permute-start(f32[1,8,3168]{2,1,0:T(8,128)} %get-tuple-element.40), channel_id=1, source_target_pairs={{0,64},{16,80},{32,96},{48,112},{64,0},{80,16},{96,32},{112,48},{1... | collective-permute-start | bytes 304136 | tf_op jit(solution)/shard_map/ppermute | solution.py:114
  226.6 13.4 %collective-permute-start.20 = (f32[1,8,3168]{2,1,0:T(8,128)}, f32[1,8,3168]{2,1,0:T(8,128)}, u32[]{:S(2)}, u32[]{:S(2)}) collective-permute-start(f32[1,8,3168]{2,1,0:T(8,128)} %get-tuple-element.42), channel_id=1, source_target_pairs={{0,256},{16,272},{32,288},{48,304},{64,320},{80,336},{96,352},{112... | collective-permute-start | bytes 304136 | tf_op jit(solution)/shard_map/ppermute | solution.py:114
  231.7 10.0 %collective-permute-start.21 = (f32[1,8,3168]{2,1,0:T(8,128)S(1)}, f32[1,8,3168]{2,1,0:T(8,128)}, u32[]{:S(2)}, u32[]{:S(2)}) collective-permute-start(f32[1,8,3168]{2,1,0:T(8,128)S(1)} %get-tuple-element.41), channel_id=1, source_target_pairs={{0,320},{16,336},{32,352},{48,368},{64,256},{80,272},{96,288},{112... | collective-permute-start | bytes 304136 | tf_op jit(solution)/shard_map/ppermute | solution.py:114
  235.5 1.4 copy-start.11
  240.0 13.6 %copy-start.7 = (f32[128,2816]{1,0:T(8,128)S(1)}, f32[128,2816]{1,0:T(8,128)}, u32[]{:S(2)}) copy-start(f32[128,2816]{1,0:T(8,128)} %copy.63) | copy-start | bytes 4325380
  243.1 22.2 %collective-permute-start.22 = (f32[4,8,528]{2,1,0:T(8,128)S(1)}, f32[4,8,528]{2,1,0:T(8,128)S(1)}, u32[]{:S(2)}, u32[]{:S(2)}) collective-permute-start(f32[4,8,528]{2,1,0:T(8,128)S(1)} %get-tuple-element.45), channel_id=1, source_target_pairs={{0,4},{1,5},{2,6},{3,7},{4,0},{5,1},{6,2},{7,3},{8,12},{9,13},{10,... | collective-permute-start | bytes 202760 | tf_op jit(solution)/shard_map/ppermute | solution.py:114
  246.0 19.3 %collective-permute-start.23 = (f32[4,8,528]{2,1,0:T(8,128)S(1)}, f32[4,8,528]{2,1,0:T(8,128)S(1)}, u32[]{:S(2)}, u32[]{:S(2)}) collective-permute-start(f32[4,8,528]{2,1,0:T(8,128)S(1)} %get-tuple-element.47), channel_id=1, source_target_pairs={{0,8},{1,9},{2,10},{3,11},{4,12},{5,13},{6,14},{7,15},{8,0},{9,1},... | collective-permute-start | bytes 202760 | tf_op jit(solution)/shard_map/ppermute | solution.py:114
  249.8 15.5 %collective-permute-start.24 = (f32[4,8,528]{2,1,0:T(8,128)S(1)}, f32[4,8,528]{2,1,0:T(8,128)S(1)}, u32[]{:S(2)}, u32[]{:S(2)}) collective-permute-start(f32[4,8,528]{2,1,0:T(8,128)S(1)} %get-tuple-element.46), channel_id=1, source_target_pairs={{0,12},{1,13},{2,14},{3,15},{4,8},{5,9},{6,10},{7,11},{8,4},{9,5},... | collective-permute-start | bytes 202760 | tf_op jit(solution)/shard_map/ppermute | solution.py:114
  256.2 26.3 %collective-permute-start.14 = (f32[3,2816]{1,0:T(4,128)S(1)}, f32[3,2816]{1,0:T(4,128)S(1)}, u32[]{:S(2)}, u32[]{:S(2)}) collective-permute-start(f32[3,2816]{1,0:T(4,128)S(1)} %slice.215), channel_id=1, source_target_pairs={{1,0},{2,1},{3,2},{4,3},{5,4},{6,5},{7,6},{8,7},{9,8},{10,9},{11,1... | collective-permute-start | bytes 101384 | tf_op jit(solution)/shard_map/ppermute | solution.py:13
  265.4 18.6 %collective-permute-start.25 = (f32[1,8,528]{2,1,0:T(8,128)S(1)}, f32[1,8,528]{2,1,0:T(8,128)S(1)}, u32[]{:S(2)}, u32[]{:S(2)}) collective-permute-start(f32[1,8,528]{2,1,0:T(8,128)S(1)} %get-tuple-element.59), channel_id=1, source_target_pairs={{0,1},{1,0},{2,3},{3,2},{4,5},{5,4},{6,7},{7,6},{8,9},{9,8},{10,11... | collective-permute-start | bytes 50696 | tf_op jit(solution)/shard_map/ppermute | solution.py:114
  268.3 15.7 %collective-permute-start.26 = (f32[1,8,528]{2,1,0:T(8,128)S(1)}, f32[1,8,528]{2,1,0:T(8,128)S(1)}, u32[]{:S(2)}, u32[]{:S(2)}) collective-permute-start(f32[1,8,528]{2,1,0:T(8,128)S(1)} %get-tuple-element.61), channel_id=1, source_target_pairs={{0,2},{1,3},{2,0},{3,1},{4,6},{5,7},{6,4},{7,5},{8,10},{9,11},{10,... | collective-permute-start | bytes 50696 | tf_op jit(solution)/shard_map/ppermute | solution.py:114
  278.2 9.6 %collective-permute-start.27 = (f32[1,8,528]{2,1,0:T(8,128)S(1)}, f32[1,8,528]{2,1,0:T(8,128)S(1)}, u32[]{:S(2)}, u32[]{:S(2)}) collective-permute-start(f32[1,8,528]{2,1,0:T(8,128)S(1)} %get-tuple-element.60), channel_id=1, source_target_pairs={{0,3},{1,2},{2,1},{3,0},{4,7},{5,6},{6,5},{7,4},{8,11},{9,10},{10,... | collective-permute-start | bytes 50696 | tf_op jit(solution)/shard_map/ppermute | solution.py:114

commit v5 on v3

--- a/solution.py
+++ b/solution.py
@@ -267,7 +267,8 @@
         start = taps - 1 - tap
         grad_in = grad_in + taps_f[tap] * dpad[start : start + length]
     local_wgrad = grad_heads(conv_b, d_recur, head_width)
-    local_rgrad = jnp.sum(d_log * (-8.0 * recur_gate), axis=0)
+    token_ones = jnp.ones((1, length), jnp.float32)
+    local_rgrad = jnp.dot(token_ones, d_log * (-8.0 * recur_gate), precision=exact)[0]
     by_row = local_wgrad.reshape(dp_size, rows, width)
     row_sum, rgrad = summed_apart(by_row, local_rgrad, "dp", spread_steps(dp_size, 1))
     by_channel = row_sum.reshape(rows, ctx_size, cols).transpose(1, 0, 2)

time: 290 us -> 292 us (level)
    dot_general x0 -> x1, other arithmetic: none -> 4.67 us  [on_device(): jnp.dot(token_ones, d_log * (-8.0 * recur_gate), precision=exact)[0]]
    reduce_sum x1 -> x0, other arithmetic: 4.58 us -> none  [on_device(): local_rgrad = jnp.sum(d_log * (-8.0 * recur_gate), axis=0)]
where the time goes in v5:
time: 292 us; the launch traced here: 289 us
  starting transfers between devices  136 us (47%)
  waiting for transfers between devices  67.1 us (23%)
  local copies, waits for them, and re-layouts  39.9 us (14%)
  other arithmetic  26.7 us (9%)
  matrix products  16.6 us (6%)
    ppermute x26, starting transfers between devices, exchanged(): return lax.ppermute(array, axis, [(i, i ^ mask) for i in range(length)])  121 us
    ppermute x26, waiting for transfers between devices, exchanged(): return lax.ppermute(array, axis, [(i, i ^ mask) for i in range(length)])  64.1 us
    ppermute x2, starting transfers between devices, passed_along(): return lax.ppermute(array, axis, pairs)  15.6 us
    reshape x2, local copies, waits for them, and re-layouts, mix_heads(): return result.reshape(tokens, head_count * head_width)  6 us
  transfers between devices with their start and end apart: 28, of which 18 were waited for; matrix products, arithmetic and copies ran while one was open for 7% of the time, Pallas kernels for 0%

profile of v5, /device:TPU:6, one launch (start us, length us, event | category | flops | bytes accessed | tf_op | source)
XLA Modules:
  0.0 288.7 jit_solution(6206703404028272373)
XLA Ops:
  5.3 9.1 %collective-permute-start = (bf16[24,176]{1,0:T(8,128)(2,1)S(1)}, bf16[24,176]{1,0:T(8,128)(2,1)S(1)}, u32[]{:S(2)}, u32[]{:S(2)}) collective-permute-start(bf16[24,176]{1,0:T(8,128)(2,1)S(1)} %concatenate.21), channel_id=1, source_target_pairs={{0,1},{1,0},{2,3},{3,2},{4,5},{5,4},{6,7},{7,6},{8,9},{9,8},{10,11... | collective-permute-start | bytes 25352 | tf_op jit(solution)/shard_map/ppermute | solution.py:108
  16.1 14.5 %collective-permute-start.1 = (bf16[2,24,176]{2,1,0:T(8,128)(2,1)S(1)}, bf16[2,24,176]{2,1,0:T(8,128)(2,1)S(1)}, u32[]{:S(2)}, u32[]{:S(2)}) collective-permute-start(bf16[2,24,176]{2,1,0:T(8,128)(2,1)S(1)} %get-tuple-element.72), channel_id=1, source_target_pairs={{0,2},{1,3},{2,0},{3,1},{4,6},{5,7},{6,4},{7,5},{8,10},{9,11},{10,... | collective-permute-start | bytes 50696 | tf_op jit(solution)/shard_map/ppermute | solution.py:108
  32.5 2.7 collective-permute-start.2
  35.2 3.2 %collective-permute-done.2 = bf16[2,2,24,176]{3,2,1,0:T(8,128)(2,1)S(1)} collective-permute-done((bf16[2,2,24,176]{3,2,1,0:T(8,128)(2,1)S(1)}, bf16[2,2,24,176]{3,2,1,0:T(8,128)(2,1)S(1)}, u32[]{:S(2)}, u32[]{:S(2)}) %collective-permute-start.2) | collective-permute-done | bytes 33824 | tf_op jit(solution)/shard_map/ppermute | solution.py:108
  38.5 4.2 %collective-permute-start.3 = (bf16[2,2,2,24,176]{4,3,2,1,0:T(8,128)(2,1)S(1)}, bf16[2,2,2,24,176]{4,3,2,1,0:T(8,128)(2,1)S(1)}, u32[]{:S(2)}, u32[]{:S(2)}) collective-permute-start(bf16[2,2,2,24,176]{4,3,2,1,0:T(8,128)(2,1)S(1)} %get-tuple-element.55), channel_id=1, source_target_pairs={{0,8},{1,9},{2,10},{3,11},{4,12},{5,13},{6,14},{7,15},{8,0},{9,1},... | collective-permute-start | bytes 202760 | tf_op jit(solution)/shard_map/ppermute | solution.py:108
  42.8 3.8 %collective-permute-done.3 = bf16[2,2,2,24,176]{4,3,2,1,0:T(8,128)(2,1)S(1)} collective-permute-done((bf16[2,2,2,24,176]{4,3,2,1,0:T(8,128)(2,1)S(1)}, bf16[2,2,2,24,176]{4,3,2,1,0:T(8,128)(2,1)S(1)}, u32[]{:S(2)}, u32[]{:S(2)}) %collective-permute-start.3) | collective-permute-done | bytes 67616 | tf_op jit(solution)/shard_map/ppermute | solution.py:108
  47.1 5.1 %collective-permute-start.4 = (bf16[11,16,256]{2,0,1:T(8,128)(2,1)S(1)}, bf16[11,16,256]{2,0,1:T(8,128)(2,1)S(1)}, u32[]{:S(2)}, u32[]{:S(2)}) collective-permute-start(bf16[11,16,256]{2,0,1:T(8,128)(2,1)S(1)} %bitcast.199), channel_id=1, source_target_pairs={{0,256},{16,272},{32,288},{48,304},{64,320},{80,336},{96,352},{112... | collective-permute-start | bytes 270344 | tf_op jit(solution)/shard_map/ppermute | solution.py:108
  52.2 3.2 %collective-permute-done.4 = bf16[11,16,256]{2,0,1:T(8,128)(2,1)S(1)} collective-permute-done((bf16[11,16,256]{2,0,1:T(8,128)(2,1)S(1)}, bf16[11,16,256]{2,0,1:T(8,128)(2,1)S(1)}, u32[]{:S(2)}, u32[]{:S(2)}) %collective-permute-start.4) | collective-permute-done | bytes 90144 | tf_op jit(solution)/shard_map/ppermute | solution.py:108
  55.6 3.4 %collective-permute-start.5 = (bf16[2,11,16,256]{3,1,2,0:T(8,128)(2,1)S(1)}, bf16[2,11,16,256]{3,1,2,0:T(8,128)(2,1)S(1)}, u32[]{:S(2)}, u32[]{:S(2)}) collective-permute-start(bf16[2,11,16,256]{3,1,2,0:T(8,128)(2,1)S(1)} %get-tuple-element.48), channel_id=1, source_target_pairs={{0,64},{16,80},{32,96},{48,112},{64,0},{80,16},{96,32},{112,48},{1... | collective-permute-start | bytes 540680 | tf_op jit(solution)/shard_map/ppermute | solution.py:108
  59.0 8.5 %collective-permute-done.5 = bf16[2,11,16,256]{3,1,2,0:T(8,128)(2,1)S(1)} collective-permute-done((bf16[2,11,16,256]{3,1,2,0:T(8,128)(2,1)S(1)}, bf16[2,11,16,256]{3,1,2,0:T(8,128)(2,1)S(1)}, u32[]{:S(2)}, u32[]{:S(2)}) %collective-permute-start.5) | collective-permute-done | bytes 180256 | tf_op jit(solution)/shard_map/ppermute | solution.py:108
  68.0 3.5 %collective-permute-start.6 = (bf16[2,2,11,16,256]{4,3,2,0,1:T(8,128)(2,1)S(1)}, bf16[2,2,11,16,256]{4,3,2,0,1:T(8,128)(2,1)S(1)}, u32[]{:S(2)}, u32[]{:S(2)}) collective-permute-start(bf16[2,2,11,16,256]{4,3,2,0,1:T(8,128)(2,1)S(1)} %get-tuple-element.43), channel_id=1, source_target_pairs={{0,128},{16,144},{32,160},{48,176},{64,192},{80,208},{96,224},{112... | collective-permute-start | bytes 1081352 | tf_op jit(solution)/shard_map/ppermute | solution.py:108
  71.5 5.8 %collective-permute-done.6 = bf16[2,2,11,16,256]{4,3,2,0,1:T(8,128)(2,1)S(1)} collective-permute-done((bf16[2,2,11,16,256]{4,3,2,0,1:T(8,128)(2,1)S(1)}, bf16[2,2,11,16,256]{4,3,2,0,1:T(8,128)(2,1)S(1)}, u32[]{:S(2)}, u32[]{:S(2)}) %collective-permute-start.6) | collective-permute-done | bytes 360480 | tf_op jit(solution)/shard_map/ppermute | solution.py:108
  80.5 7.4 %collective-permute-start.9 = (bf16[3,2816]{1,0:T(4,128)(2,1)S(1)}, bf16[3,2816]{1,0:T(4,128)(2,1)S(1)}, u32[]{:S(2)}, u32[]{:S(2)}) collective-permute-start(bf16[3,2816]{1,0:T(4,128)(2,1)S(1)} %slice_bitcast_fusion.2), channel_id=1, source_target_pairs={{0,1},{1,2},{2,3},{3,4},{4,5},{5,6},{6,7},{7,8},{8,9},{9,10},{10,1... | collective-permute-start | bytes 50696 | tf_op jit(solution)/shard_map/ppermute | solution.py:13
  87.9 3.0 %collective-permute-done.7 = bf16[2,2,2,11,16,256]{5,4,3,1,0,2:T(8,128)(2,1)S(1)} collective-permute-done((bf16[2,2,2,11,16,256]{5,4,3,1,0,2:T(8,128)(2,1)S(1)}, bf16[2,2,2,11,16,256]{5,4,3,1,0,2:T(8,128)(2,1)S(1)}, u32[]{:S(2)}, u32[]{:S(2)}) %collective-permute-start.7) | collective-permute-done | bytes 720928 | tf_op jit(solution)/shard_map/ppermute | solution.py:108
  95.0 3.0 %collective-permute-done.9 = bf16[3,2816]{1,0:T(4,128)(2,1)S(1)} collective-permute-done((bf16[3,2816]{1,0:T(4,128)(2,1)S(1)}, bf16[3,2816]{1,0:T(4,128)(2,1)S(1)}, u32[]{:S(2)}, u32[]{:S(2)}) %collective-permute-start.9) | collective-permute-done | bytes 16928 | tf_op jit(solution)/shard_map/ppermute | solution.py:13
  100.5 2.3 copy.124
  103.1 2.4 fusion.17
  109.2 2.9 %copy.127 = f32[128,2816]{1,0:T(8,128)} copy(f32[128,2816]{0,1:T(8,128)} %bitcast.182) | data formatting | bytes 2883584 | tf_op jit(solution)/shard_map/reshape | solution.py:21
  112.1 2.9 fusion.28
  115.0 3.1 %copy.131 = f32[128,2816]{1,0:T(8,128)} copy(f32[128,2816]{0,1:T(8,128)} %bitcast.183) | data formatting | bytes 2883584 | tf_op jit(solution)/shard_map/reshape | solution.py:21
  119.7 2.8 convolution_multiply_fusion
  124.8 3.5 %collective-permute-start.10 = (f32[3,2816]{1,0:T(4,128)S(1)}, f32[3,2816]{1,0:T(4,128)S(1)}, u32[]{:S(2)}, u32[]{:S(2)}) collective-permute-start(f32[3,2816]{1,0:T(4,128)S(1)} %pad_maximum_fusion.9), channel_id=1, source_target_pairs={{0,1},{1,0},{2,3},{3,2},{4,5},{5,4},{6,7},{7,6},{8,9},{9,8},{10,11... | collective-permute-start | bytes 101384 | tf_op jit(solution)/shard_map/ppermute | solution.py:108
  128.3 6.6 %collective-permute-done.10 = f32[3,2816]{1,0:T(4,128)S(1)} collective-permute-done((f32[3,2816]{1,0:T(4,128)S(1)}, f32[3,2816]{1,0:T(4,128)S(1)}, u32[]{:S(2)}, u32[]{:S(2)}) %collective-permute-start.10) | collective-permute-done | bytes 33824 | tf_op jit(solution)/shard_map/ppermute | solution.py:108
  136.0 12.1 %collective-permute-start.11 = (f32[3,2816]{1,0:T(4,128)S(1)}, f32[3,2816]{1,0:T(4,128)S(1)}, u32[]{:S(2)}, u32[]{:S(2)}) collective-permute-start(f32[3,2816]{1,0:T(4,128)S(1)} %pad_maximum_fusion.10), channel_id=1, source_target_pairs={{0,2},{1,3},{2,0},{3,1},{4,6},{5,7},{6,4},{7,5},{8,10},{9,11},{10,... | collective-permute-start | bytes 101384 | tf_op jit(solution)/shard_map/ppermute | solution.py:108
  148.2 2.5 collective-permute-done.11
  150.8 2.7 collective-permute-start.12
  153.5 3.2 %collective-permute-done.12 = f32[3,2816]{1,0:T(4,128)S(1)} collective-permute-done((f32[3,2816]{1,0:T(4,128)S(1)}, f32[3,2816]{1,0:T(4,128)S(1)}, u32[]{:S(2)}, u32[]{:S(2)}) %collective-permute-start.12) | collective-permute-done | bytes 33824 | tf_op jit(solution)/shard_map/ppermute | solution.py:108
  156.8 3.5 %collective-permute-start.13 = (f32[3,2816]{1,0:T(4,128)S(1)}, f32[3,2816]{1,0:T(4,128)S(1)}, u32[]{:S(2)}, u32[]{:S(2)}) collective-permute-start(f32[3,2816]{1,0:T(4,128)S(1)} %pad_maximum_fusion.12), channel_id=1, source_target_pairs={{0,8},{1,9},{2,10},{3,11},{4,12},{5,13},{6,14},{7,15},{8,0},{9,1},... | collective-permute-start | bytes 101384 | tf_op jit(solution)/shard_map/ppermute | solution.py:108
  160.3 3.9 %collective-permute-done.13 = f32[3,2816]{1,0:T(4,128)S(1)} collective-permute-done((f32[3,2816]{1,0:T(4,128)S(1)}, f32[3,2816]{1,0:T(4,128)S(1)}, u32[]{:S(2)}, u32[]{:S(2)}) %collective-permute-start.13) | collective-permute-done | bytes 33824 | tf_op jit(solution)/shard_map/ppermute | solution.py:108
  167.5 4.7 %multiply_bitcast_fusion = (f32[2816,128]{0,1:T(8,128)}, f32[128,2816]{1,0:T(8,128)S(1)}, bf16[128,2816]{1,0:T(8,128)(2,1)}, f32[128,2816]{1,0:T(8,128)}) fusion(f32[128,2816]{1,0:T(8,128)S(1)} %copy-done.4, f32[2816]{0:T(1024)S(1)} %add.402, f32[128,2816]{1,0:T(8,128)S(1)} %copy-done.6, f32[2816]{0:T(1024)S(1)} %add.406, f32[2816]{0:T(1024)S(1)} %mul.339, ...), kind=kLoop, calls=%fused_computation.69 | loop fusion | flops 17301504 | bytes 18135040 | tf_op jit(solution)/shard_map/dot_general | solution.py:271
  175.7 3.4 %copy.139 = f32[256,11,256]{2,1,0:T(8,128)} copy(f32[256,11,256]{0,2,1:T(8,128)S(1)} %convolution_bitcast_fusion) | data formatting | bytes 5767168 | tf_op jit(solution)/shard_map/thk,thj->khj/transpose | solution.py:37
  179.1 4.8 %concatenate.25 = f32[2,2,2,2,2,8,2816]{6,5,4,3,2,1,0:T(8,128)} reshape(f32[256,11,256]{2,1,0:T(8,128)} %copy.139) | data formatting | bytes 5767168 | tf_op jit(solution)/shard_map/concatenate | solution.py:185
  191.4 3.8 %collective-permute-done.15 = f32[16,8,3168]{2,1,0:T(8,128)} collective-permute-done((f32[16,8,3168]{2,1,0:T(8,128)}, f32[16,8,3168]{2,1,0:T(8,128)}, u32[]{:S(2)}, u32[]{:S(2)}) %collective-permute-start.15) | collective-permute-done | bytes 1622048 | tf_op jit(solution)/shard_map/ppermute | solution.py:108
  199.8 3.5 %collective-permute-start.17 = (f32[4,8,3168]{2,1,0:T(8,128)}, f32[4,8,3168]{2,1,0:T(8,128)}, u32[]{:S(2)}, u32[]{:S(2)}) collective-permute-start(f32[4,8,3168]{2,1,0:T(8,128)} %get-tuple-element.25), channel_id=1, source_target_pairs={{0,128},{16,144},{32,160},{48,176},{64,192},{80,208},{96,224},{112... | collective-permute-start | bytes 1216520 | tf_op jit(solution)/shard_map/ppermute | solution.py:108
  203.3 3.8 %collective-permute-start.18 = (f32[4,8,3168]{2,1,0:T(8,128)S(1)}, f32[4,8,3168]{2,1,0:T(8,128)}, u32[]{:S(2)}, u32[]{:S(2)}) collective-permute-start(f32[4,8,3168]{2,1,0:T(8,128)S(1)} %get-tuple-element.24), channel_id=1, source_target_pairs={{0,160},{16,176},{32,128},{48,144},{64,224},{80,240},{96,192},{112... | collective-permute-start | bytes 1216520 | tf_op jit(solution)/shard_map/ppermute | solution.py:108
  209.5 2.8 fusion.30
  212.4 9.9 %collective-permute-done.17 = f32[4,8,3168]{2,1,0:T(8,128)} collective-permute-done((f32[4,8,3168]{2,1,0:T(8,128)}, f32[4,8,3168]{2,1,0:T(8,128)}, u32[]{:S(2)}, u32[]{:S(2)}) %collective-permute-start.17) | collective-permute-done | bytes 405536 | tf_op jit(solution)/shard_map/ppermute | solution.py:108
  224.4 3.9 %collective-permute-start.19 = (f32[1,8,3168]{2,1,0:T(8,128)}, f32[1,8,3168]{2,1,0:T(8,128)}, u32[]{:S(2)}, u32[]{:S(2)}) collective-permute-start(f32[1,8,3168]{2,1,0:T(8,128)} %get-tuple-element.40), channel_id=1, source_target_pairs={{0,64},{16,80},{32,96},{48,112},{64,0},{80,16},{96,32},{112,48},{1... | collective-permute-start | bytes 304136 | tf_op jit(solution)/shard_map/ppermute | solution.py:108
  228.3 5.1 %collective-permute-start.20 = (f32[1,8,3168]{2,1,0:T(8,128)}, f32[1,8,3168]{2,1,0:T(8,128)}, u32[]{:S(2)}, u32[]{:S(2)}) collective-permute-start(f32[1,8,3168]{2,1,0:T(8,128)} %get-tuple-element.42), channel_id=1, source_target_pairs={{0,256},{16,272},{32,288},{48,304},{64,320},{80,336},{96,352},{112... | collective-permute-start | bytes 304136 | tf_op jit(solution)/shard_map/ppermute | solution.py:108
  233.4 2.6 collective-permute-start.21
  240.5 2.8 collective-permute-done.21
  244.8 8.0 %collective-permute-start.22 = (f32[4,8,528]{2,1,0:T(8,128)S(1)}, f32[4,8,528]{2,1,0:T(8,128)S(1)}, u32[]{:S(2)}, u32[]{:S(2)}) collective-permute-start(f32[4,8,528]{2,1,0:T(8,128)S(1)} %get-tuple-element.45), channel_id=1, source_target_pairs={{0,1},{1,0},{2,3},{3,2},{4,5},{5,4},{6,7},{7,6},{8,9},{9,8},{10,11... | collective-permute-start | bytes 202760 | tf_op jit(solution)/shard_map/ppermute | solution.py:108
  252.8 9.4 %collective-permute-start.23 = (f32[4,8,528]{2,1,0:T(8,128)S(1)}, f32[4,8,528]{2,1,0:T(8,128)S(1)}, u32[]{:S(2)}, u32[]{:S(2)}) collective-permute-start(f32[4,8,528]{2,1,0:T(8,128)S(1)} %get-tuple-element.47), channel_id=1, source_target_pairs={{0,2},{1,3},{2,0},{3,1},{4,6},{5,7},{6,4},{7,5},{8,10},{9,11},{10,... | collective-permute-start | bytes 202760 | tf_op jit(solution)/shard_map/ppermute | solution.py:108
  264.2 2.6 add_add_fusion
  266.8 8.2 %collective-permute-start.14 = (f32[3,2816]{1,0:T(4,128)S(1)}, f32[3,2816]{1,0:T(4,128)S(1)}, u32[]{:S(2)}, u32[]{:S(2)}) collective-permute-start(f32[3,2816]{1,0:T(4,128)S(1)} %slice.215), channel_id=1, source_target_pairs={{1,0},{2,1},{3,2},{4,3},{5,4},{6,5},{7,6},{8,7},{9,8},{10,9},{11,1... | collective-permute-start | bytes 101384 | tf_op jit(solution)/shard_map/ppermute | solution.py:13
  275.1 2.4 collective-permute-start.25
  277.6 2.5 collective-permute-start.26
  280.1 5.5 %collective-permute-start.27 = (f32[1,8,528]{2,1,0:T(8,128)S(1)}, f32[1,8,528]{2,1,0:T(8,128)S(1)}, u32[]{:S(2)}, u32[]{:S(2)}) collective-permute-start(f32[1,8,528]{2,1,0:T(8,128)S(1)} %get-tuple-element.60), channel_id=1, source_target_pairs={{0,12},{1,13},{2,14},{3,15},{4,8},{5,9},{6,10},{7,11},{8,4},{9,5},... | collective-permute-start | bytes 50696 | tf_op jit(solution)/shard_map/ppermute | solution.py:108
  (158 shorter events, 62.2 us)
Async XLA Ops:
  5.3 10.8 %collective-permute-start = (bf16[24,176]{1,0:T(8,128)(2,1)S(1)}, bf16[24,176]{1,0:T(8,128)(2,1)S(1)}, u32[]{:S(2)}, u32[]{:S(2)}) collective-permute-start(bf16[24,176]{1,0:T(8,128)(2,1)S(1)} %concatenate.21), channel_id=1, source_target_pairs={{0,1},{1,0},{2,3},{3,2},{4,5},{5,4},{6,7},{7,6},{8,9},{9,8},{10,11... | collective-permute-start | bytes 25352 | tf_op jit(solution)/shard_map/ppermute | solution.py:108
  16.1 16.3 %collective-permute-start.1 = (bf16[2,24,176]{2,1,0:T(8,128)(2,1)S(1)}, bf16[2,24,176]{2,1,0:T(8,128)(2,1)S(1)}, u32[]{:S(2)}, u32[]{:S(2)}) collective-permute-start(bf16[2,24,176]{2,1,0:T(8,128)(2,1)S(1)} %get-tuple-element.72), channel_id=1, source_target_pairs={{0,2},{1,3},{2,0},{3,1},{4,6},{5,7},{6,4},{7,5},{8,10},{9,11},{10,... | collective-permute-start | bytes 50696 | tf_op jit(solution)/shard_map/ppermute | solution.py:108
  32.5 6.0 %collective-permute-start.2 = (bf16[2,2,24,176]{3,2,1,0:T(8,128)(2,1)S(1)}, bf16[2,2,24,176]{3,2,1,0:T(8,128)(2,1)S(1)}, u32[]{:S(2)}, u32[]{:S(2)}) collective-permute-start(bf16[2,2,24,176]{3,2,1,0:T(8,128)(2,1)S(1)} %get-tuple-element.68), channel_id=1, source_target_pairs={{0,4},{1,5},{2,6},{3,7},{4,0},{5,1},{6,2},{7,3},{8,12},{9,13},{10,... | collective-permute-start | bytes 101384 | tf_op jit(solution)/shard_map/ppermute | solution.py:108
  38.5 8.0 %collective-permute-start.3 = (bf16[2,2,2,24,176]{4,3,2,1,0:T(8,128)(2,1)S(1)}, bf16[2,2,2,24,176]{4,3,2,1,0:T(8,128)(2,1)S(1)}, u32[]{:S(2)}, u32[]{:S(2)}) collective-permute-start(bf16[2,2,2,24,176]{4,3,2,1,0:T(8,128)(2,1)S(1)} %get-tuple-element.55), channel_id=1, source_target_pairs={{0,8},{1,9},{2,10},{3,11},{4,12},{5,13},{6,14},{7,15},{8,0},{9,1},... | collective-permute-start | bytes 202760 | tf_op jit(solution)/shard_map/ppermute | solution.py:108
  47.1 8.4 %collective-permute-start.4 = (bf16[11,16,256]{2,0,1:T(8,128)(2,1)S(1)}, bf16[11,16,256]{2,0,1:T(8,128)(2,1)S(1)}, u32[]{:S(2)}, u32[]{:S(2)}) collective-permute-start(bf16[11,16,256]{2,0,1:T(8,128)(2,1)S(1)} %bitcast.199), channel_id=1, source_target_pairs={{0,256},{16,272},{32,288},{48,304},{64,320},{80,336},{96,352},{112... | collective-permute-start | bytes 270344 | tf_op jit(solution)/shard_map/ppermute | solution.py:108
  55.6 12.0 %collective-permute-start.5 = (bf16[2,11,16,256]{3,1,2,0:T(8,128)(2,1)S(1)}, bf16[2,11,16,256]{3,1,2,0:T(8,128)(2,1)S(1)}, u32[]{:S(2)}, u32[]{:S(2)}) collective-permute-start(bf16[2,11,16,256]{3,1,2,0:T(8,128)(2,1)S(1)} %get-tuple-element.48), channel_id=1, source_target_pairs={{0,64},{16,80},{32,96},{48,112},{64,0},{80,16},{96,32},{112,48},{1... | collective-permute-start | bytes 540680 | tf_op jit(solution)/shard_map/ppermute | solution.py:108
  68.0 9.3 %collective-permute-start.6 = (bf16[2,2,11,16,256]{4,3,2,0,1:T(8,128)(2,1)S(1)}, bf16[2,2,11,16,256]{4,3,2,0,1:T(8,128)(2,1)S(1)}, u32[]{:S(2)}, u32[]{:S(2)}) collective-permute-start(bf16[2,2,11,16,256]{4,3,2,0,1:T(8,128)(2,1)S(1)} %get-tuple-element.43), channel_id=1, source_target_pairs={{0,128},{16,144},{32,160},{48,176},{64,192},{80,208},{96,224},{112... | collective-permute-start | bytes 1081352 | tf_op jit(solution)/shard_map/ppermute | solution.py:108
  77.7 13.2 %collective-permute-start.7 = (bf16[2,2,2,11,16,256]{5,4,3,1,0,2:T(8,128)(2,1)S(1)}, bf16[2,2,2,11,16,256]{5,4,3,1,0,2:T(8,128)(2,1)S(1)}, u32[]{:S(2)}, u32[]{:S(2)}) collective-permute-start(bf16[2,2,2,11,16,256]{5,4,3,1,0,2:T(8,128)(2,1)S(1)} %get-tuple-element.34), channel_id=1, source_target_pairs={{0,32},{16,48},{32,0},{48,16},{64,96},{80,112},{96,64},{112,80},{1... | collective-permute-start | bytes 2162696 | tf_op jit(solution)/shard_map/ppermute | solution.py:108
  80.5 17.5 %collective-permute-start.9 = (bf16[3,2816]{1,0:T(4,128)(2,1)S(1)}, bf16[3,2816]{1,0:T(4,128)(2,1)S(1)}, u32[]{:S(2)}, u32[]{:S(2)}) collective-permute-start(bf16[3,2816]{1,0:T(4,128)(2,1)S(1)} %slice_bitcast_fusion.2), channel_id=1, source_target_pairs={{0,1},{1,2},{2,3},{3,4},{4,5},{5,6},{6,7},{7,8},{8,9},{9,10},{10,1... | collective-permute-start | bytes 50696 | tf_op jit(solution)/shard_map/ppermute | solution.py:13
  91.6 6.4 %copy-start.19 = (bf16[1,128,2816]{2,1,0:T(8,128)(2,1)S(1)}, bf16[1,128,2816]{2,1,0:T(8,128)(2,1)}, u32[]{:S(2)}) copy-start(bf16[1,128,2816]{2,1,0:T(8,128)(2,1)} %param.9) | copy-start | bytes 2162692
  92.9 10.1 %collective-permute-start.8 = (bf16[2,2,2,2,11,16,256]{6,5,4,2,1,0,3:T(8,128)(2,1)}, bf16[2,2,2,2,11,16,256]{6,5,4,2,1,0,3:T(8,128)(2,1)}, u32[]{:S(2)}, u32[]{:S(2)}) collective-permute-start(bf16[2,2,2,2,11,16,256]{6,5,4,2,1,0,3:T(8,128)(2,1)} %get-tuple-element.30), channel_id=1, source_target_pairs={{0,16},{16,0},{32,48},{48,32},{64,80},{80,64},{96,112},{112,96},{1... | collective-permute-start | bytes 4325384 | tf_op jit(solution)/shard_map/ppermute | solution.py:108
  106.6 2.7 copy-start.2
  106.6 5.6 %copy-start = (bf16[11,32,8,256]{3,2,0,1:T(8,128)(2,1)}, bf16[11,32,8,256]{3,2,0,1:T(8,128)(2,1)S(1)}, u32[]{:S(2)}) copy-start(bf16[11,32,8,256]{3,2,0,1:T(8,128)(2,1)S(1)} %get-tuple-element.20) | copy-start | bytes 4325380
  115.0 3.1 %copy-start.4 = (f32[128,2816]{1,0:T(8,128)S(1)}, f32[128,2816]{1,0:T(8,128)}, u32[]{:S(2)}) copy-start(f32[128,2816]{1,0:T(8,128)} %copy.127) | copy-start | bytes 4325380
  118.1 1.4 copy-start.5
  118.1 1.5 copy-start.16
  119.4 3.0 %copy-start.12 = (f32[128,2816]{1,0:T(8,128)}, f32[128,2816]{1,0:T(8,128)S(1)}, u32[]{:S(2)}) copy-start(f32[128,2816]{1,0:T(8,128)S(1)} %get-tuple-element.77) | copy-start | bytes 4325380
  119.4 5.3 %copy-start.18 = (f32[128,2816]{1,0:T(8,128)}, f32[128,2816]{1,0:T(8,128)S(1)}, u32[]{:S(2)}) copy-start(f32[128,2816]{1,0:T(8,128)S(1)} %get-tuple-element.76) | copy-start | bytes 4325380
  119.7 2.8 copy-start.20
  122.4 1.2 copy-start.17
  123.6 1.1 copy-start.9
  124.8 10.1 %collective-permute-start.10 = (f32[3,2816]{1,0:T(4,128)S(1)}, f32[3,2816]{1,0:T(4,128)S(1)}, u32[]{:S(2)}, u32[]{:S(2)}) collective-permute-start(f32[3,2816]{1,0:T(4,128)S(1)} %pad_maximum_fusion.9), channel_id=1, source_target_pairs={{0,1},{1,0},{2,3},{3,2},{4,5},{5,4},{6,7},{7,6},{8,9},{9,8},{10,11... | collective-permute-start | bytes 101384 | tf_op jit(solution)/shard_map/ppermute | solution.py:108
  136.0 14.7 %collective-permute-start.11 = (f32[3,2816]{1,0:T(4,128)S(1)}, f32[3,2816]{1,0:T(4,128)S(1)}, u32[]{:S(2)}, u32[]{:S(2)}) collective-permute-start(f32[3,2816]{1,0:T(4,128)S(1)} %pad_maximum_fusion.10), channel_id=1, source_target_pairs={{0,2},{1,3},{2,0},{3,1},{4,6},{5,7},{6,4},{7,5},{8,10},{9,11},{10,... | collective-permute-start | bytes 101384 | tf_op jit(solution)/shard_map/ppermute | solution.py:108
  150.8 5.9 %collective-permute-start.12 = (f32[3,2816]{1,0:T(4,128)S(1)}, f32[3,2816]{1,0:T(4,128)S(1)}, u32[]{:S(2)}, u32[]{:S(2)}) collective-permute-start(f32[3,2816]{1,0:T(4,128)S(1)} %pad_maximum_fusion.11), channel_id=1, source_target_pairs={{0,4},{1,5},{2,6},{3,7},{4,0},{5,1},{6,2},{7,3},{8,12},{9,13},{10,... | collective-permute-start | bytes 101384 | tf_op jit(solution)/shard_map/ppermute | solution.py:108
  156.8 7.4 %collective-permute-start.13 = (f32[3,2816]{1,0:T(4,128)S(1)}, f32[3,2816]{1,0:T(4,128)S(1)}, u32[]{:S(2)}, u32[]{:S(2)}) collective-permute-start(f32[3,2816]{1,0:T(4,128)S(1)} %pad_maximum_fusion.12), channel_id=1, source_target_pairs={{0,8},{1,9},{2,10},{3,11},{4,12},{5,13},{6,14},{7,15},{8,0},{9,1},... | collective-permute-start | bytes 101384 | tf_op jit(solution)/shard_map/ppermute | solution.py:108
  164.4 2.2 copy-start.6
  164.5 2.7 copy-start.10
  164.5 3.1 %copy-start.13 = (f32[128,2816]{1,0:T(8,128)S(1)}, f32[128,2816]{1,0:T(8,128)}, u32[]{:S(2)}) copy-start(f32[128,2816]{1,0:T(8,128)} %copy-done.12) | copy-start | bytes 4325380
  179.1 4.8 %copy-start.14 = (f32[2816,128]{0,1:T(8,128)S(1)}, f32[2816,128]{0,1:T(8,128)}, u32[]{:S(2)}) copy-start(f32[2816,128]{0,1:T(8,128)} %get-tuple-element.11) | copy-start | bytes 4325380
  189.5 5.7 %collective-permute-start.15 = (f32[16,8,3168]{2,1,0:T(8,128)}, f32[16,8,3168]{2,1,0:T(8,128)}, u32[]{:S(2)}, u32[]{:S(2)}) collective-permute-start(f32[16,8,3168]{2,1,0:T(8,128)} %dynamic-slice_bitcast_fusion), channel_id=1, source_target_pairs={{0,16},{16,0},{32,48},{48,32},{64,80},{80,64},{96,112},{112,96},{1... | collective-permute-start | bytes 4866056 | tf_op jit(solution)/shard_map/ppermute | solution.py:108
  196.9 12.6 %copy-start.3 = (bf16[11,32,8,256]{3,2,0,1:T(8,128)(2,1)S(1)}, bf16[11,32,8,256]{3,2,0,1:T(8,128)(2,1)}, u32[]{:S(2)}) copy-start(bf16[11,32,8,256]{3,2,0,1:T(8,128)(2,1)} %copy-done.2) | copy-start | bytes 4325380
  197.9 14.5 %collective-permute-start.16 = (f32[4,8,3168]{2,1,0:T(8,128)}, f32[4,8,3168]{2,1,0:T(8,128)}, u32[]{:S(2)}, u32[]{:S(2)}) collective-permute-start(f32[4,8,3168]{2,1,0:T(8,128)} %get-tuple-element.23), channel_id=1, source_target_pairs={{0,32},{16,48},{32,0},{48,16},{64,96},{80,112},{96,64},{112,80},{1... | collective-permute-start | bytes 1216520 | tf_op jit(solution)/shard_map/ppermute | solution.py:108
  199.8 22.5 %collective-permute-start.17 = (f32[4,8,3168]{2,1,0:T(8,128)}, f32[4,8,3168]{2,1,0:T(8,128)}, u32[]{:S(2)}, u32[]{:S(2)}) collective-permute-start(f32[4,8,3168]{2,1,0:T(8,128)} %get-tuple-element.25), channel_id=1, source_target_pairs={{0,128},{16,144},{32,160},{48,176},{64,192},{80,208},{96,224},{112... | collective-permute-start | bytes 1216520 | tf_op jit(solution)/shard_map/ppermute | solution.py:108
  203.3 19.0 %collective-permute-start.18 = (f32[4,8,3168]{2,1,0:T(8,128)S(1)}, f32[4,8,3168]{2,1,0:T(8,128)}, u32[]{:S(2)}, u32[]{:S(2)}) collective-permute-start(f32[4,8,3168]{2,1,0:T(8,128)S(1)} %get-tuple-element.24), channel_id=1, source_target_pairs={{0,160},{16,176},{32,128},{48,144},{64,224},{80,240},{96,192},{112... | collective-permute-start | bytes 1216520 | tf_op jit(solution)/shard_map/ppermute | solution.py:108
  212.2 23.8 %copy-start.1 = (bf16[11,32,8,256]{3,2,0,1:T(8,128)(2,1)S(1)}, bf16[11,32,8,256]{3,2,0,1:T(8,128)(2,1)}, u32[]{:S(2)}) copy-start(bf16[11,32,8,256]{3,2,0,1:T(8,128)(2,1)} %copy-done) | copy-start | bytes 4325380
  212.2 23.8 %copy-start.15 = (bf16[128,2816]{0,1:T(8,128)(2,1)S(1)}, bf16[128,2816]{0,1:T(8,128)(2,1)}, u32[]{:S(2)}) copy-start(bf16[128,2816]{0,1:T(8,128)(2,1)} %copy.135) | copy-start | bytes 2162692
  224.4 16.1 %collective-permute-start.19 = (f32[1,8,3168]{2,1,0:T(8,128)}, f32[1,8,3168]{2,1,0:T(8,128)}, u32[]{:S(2)}, u32[]{:S(2)}) collective-permute-start(f32[1,8,3168]{2,1,0:T(8,128)} %get-tuple-element.40), channel_id=1, source_target_pairs={{0,64},{16,80},{32,96},{48,112},{64,0},{80,16},{96,32},{112,48},{1... | collective-permute-start | bytes 304136 | tf_op jit(solution)/shard_map/ppermute | solution.py:108
  228.3 12.3 %collective-permute-start.20 = (f32[1,8,3168]{2,1,0:T(8,128)}, f32[1,8,3168]{2,1,0:T(8,128)}, u32[]{:S(2)}, u32[]{:S(2)}) collective-permute-start(f32[1,8,3168]{2,1,0:T(8,128)} %get-tuple-element.42), channel_id=1, source_target_pairs={{0,256},{16,272},{32,288},{48,304},{64,320},{80,336},{96,352},{112... | collective-permute-start | bytes 304136 | tf_op jit(solution)/shard_map/ppermute | solution.py:108
  233.4 10.0 %collective-permute-start.21 = (f32[1,8,3168]{2,1,0:T(8,128)S(1)}, f32[1,8,3168]{2,1,0:T(8,128)}, u32[]{:S(2)}, u32[]{:S(2)}) collective-permute-start(f32[1,8,3168]{2,1,0:T(8,128)S(1)} %get-tuple-element.41), channel_id=1, source_target_pairs={{0,320},{16,336},{32,352},{48,368},{64,256},{80,272},{96,288},{112... | collective-permute-start | bytes 304136 | tf_op jit(solution)/shard_map/ppermute | solution.py:108
  236.0 1.4 copy-start.11
  240.5 23.7 %copy-start.7 = (f32[128,2816]{1,0:T(8,128)S(1)}, f32[128,2816]{1,0:T(8,128)}, u32[]{:S(2)}) copy-start(f32[128,2816]{1,0:T(8,128)} %copy.131) | copy-start | bytes 4325380
  244.8 30.2 %collective-permute-start.22 = (f32[4,8,528]{2,1,0:T(8,128)S(1)}, f32[4,8,528]{2,1,0:T(8,128)S(1)}, u32[]{:S(2)}, u32[]{:S(2)}) collective-permute-start(f32[4,8,528]{2,1,0:T(8,128)S(1)} %get-tuple-element.45), channel_id=1, source_target_pairs={{0,1},{1,0},{2,3},{3,2},{4,5},{5,4},{6,7},{7,6},{8,9},{9,8},{10,11... | collective-permute-start | bytes 202760 | tf_op jit(solution)/shard_map/ppermute | solution.py:108
  252.8 22.2 %collective-permute-start.23 = (f32[4,8,528]{2,1,0:T(8,128)S(1)}, f32[4,8,528]{2,1,0:T(8,128)S(1)}, u32[]{:S(2)}, u32[]{:S(2)}) collective-permute-start(f32[4,8,528]{2,1,0:T(8,128)S(1)} %get-tuple-element.47), channel_id=1, source_target_pairs={{0,2},{1,3},{2,0},{3,1},{4,6},{5,7},{6,4},{7,5},{8,10},{9,11},{10,... | collective-permute-start | bytes 202760 | tf_op jit(solution)/shard_map/ppermute | solution.py:108
  262.3 12.8 %collective-permute-start.24 = (f32[4,8,528]{2,1,0:T(8,128)S(1)}, f32[4,8,528]{2,1,0:T(8,128)S(1)}, u32[]{:S(2)}, u32[]{:S(2)}) collective-permute-start(f32[4,8,528]{2,1,0:T(8,128)S(1)} %get-tuple-element.46), channel_id=1, source_target_pairs={{0,3},{1,2},{2,1},{3,0},{4,7},{5,6},{6,5},{7,4},{8,11},{9,10},{10,... | collective-permute-start | bytes 202760 | tf_op jit(solution)/shard_map/ppermute | solution.py:108
  266.8 18.8 %collective-permute-start.14 = (f32[3,2816]{1,0:T(4,128)S(1)}, f32[3,2816]{1,0:T(4,128)S(1)}, u32[]{:S(2)}, u32[]{:S(2)}) collective-permute-start(f32[3,2816]{1,0:T(4,128)S(1)} %slice.215), channel_id=1, source_target_pairs={{1,0},{2,1},{3,2},{4,3},{5,4},{6,5},{7,6},{8,7},{9,8},{10,9},{11,1... | collective-permute-start | bytes 101384 | tf_op jit(solution)/shard_map/ppermute | solution.py:13
  275.1 12.0 %collective-permute-start.25 = (f32[1,8,528]{2,1,0:T(8,128)S(1)}, f32[1,8,528]{2,1,0:T(8,128)S(1)}, u32[]{:S(2)}, u32[]{:S(2)}) collective-permute-start(f32[1,8,528]{2,1,0:T(8,128)S(1)} %get-tuple-element.59), channel_id=1, source_target_pairs={{0,4},{1,5},{2,6},{3,7},{4,0},{5,1},{6,2},{7,3},{8,12},{9,13},{10,... | collective-permute-start | bytes 50696 | tf_op jit(solution)/shard_map/ppermute | solution.py:108
  277.6 9.5 %collective-permute-start.26 = (f32[1,8,528]{2,1,0:T(8,128)S(1)}, f32[1,8,528]{2,1,0:T(8,128)S(1)}, u32[]{:S(2)}, u32[]{:S(2)}) collective-permute-start(f32[1,8,528]{2,1,0:T(8,128)S(1)} %get-tuple-element.61), channel_id=1, source_target_pairs={{0,8},{1,9},{2,10},{3,11},{4,12},{5,13},{6,14},{7,15},{8,0},{9,1},... | collective-permute-start | bytes 50696 | tf_op jit(solution)/shard_map/ppermute | solution.py:108
  280.1 7.2 %collective-permute-start.27 = (f32[1,8,528]{2,1,0:T(8,128)S(1)}, f32[1,8,528]{2,1,0:T(8,128)S(1)}, u32[]{:S(2)}, u32[]{:S(2)}) collective-permute-start(f32[1,8,528]{2,1,0:T(8,128)S(1)} %get-tuple-element.60), channel_id=1, source_target_pairs={{0,12},{1,13},{2,14},{3,15},{4,8},{5,9},{6,10},{7,11},{8,4},{9,5},... | collective-permute-start | bytes 50696 | tf_op jit(solution)/shard_map/ppermute | solution.py:108
  (1 other events, 1.1 us)

commit v6 on v3

--- a/solution.py
+++ b/solution.py
@@ -271,7 +271,7 @@
     by_row = local_wgrad.reshape(dp_size, rows, width)
     row_sum, rgrad = summed_apart(by_row, local_rgrad, "dp", spread_steps(dp_size, 1))
     by_channel = row_sum.reshape(rows, ctx_size, cols).transpose(1, 0, 2)
-    wgrad, rgrad = summed_apart(by_channel, rgrad, "ctx", digit_steps(ctx_size))
+    wgrad, rgrad = summed_apart(by_channel, rgrad, "ctx", bit_steps(ctx_size))
     return (grad_in.astype(jnp.bfloat16)[None], wgrad, rgrad)
 
 

time: 290 us -> 300 us (1.034)
  waiting for transfers between devices: 67.1 us -> 90.1 us
  starting transfers between devices: 136 us -> 127 us
    ppermute x26 -> x24, waiting for transfers between devices: 64.1 us -> 82.9 us  [exchanged(): return lax.ppermute(array, axis, [(i, i ^ mask) for i in range(length)])]
    ppermute x2, starting transfers between devices: 15.6 us -> 10.5 us  [passed_along(): return lax.ppermute(array, axis, pairs)]
    ppermute x26 -> x24, starting transfers between devices: 121 us -> 116 us  [exchanged(): return lax.ppermute(array, axis, [(i, i ^ mask) for i in range(length)])]
    ppermute x2, waiting for transfers between devices: 2.96 us -> 7.18 us  [passed_along(): return lax.ppermute(array, axis, pairs)]
  transfers between devices with their start and end apart: 28 -> 26, of which waited for: 18 -> 20; matrix products, arithmetic and copies ran while one was open for 7% -> 7% of each run, Pallas kernels for 0% -> 0%
where the time goes in v6:
time: 300 us; the launch traced here: 299 us
  starting transfers between devices  127 us (42%)
  waiting for transfers between devices  90.1 us (30%)
  local copies, waits for them, and re-layouts  37.5 us (12%)
  other arithmetic  26 us (9%)
  matrix products  16.1 us (5%)
    ppermute x24, starting transfers between devices, exchanged(): return lax.ppermute(array, axis, [(i, i ^ mask) for i in range(length)])  116 us
    ppermute x24, waiting for transfers between devices, exchanged(): return lax.ppermute(array, axis, [(i, i ^ mask) for i in range(length)])  82.9 us
    ppermute x2, starting transfers between devices, passed_along(): return lax.ppermute(array, axis, pairs)  10.5 us
    ppermute x2, waiting for transfers between devices, passed_along(): return lax.ppermute(array, axis, pairs)  7.18 us
    reshape x2, local copies, waits for them, and re-layouts, mix_heads(): return result.reshape(tokens, head_count * head_width)  6.07 us
  transfers between devices with their start and end apart: 26, of which 20 were waited for; matrix products, arithmetic and copies ran while one was open for 7% of the time, Pallas kernels for 0%

profile of v6, /device:TPU:6, one launch (start us, length us, event | category | flops | bytes accessed | tf_op | source)
XLA Modules:
  0.0 298.6 jit_solution(4416064303695104986)
XLA Ops:
  5.3 9.1 %collective-permute-start = (bf16[24,176]{1,0:T(8,128)(2,1)S(1)}, bf16[24,176]{1,0:T(8,128)(2,1)S(1)}, u32[]{:S(2)}, u32[]{:S(2)}) collective-permute-start(bf16[24,176]{1,0:T(8,128)(2,1)S(1)} %concatenate.21), channel_id=1, source_target_pairs={{0,1},{1,0},{2,3},{3,2},{4,5},{5,4},{6,7},{7,6},{8,9},{9,8},{10,11... | collective-permute-start | bytes 25352 | tf_op jit(solution)/shard_map/ppermute | solution.py:108
  16.1 14.5 %collective-permute-start.1 = (bf16[2,24,176]{2,1,0:T(8,128)(2,1)S(1)}, bf16[2,24,176]{2,1,0:T(8,128)(2,1)S(1)}, u32[]{:S(2)}, u32[]{:S(2)}) collective-permute-start(bf16[2,24,176]{2,1,0:T(8,128)(2,1)S(1)} %get-tuple-element.66), channel_id=1, source_target_pairs={{0,2},{1,3},{2,0},{3,1},{4,6},{5,7},{6,4},{7,5},{8,10},{9,11},{10,... | collective-permute-start | bytes 50696 | tf_op jit(solution)/shard_map/ppermute | solution.py:108
  32.5 2.7 collective-permute-start.2
  35.2 3.2 %collective-permute-done.2 = bf16[2,2,24,176]{3,2,1,0:T(8,128)(2,1)S(1)} collective-permute-done((bf16[2,2,24,176]{3,2,1,0:T(8,128)(2,1)S(1)}, bf16[2,2,24,176]{3,2,1,0:T(8,128)(2,1)S(1)}, u32[]{:S(2)}, u32[]{:S(2)}) %collective-permute-start.2) | collective-permute-done | bytes 33824 | tf_op jit(solution)/shard_map/ppermute | solution.py:108
  38.5 4.2 %collective-permute-start.3 = (bf16[2,2,2,24,176]{4,3,2,1,0:T(8,128)(2,1)S(1)}, bf16[2,2,2,24,176]{4,3,2,1,0:T(8,128)(2,1)S(1)}, u32[]{:S(2)}, u32[]{:S(2)}) collective-permute-start(bf16[2,2,2,24,176]{4,3,2,1,0:T(8,128)(2,1)S(1)} %get-tuple-element.52), channel_id=1, source_target_pairs={{0,8},{1,9},{2,10},{3,11},{4,12},{5,13},{6,14},{7,15},{8,0},{9,1},... | collective-permute-start | bytes 202760 | tf_op jit(solution)/shard_map/ppermute | solution.py:108
  42.8 3.8 %collective-permute-done.3 = bf16[2,2,2,24,176]{4,3,2,1,0:T(8,128)(2,1)S(1)} collective-permute-done((bf16[2,2,2,24,176]{4,3,2,1,0:T(8,128)(2,1)S(1)}, bf16[2,2,2,24,176]{4,3,2,1,0:T(8,128)(2,1)S(1)}, u32[]{:S(2)}, u32[]{:S(2)}) %collective-permute-start.3) | collective-permute-done | bytes 67616 | tf_op jit(solution)/shard_map/ppermute | solution.py:108
  47.1 5.1 %collective-permute-start.4 = (bf16[11,16,256]{2,0,1:T(8,128)(2,1)S(1)}, bf16[11,16,256]{2,0,1:T(8,128)(2,1)S(1)}, u32[]{:S(2)}, u32[]{:S(2)}) collective-permute-start(bf16[11,16,256]{2,0,1:T(8,128)(2,1)S(1)} %bitcast.199), channel_id=1, source_target_pairs={{0,256},{16,272},{32,288},{48,304},{64,320},{80,336},{96,352},{112... | collective-permute-start | bytes 270344 | tf_op jit(solution)/shard_map/ppermute | solution.py:108
  52.2 3.2 %collective-permute-done.4 = bf16[11,16,256]{2,0,1:T(8,128)(2,1)S(1)} collective-permute-done((bf16[11,16,256]{2,0,1:T(8,128)(2,1)S(1)}, bf16[11,16,256]{2,0,1:T(8,128)(2,1)S(1)}, u32[]{:S(2)}, u32[]{:S(2)}) %collective-permute-start.4) | collective-permute-done | bytes 90144 | tf_op jit(solution)/shard_map/ppermute | solution.py:108
  55.6 3.4 %collective-permute-start.5 = (bf16[2,11,16,256]{3,1,2,0:T(8,128)(2,1)S(1)}, bf16[2,11,16,256]{3,1,2,0:T(8,128)(2,1)S(1)}, u32[]{:S(2)}, u32[]{:S(2)}) collective-permute-start(bf16[2,11,16,256]{3,1,2,0:T(8,128)(2,1)S(1)} %get-tuple-element.45), channel_id=1, source_target_pairs={{0,64},{16,80},{32,96},{48,112},{64,0},{80,16},{96,32},{112,48},{1... | collective-permute-start | bytes 540680 | tf_op jit(solution)/shard_map/ppermute | solution.py:108
  59.0 8.5 %collective-permute-done.5 = bf16[2,11,16,256]{3,1,2,0:T(8,128)(2,1)S(1)} collective-permute-done((bf16[2,11,16,256]{3,1,2,0:T(8,128)(2,1)S(1)}, bf16[2,11,16,256]{3,1,2,0:T(8,128)(2,1)S(1)}, u32[]{:S(2)}, u32[]{:S(2)}) %collective-permute-start.5) | collective-permute-done | bytes 180256 | tf_op jit(solution)/shard_map/ppermute | solution.py:108
  68.0 3.5 %collective-permute-start.6 = (bf16[2,2,11,16,256]{4,3,2,0,1:T(8,128)(2,1)S(1)}, bf16[2,2,11,16,256]{4,3,2,0,1:T(8,128)(2,1)S(1)}, u32[]{:S(2)}, u32[]{:S(2)}) collective-permute-start(bf16[2,2,11,16,256]{4,3,2,0,1:T(8,128)(2,1)S(1)} %get-tuple-element.43), channel_id=1, source_target_pairs={{0,128},{16,144},{32,160},{48,176},{64,192},{80,208},{96,224},{112... | collective-permute-start | bytes 1081352 | tf_op jit(solution)/shard_map/ppermute | solution.py:108
  71.5 5.8 %collective-permute-done.6 = bf16[2,2,11,16,256]{4,3,2,0,1:T(8,128)(2,1)S(1)} collective-permute-done((bf16[2,2,11,16,256]{4,3,2,0,1:T(8,128)(2,1)S(1)}, bf16[2,2,11,16,256]{4,3,2,0,1:T(8,128)(2,1)S(1)}, u32[]{:S(2)}, u32[]{:S(2)}) %collective-permute-start.6) | collective-permute-done | bytes 360480 | tf_op jit(solution)/shard_map/ppermute | solution.py:108
  80.5 7.4 %collective-permute-start.9 = (bf16[3,2816]{1,0:T(4,128)(2,1)S(1)}, bf16[3,2816]{1,0:T(4,128)(2,1)S(1)}, u32[]{:S(2)}, u32[]{:S(2)}) collective-permute-start(bf16[3,2816]{1,0:T(4,128)(2,1)S(1)} %slice_bitcast_fusion.2), channel_id=1, source_target_pairs={{0,1},{1,2},{2,3},{3,4},{4,5},{5,6},{6,7},{7,8},{8,9},{9,10},{10,1... | collective-permute-start | bytes 50696 | tf_op jit(solution)/shard_map/ppermute | solution.py:13
  87.9 3.0 %collective-permute-done.7 = bf16[2,2,2,11,16,256]{5,4,3,1,0,2:T(8,128)(2,1)S(1)} collective-permute-done((bf16[2,2,2,11,16,256]{5,4,3,1,0,2:T(8,128)(2,1)S(1)}, bf16[2,2,2,11,16,256]{5,4,3,1,0,2:T(8,128)(2,1)S(1)}, u32[]{:S(2)}, u32[]{:S(2)}) %collective-permute-start.7) | collective-permute-done | bytes 720928 | tf_op jit(solution)/shard_map/ppermute | solution.py:108
  95.1 2.9 collective-permute-done.9
  109.2 3.0 copy.124
  112.1 2.8 fusion.28
  115.0 3.1 %copy.128 = f32[128,2816]{1,0:T(8,128)} copy(f32[128,2816]{0,1:T(8,128)} %bitcast.182) | data formatting | bytes 2883584 | tf_op jit(solution)/shard_map/reshape | solution.py:21
  119.6 2.8 convolution_multiply_fusion
  124.8 3.5 %collective-permute-start.10 = (f32[3,2816]{1,0:T(4,128)S(1)}, f32[3,2816]{1,0:T(4,128)S(1)}, u32[]{:S(2)}, u32[]{:S(2)}) collective-permute-start(f32[3,2816]{1,0:T(4,128)S(1)} %pad_maximum_fusion.9), channel_id=1, source_target_pairs={{0,1},{1,0},{2,3},{3,2},{4,5},{5,4},{6,7},{7,6},{8,9},{9,8},{10,11... | collective-permute-start | bytes 101384 | tf_op jit(solution)/shard_map/ppermute | solution.py:108
  128.3 6.6 %collective-permute-done.10 = f32[3,2816]{1,0:T(4,128)S(1)} collective-permute-done((f32[3,2816]{1,0:T(4,128)S(1)}, f32[3,2816]{1,0:T(4,128)S(1)}, u32[]{:S(2)}, u32[]{:S(2)}) %collective-permute-start.10) | collective-permute-done | bytes 33824 | tf_op jit(solution)/shard_map/ppermute | solution.py:108
  136.0 12.1 %collective-permute-start.11 = (f32[3,2816]{1,0:T(4,128)S(1)}, f32[3,2816]{1,0:T(4,128)S(1)}, u32[]{:S(2)}, u32[]{:S(2)}) collective-permute-start(f32[3,2816]{1,0:T(4,128)S(1)} %pad_maximum_fusion.10), channel_id=1, source_target_pairs={{0,2},{1,3},{2,0},{3,1},{4,6},{5,7},{6,4},{7,5},{8,10},{9,11},{10,... | collective-permute-start | bytes 101384 | tf_op jit(solution)/shard_map/ppermute | solution.py:108
  148.1 2.5 collective-permute-done.11
  150.7 2.7 collective-permute-start.12
  153.5 3.2 %collective-permute-done.12 = f32[3,2816]{1,0:T(4,128)S(1)} collective-permute-done((f32[3,2816]{1,0:T(4,128)S(1)}, f32[3,2816]{1,0:T(4,128)S(1)}, u32[]{:S(2)}, u32[]{:S(2)}) %collective-permute-start.12) | collective-permute-done | bytes 33824 | tf_op jit(solution)/shard_map/ppermute | solution.py:108
  156.8 3.5 %collective-permute-start.13 = (f32[3,2816]{1,0:T(4,128)S(1)}, f32[3,2816]{1,0:T(4,128)S(1)}, u32[]{:S(2)}, u32[]{:S(2)}) collective-permute-start(f32[3,2816]{1,0:T(4,128)S(1)} %pad_maximum_fusion.12), channel_id=1, source_target_pairs={{0,8},{1,9},{2,10},{3,11},{4,12},{5,13},{6,14},{7,15},{8,0},{9,1},... | collective-permute-start | bytes 101384 | tf_op jit(solution)/shard_map/ppermute | solution.py:108
  160.3 3.9 %collective-permute-done.13 = f32[3,2816]{1,0:T(4,128)S(1)} collective-permute-done((f32[3,2816]{1,0:T(4,128)S(1)}, f32[3,2816]{1,0:T(4,128)S(1)}, u32[]{:S(2)}, u32[]{:S(2)}) %collective-permute-start.13) | collective-permute-done | bytes 33824 | tf_op jit(solution)/shard_map/ppermute | solution.py:108
  167.5 4.6 %multiply_reduce_fusion = (f32[2816]{0:T(1024)S(1)}, f32[128,2816]{1,0:T(8,128)S(1)}, bf16[128,2816]{1,0:T(8,128)(2,1)}, f32[128,2816]{1,0:T(8,128)}) fusion(f32[128,2816]{1,0:T(8,128)S(1)} %copy-done.4, f32[2816]{0:T(1024)S(1)} %add.376, f32[128,2816]{1,0:T(8,128)S(1)} %copy-done.6, f32[2816]{0:T(1024)S(1)} %add.380, f32[2816]{0:T(1024)S(1)} %mul.333, ...), kind=kLoop, calls=%fused_computation.69 | loop fusion | flops 17659136 | bytes 16704512 | tf_op jit(solution)/shard_map/reduce_sum | solution.py:270
  175.6 3.4 %copy.136 = f32[256,11,256]{2,1,0:T(8,128)} copy(f32[256,11,256]{0,2,1:T(8,128)S(1)} %convolution_bitcast_fusion) | data formatting | bytes 5767168 | tf_op jit(solution)/shard_map/thk,thj->khj/transpose | solution.py:37
  179.0 4.7 %concatenate.25 = f32[2,2,2,2,2,8,2816]{6,5,4,3,2,1,0:T(8,128)} reshape(f32[256,11,256]{2,1,0:T(8,128)} %copy.136) | data formatting | bytes 5767168 | tf_op jit(solution)/shard_map/concatenate | solution.py:185
  189.1 3.8 %collective-permute-done.15 = f32[16,8,3168]{2,1,0:T(8,128)} collective-permute-done((f32[16,8,3168]{2,1,0:T(8,128)}, f32[16,8,3168]{2,1,0:T(8,128)}, u32[]{:S(2)}, u32[]{:S(2)}) %collective-permute-start.15) | collective-permute-done | bytes 1622048 | tf_op jit(solution)/shard_map/ppermute | solution.py:108
  196.6 3.5 %collective-permute-start.17 = (f32[4,8,3168]{2,1,0:T(8,128)S(1)}, f32[4,8,3168]{2,1,0:T(8,128)}, u32[]{:S(2)}, u32[]{:S(2)}) collective-permute-start(f32[4,8,3168]{2,1,0:T(8,128)S(1)} %get-tuple-element.25), channel_id=1, source_target_pairs={{0,128},{16,144},{32,160},{48,176},{64,192},{80,208},{96,224},{112... | collective-permute-start | bytes 1216520 | tf_op jit(solution)/shard_map/ppermute | solution.py:108
  200.1 3.8 %collective-permute-start.18 = (f32[4,8,3168]{2,1,0:T(8,128)S(1)}, f32[4,8,3168]{2,1,0:T(8,128)}, u32[]{:S(2)}, u32[]{:S(2)}) collective-permute-start(f32[4,8,3168]{2,1,0:T(8,128)S(1)} %get-tuple-element.24), channel_id=1, source_target_pairs={{0,160},{16,176},{32,128},{48,144},{64,224},{80,240},{96,192},{112... | collective-permute-start | bytes 1216520 | tf_op jit(solution)/shard_map/ppermute | solution.py:108
  204.0 4.9 %collective-permute-done.16 = f32[4,8,3168]{2,1,0:T(8,128)S(1)} collective-permute-done((f32[4,8,3168]{2,1,0:T(8,128)S(1)}, f32[4,8,3168]{2,1,0:T(8,128)S(1)}, u32[]{:S(2)}, u32[]{:S(2)}) %collective-permute-start.16) | collective-permute-done | bytes 405536 | tf_op jit(solution)/shard_map/ppermute | solution.py:108
  208.9 10.0 %collective-permute-done.17 = f32[4,8,3168]{2,1,0:T(8,128)} collective-permute-done((f32[4,8,3168]{2,1,0:T(8,128)S(1)}, f32[4,8,3168]{2,1,0:T(8,128)}, u32[]{:S(2)}, u32[]{:S(2)}) %collective-permute-start.17) | collective-permute-done | bytes 405536 | tf_op jit(solution)/shard_map/ppermute | solution.py:108
  220.2 4.0 %collective-permute-start.19 = (f32[1,8,3168]{2,1,0:T(8,128)S(1)}, f32[1,8,3168]{2,1,0:T(8,128)S(1)}, u32[]{:S(2)}, u32[]{:S(2)}) collective-permute-start(f32[1,8,3168]{2,1,0:T(8,128)S(1)} %get-tuple-element.40), channel_id=1, source_target_pairs={{0,64},{16,80},{32,96},{48,112},{64,0},{80,16},{96,32},{112,48},{1... | collective-permute-start | bytes 304136 | tf_op jit(solution)/shard_map/ppermute | solution.py:108
  224.3 5.1 %collective-permute-start.20 = (f32[1,8,3168]{2,1,0:T(8,128)S(1)}, f32[1,8,3168]{2,1,0:T(8,128)S(1)}, u32[]{:S(2)}, u32[]{:S(2)}) collective-permute-start(f32[1,8,3168]{2,1,0:T(8,128)S(1)} %get-tuple-element.42), channel_id=1, source_target_pairs={{0,256},{16,272},{32,288},{48,304},{64,320},{80,336},{96,352},{112... | collective-permute-start | bytes 304136 | tf_op jit(solution)/shard_map/ppermute | solution.py:108
  229.4 2.6 collective-permute-start.21
  232.3 6.9 %collective-permute-done.21 = f32[1,8,3168]{2,1,0:T(8,128)S(1)} collective-permute-done((f32[1,8,3168]{2,1,0:T(8,128)S(1)}, f32[1,8,3168]{2,1,0:T(8,128)S(1)}, u32[]{:S(2)}, u32[]{:S(2)}) %collective-permute-start.21) | collective-permute-done | bytes 101408 | tf_op jit(solution)/shard_map/ppermute | solution.py:108
  239.7 8.2 %collective-permute-start.22 = (f32[8,8,528]{2,1,0:T(8,128)S(1)}, f32[8,8,528]{2,1,0:T(8,128)}, u32[]{:S(2)}, u32[]{:S(2)}) collective-permute-start(f32[8,8,528]{2,1,0:T(8,128)S(1)} %dynamic-slice_bitcast_fusion.4), channel_id=1, source_target_pairs={{0,1},{1,0},{2,3},{3,2},{4,5},{5,4},{6,7},{7,6},{8,9},{9,8},{10,11... | collective-permute-start | bytes 405512 | tf_op jit(solution)/shard_map/ppermute | solution.py:108
  250.7 9.8 %collective-permute-done.22 = f32[8,8,528]{2,1,0:T(8,128)} collective-permute-done((f32[8,8,528]{2,1,0:T(8,128)S(1)}, f32[8,8,528]{2,1,0:T(8,128)}, u32[]{:S(2)}, u32[]{:S(2)}) %collective-permute-start.22) | collective-permute-done | bytes 135200 | tf_op jit(solution)/shard_map/ppermute | solution.py:108
  261.4 11.0 %collective-permute-start.23 = (f32[4,8,528]{2,1,0:T(8,128)S(1)}, f32[4,8,528]{2,1,0:T(8,128)S(1)}, u32[]{:S(2)}, u32[]{:S(2)}) collective-permute-start(f32[4,8,528]{2,1,0:T(8,128)S(1)} %dynamic-slice_bitcast_fusion.5), channel_id=1, source_target_pairs={{0,2},{1,3},{2,0},{3,1},{4,6},{5,7},{6,4},{7,5},{8,10},{9,11},{10,... | collective-permute-start | bytes 202760 | tf_op jit(solution)/shard_map/ppermute | solution.py:108
  272.5 2.9 fusion.26
  276.9 3.0 %copy.134 = f32[128,2816]{1,0:T(8,128)} copy(f32[128,2816]{0,1:T(8,128)} %bitcast.180) | data formatting | bytes 2883584 | tf_op jit(solution)/shard_map/reshape | solution.py:29
  280.0 3.0 %collective-permute-start.24 = (f32[2,8,528]{2,1,0:T(8,128)S(1)}, f32[2,8,528]{2,1,0:T(8,128)S(1)}, u32[]{:S(2)}, u32[]{:S(2)}) collective-permute-start(f32[2,8,528]{2,1,0:T(8,128)S(1)} %dynamic-slice_bitcast_fusion.6), channel_id=1, source_target_pairs={{0,4},{1,5},{2,6},{3,7},{4,0},{5,1},{6,2},{7,3},{8,12},{9,13},{10,... | collective-permute-start | bytes 101384 | tf_op jit(solution)/shard_map/ppermute | solution.py:108
  285.3 3.1 %collective-permute-start.14 = (f32[3,2816]{1,0:T(4,128)S(1)}, f32[3,2816]{1,0:T(4,128)S(1)}, u32[]{:S(2)}, u32[]{:S(2)}) collective-permute-start(f32[3,2816]{1,0:T(4,128)S(1)} %slice.215), channel_id=1, source_target_pairs={{1,0},{2,1},{3,2},{4,3},{5,4},{6,5},{7,6},{8,7},{9,8},{10,9},{11,1... | collective-permute-start | bytes 101384 | tf_op jit(solution)/shard_map/ppermute | solution.py:13
  288.5 3.0 collective-permute-start.25
  291.4 4.2 %collective-permute-done.14 = f32[3,2816]{1,0:T(4,128)S(1)} collective-permute-done((f32[3,2816]{1,0:T(4,128)S(1)}, f32[3,2816]{1,0:T(4,128)S(1)}, u32[]{:S(2)}, u32[]{:S(2)}) %collective-permute-start.14) | collective-permute-done | bytes 33824 | tf_op jit(solution)/shard_map/ppermute | solution.py:13
  (158 shorter events, 60.9 us)
Async XLA Ops:
  5.3 10.8 %collective-permute-start = (bf16[24,176]{1,0:T(8,128)(2,1)S(1)}, bf16[24,176]{1,0:T(8,128)(2,1)S(1)}, u32[]{:S(2)}, u32[]{:S(2)}) collective-permute-start(bf16[24,176]{1,0:T(8,128)(2,1)S(1)} %concatenate.21), channel_id=1, source_target_pairs={{0,1},{1,0},{2,3},{3,2},{4,5},{5,4},{6,7},{7,6},{8,9},{9,8},{10,11... | collective-permute-start | bytes 25352 | tf_op jit(solution)/shard_map/ppermute | solution.py:108
  16.1 16.3 %collective-permute-start.1 = (bf16[2,24,176]{2,1,0:T(8,128)(2,1)S(1)}, bf16[2,24,176]{2,1,0:T(8,128)(2,1)S(1)}, u32[]{:S(2)}, u32[]{:S(2)}) collective-permute-start(bf16[2,24,176]{2,1,0:T(8,128)(2,1)S(1)} %get-tuple-element.66), channel_id=1, source_target_pairs={{0,2},{1,3},{2,0},{3,1},{4,6},{5,7},{6,4},{7,5},{8,10},{9,11},{10,... | collective-permute-start | bytes 50696 | tf_op jit(solution)/shard_map/ppermute | solution.py:108
  32.5 6.0 %collective-permute-start.2 = (bf16[2,2,24,176]{3,2,1,0:T(8,128)(2,1)S(1)}, bf16[2,2,24,176]{3,2,1,0:T(8,128)(2,1)S(1)}, u32[]{:S(2)}, u32[]{:S(2)}) collective-permute-start(bf16[2,2,24,176]{3,2,1,0:T(8,128)(2,1)S(1)} %get-tuple-element.62), channel_id=1, source_target_pairs={{0,4},{1,5},{2,6},{3,7},{4,0},{5,1},{6,2},{7,3},{8,12},{9,13},{10,... | collective-permute-start | bytes 101384 | tf_op jit(solution)/shard_map/ppermute | solution.py:108
  38.5 8.0 %collective-permute-start.3 = (bf16[2,2,2,24,176]{4,3,2,1,0:T(8,128)(2,1)S(1)}, bf16[2,2,2,24,176]{4,3,2,1,0:T(8,128)(2,1)S(1)}, u32[]{:S(2)}, u32[]{:S(2)}) collective-permute-start(bf16[2,2,2,24,176]{4,3,2,1,0:T(8,128)(2,1)S(1)} %get-tuple-element.52), channel_id=1, source_target_pairs={{0,8},{1,9},{2,10},{3,11},{4,12},{5,13},{6,14},{7,15},{8,0},{9,1},... | collective-permute-start | bytes 202760 | tf_op jit(solution)/shard_map/ppermute | solution.py:108
  47.1 8.4 %collective-permute-start.4 = (bf16[11,16,256]{2,0,1:T(8,128)(2,1)S(1)}, bf16[11,16,256]{2,0,1:T(8,128)(2,1)S(1)}, u32[]{:S(2)}, u32[]{:S(2)}) collective-permute-start(bf16[11,16,256]{2,0,1:T(8,128)(2,1)S(1)} %bitcast.199), channel_id=1, source_target_pairs={{0,256},{16,272},{32,288},{48,304},{64,320},{80,336},{96,352},{112... | collective-permute-start | bytes 270344 | tf_op jit(solution)/shard_map/ppermute | solution.py:108
  55.6 12.0 %collective-permute-start.5 = (bf16[2,11,16,256]{3,1,2,0:T(8,128)(2,1)S(1)}, bf16[2,11,16,256]{3,1,2,0:T(8,128)(2,1)S(1)}, u32[]{:S(2)}, u32[]{:S(2)}) collective-permute-start(bf16[2,11,16,256]{3,1,2,0:T(8,128)(2,1)S(1)} %get-tuple-element.45), channel_id=1, source_target_pairs={{0,64},{16,80},{32,96},{48,112},{64,0},{80,16},{96,32},{112,48},{1... | collective-permute-start | bytes 540680 | tf_op jit(solution)/shard_map/ppermute | solution.py:108
  68.0 9.3 %collective-permute-start.6 = (bf16[2,2,11,16,256]{4,3,2,0,1:T(8,128)(2,1)S(1)}, bf16[2,2,11,16,256]{4,3,2,0,1:T(8,128)(2,1)S(1)}, u32[]{:S(2)}, u32[]{:S(2)}) collective-permute-start(bf16[2,2,11,16,256]{4,3,2,0,1:T(8,128)(2,1)S(1)} %get-tuple-element.43), channel_id=1, source_target_pairs={{0,128},{16,144},{32,160},{48,176},{64,192},{80,208},{96,224},{112... | collective-permute-start | bytes 1081352 | tf_op jit(solution)/shard_map/ppermute | solution.py:108
  77.7 13.2 %collective-permute-start.7 = (bf16[2,2,2,11,16,256]{5,4,3,1,0,2:T(8,128)(2,1)S(1)}, bf16[2,2,2,11,16,256]{5,4,3,1,0,2:T(8,128)(2,1)S(1)}, u32[]{:S(2)}, u32[]{:S(2)}) collective-permute-start(bf16[2,2,2,11,16,256]{5,4,3,1,0,2:T(8,128)(2,1)S(1)} %get-tuple-element.34), channel_id=1, source_target_pairs={{0,32},{16,48},{32,0},{48,16},{64,96},{80,112},{96,64},{112,80},{1... | collective-permute-start | bytes 2162696 | tf_op jit(solution)/shard_map/ppermute | solution.py:108
  80.5 17.5 %collective-permute-start.9 = (bf16[3,2816]{1,0:T(4,128)(2,1)S(1)}, bf16[3,2816]{1,0:T(4,128)(2,1)S(1)}, u32[]{:S(2)}, u32[]{:S(2)}) collective-permute-start(bf16[3,2816]{1,0:T(4,128)(2,1)S(1)} %slice_bitcast_fusion.2), channel_id=1, source_target_pairs={{0,1},{1,2},{2,3},{3,4},{4,5},{5,6},{6,7},{7,8},{8,9},{9,10},{10,1... | collective-permute-start | bytes 50696 | tf_op jit(solution)/shard_map/ppermute | solution.py:13
  91.6 6.4 %copy-start.20 = (bf16[1,128,2816]{2,1,0:T(8,128)(2,1)S(1)}, bf16[1,128,2816]{2,1,0:T(8,128)(2,1)}, u32[]{:S(2)}) copy-start(bf16[1,128,2816]{2,1,0:T(8,128)(2,1)} %param.9) | copy-start | bytes 2162692
  93.0 10.1 %collective-permute-start.8 = (bf16[2,2,2,2,11,16,256]{6,5,4,2,1,0,3:T(8,128)(2,1)}, bf16[2,2,2,2,11,16,256]{6,5,4,2,1,0,3:T(8,128)(2,1)}, u32[]{:S(2)}, u32[]{:S(2)}) collective-permute-start(bf16[2,2,2,2,11,16,256]{6,5,4,2,1,0,3:T(8,128)(2,1)} %get-tuple-element.30), channel_id=1, source_target_pairs={{0,16},{16,0},{32,48},{48,32},{64,80},{80,64},{96,112},{112,96},{1... | collective-permute-start | bytes 4325384 | tf_op jit(solution)/shard_map/ppermute | solution.py:108
  106.3 1.1 copy-start.8
  106.5 2.6 copy-start.2
  106.6 5.6 %copy-start = (bf16[11,32,8,256]{3,2,0,1:T(8,128)(2,1)}, bf16[11,32,8,256]{3,2,0,1:T(8,128)(2,1)S(1)}, u32[]{:S(2)}) copy-start(bf16[11,32,8,256]{3,2,0,1:T(8,128)(2,1)S(1)} %get-tuple-element.20) | copy-start | bytes 4325380
  115.0 3.1 %copy-start.4 = (f32[128,2816]{1,0:T(8,128)S(1)}, f32[128,2816]{1,0:T(8,128)}, u32[]{:S(2)}) copy-start(f32[128,2816]{1,0:T(8,128)} %copy.124) | copy-start | bytes 4325380
  118.1 1.4 copy-start.5
  118.1 1.5 copy-start.17
  119.4 3.0 %copy-start.13 = (f32[128,2816]{1,0:T(8,128)}, f32[128,2816]{1,0:T(8,128)S(1)}, u32[]{:S(2)}) copy-start(f32[128,2816]{1,0:T(8,128)S(1)} %get-tuple-element.71) | copy-start | bytes 4325380
  119.4 5.3 %copy-start.19 = (f32[128,2816]{1,0:T(8,128)}, f32[128,2816]{1,0:T(8,128)S(1)}, u32[]{:S(2)}) copy-start(f32[128,2816]{1,0:T(8,128)S(1)} %get-tuple-element.70) | copy-start | bytes 4325380
  119.6 2.8 copy-start.21
  122.4 1.2 copy-start.18
  123.6 1.1 copy-start.10
  124.8 10.1 %collective-permute-start.10 = (f32[3,2816]{1,0:T(4,128)S(1)}, f32[3,2816]{1,0:T(4,128)S(1)}, u32[]{:S(2)}, u32[]{:S(2)}) collective-permute-start(f32[3,2816]{1,0:T(4,128)S(1)} %pad_maximum_fusion.9), channel_id=1, source_target_pairs={{0,1},{1,0},{2,3},{3,2},{4,5},{5,4},{6,7},{7,6},{8,9},{9,8},{10,11... | collective-permute-start | bytes 101384 | tf_op jit(solution)/shard_map/ppermute | solution.py:108
  136.0 14.7 %collective-permute-start.11 = (f32[3,2816]{1,0:T(4,128)S(1)}, f32[3,2816]{1,0:T(4,128)S(1)}, u32[]{:S(2)}, u32[]{:S(2)}) collective-permute-start(f32[3,2816]{1,0:T(4,128)S(1)} %pad_maximum_fusion.10), channel_id=1, source_target_pairs={{0,2},{1,3},{2,0},{3,1},{4,6},{5,7},{6,4},{7,5},{8,10},{9,11},{10,... | collective-permute-start | bytes 101384 | tf_op jit(solution)/shard_map/ppermute | solution.py:108
  150.7 5.9 %collective-permute-start.12 = (f32[3,2816]{1,0:T(4,128)S(1)}, f32[3,2816]{1,0:T(4,128)S(1)}, u32[]{:S(2)}, u32[]{:S(2)}) collective-permute-start(f32[3,2816]{1,0:T(4,128)S(1)} %pad_maximum_fusion.11), channel_id=1, source_target_pairs={{0,4},{1,5},{2,6},{3,7},{4,0},{5,1},{6,2},{7,3},{8,12},{9,13},{10,... | collective-permute-start | bytes 101384 | tf_op jit(solution)/shard_map/ppermute | solution.py:108
  156.8 7.4 %collective-permute-start.13 = (f32[3,2816]{1,0:T(4,128)S(1)}, f32[3,2816]{1,0:T(4,128)S(1)}, u32[]{:S(2)}, u32[]{:S(2)}) collective-permute-start(f32[3,2816]{1,0:T(4,128)S(1)} %pad_maximum_fusion.12), channel_id=1, source_target_pairs={{0,8},{1,9},{2,10},{3,11},{4,12},{5,13},{6,14},{7,15},{8,0},{9,1},... | collective-permute-start | bytes 101384 | tf_op jit(solution)/shard_map/ppermute | solution.py:108
  164.4 2.2 copy-start.6
  164.4 2.7 copy-start.11
  164.4 3.1 %copy-start.14 = (f32[128,2816]{1,0:T(8,128)S(1)}, f32[128,2816]{1,0:T(8,128)}, u32[]{:S(2)}) copy-start(f32[128,2816]{1,0:T(8,128)} %copy-done.13) | copy-start | bytes 4325380
  187.2 5.7 %collective-permute-start.15 = (f32[16,8,3168]{2,1,0:T(8,128)}, f32[16,8,3168]{2,1,0:T(8,128)}, u32[]{:S(2)}, u32[]{:S(2)}) collective-permute-start(f32[16,8,3168]{2,1,0:T(8,128)} %dynamic-slice_bitcast_fusion), channel_id=1, source_target_pairs={{0,16},{16,0},{32,48},{48,32},{64,80},{80,64},{96,112},{112,96},{1... | collective-permute-start | bytes 4866056 | tf_op jit(solution)/shard_map/ppermute | solution.py:108
  194.7 14.2 %collective-permute-start.16 = (f32[4,8,3168]{2,1,0:T(8,128)S(1)}, f32[4,8,3168]{2,1,0:T(8,128)S(1)}, u32[]{:S(2)}, u32[]{:S(2)}) collective-permute-start(f32[4,8,3168]{2,1,0:T(8,128)S(1)} %get-tuple-element.23), channel_id=1, source_target_pairs={{0,32},{16,48},{32,0},{48,16},{64,96},{80,112},{96,64},{112,80},{1... | collective-permute-start | bytes 1216520 | tf_op jit(solution)/shard_map/ppermute | solution.py:108
  196.6 22.3 %collective-permute-start.17 = (f32[4,8,3168]{2,1,0:T(8,128)S(1)}, f32[4,8,3168]{2,1,0:T(8,128)}, u32[]{:S(2)}, u32[]{:S(2)}) collective-permute-start(f32[4,8,3168]{2,1,0:T(8,128)S(1)} %get-tuple-element.25), channel_id=1, source_target_pairs={{0,128},{16,144},{32,160},{48,176},{64,192},{80,208},{96,224},{112... | collective-permute-start | bytes 1216520 | tf_op jit(solution)/shard_map/ppermute | solution.py:108
  200.1 18.8 %collective-permute-start.18 = (f32[4,8,3168]{2,1,0:T(8,128)S(1)}, f32[4,8,3168]{2,1,0:T(8,128)}, u32[]{:S(2)}, u32[]{:S(2)}) collective-permute-start(f32[4,8,3168]{2,1,0:T(8,128)S(1)} %get-tuple-element.24), channel_id=1, source_target_pairs={{0,160},{16,176},{32,128},{48,144},{64,224},{80,240},{96,192},{112... | collective-permute-start | bytes 1216520 | tf_op jit(solution)/shard_map/ppermute | solution.py:108
  220.2 27.7 %copy-start.3 = (bf16[11,32,8,256]{3,2,0,1:T(8,128)(2,1)S(1)}, bf16[11,32,8,256]{3,2,0,1:T(8,128)(2,1)}, u32[]{:S(2)}) copy-start(bf16[11,32,8,256]{3,2,0,1:T(8,128)(2,1)} %copy-done.2) | copy-start | bytes 4325380
  220.2 27.7 %copy-start.9 = (bf16[128,2816]{0,1:T(8,128)(2,1)S(1)}, bf16[128,2816]{0,1:T(8,128)(2,1)}, u32[]{:S(2)}) copy-start(bf16[128,2816]{0,1:T(8,128)(2,1)} %copy.129) | copy-start | bytes 2162692
  220.2 11.8 %collective-permute-start.19 = (f32[1,8,3168]{2,1,0:T(8,128)S(1)}, f32[1,8,3168]{2,1,0:T(8,128)S(1)}, u32[]{:S(2)}, u32[]{:S(2)}) collective-permute-start(f32[1,8,3168]{2,1,0:T(8,128)S(1)} %get-tuple-element.40), channel_id=1, source_target_pairs={{0,64},{16,80},{32,96},{48,112},{64,0},{80,16},{96,32},{112,48},{1... | collective-permute-start | bytes 304136 | tf_op jit(solution)/shard_map/ppermute | solution.py:108
  224.3 8.1 %collective-permute-start.20 = (f32[1,8,3168]{2,1,0:T(8,128)S(1)}, f32[1,8,3168]{2,1,0:T(8,128)S(1)}, u32[]{:S(2)}, u32[]{:S(2)}) collective-permute-start(f32[1,8,3168]{2,1,0:T(8,128)S(1)} %get-tuple-element.42), channel_id=1, source_target_pairs={{0,256},{16,272},{32,288},{48,304},{64,320},{80,336},{96,352},{112... | collective-permute-start | bytes 304136 | tf_op jit(solution)/shard_map/ppermute | solution.py:108
  229.4 9.9 %collective-permute-start.21 = (f32[1,8,3168]{2,1,0:T(8,128)S(1)}, f32[1,8,3168]{2,1,0:T(8,128)S(1)}, u32[]{:S(2)}, u32[]{:S(2)}) collective-permute-start(f32[1,8,3168]{2,1,0:T(8,128)S(1)} %get-tuple-element.41), channel_id=1, source_target_pairs={{0,320},{16,336},{32,352},{48,368},{64,256},{80,272},{96,288},{112... | collective-permute-start | bytes 304136 | tf_op jit(solution)/shard_map/ppermute | solution.py:108
  239.7 9.9 %copy-start.16 = (bf16[128,2816]{1,0:T(8,128)(2,1)S(1)}, bf16[128,2816]{1,0:T(8,128)(2,1)}, u32[]{:S(2)}) copy-start(bf16[128,2816]{1,0:T(8,128)(2,1)} %get-tuple-element.17) | copy-start | bytes 2162692
  239.7 20.8 %collective-permute-start.22 = (f32[8,8,528]{2,1,0:T(8,128)S(1)}, f32[8,8,528]{2,1,0:T(8,128)}, u32[]{:S(2)}, u32[]{:S(2)}) collective-permute-start(f32[8,8,528]{2,1,0:T(8,128)S(1)} %dynamic-slice_bitcast_fusion.4), channel_id=1, source_target_pairs={{0,1},{1,0},{2,3},{3,2},{4,5},{5,4},{6,7},{7,6},{8,9},{9,8},{10,11... | collective-permute-start | bytes 405512 | tf_op jit(solution)/shard_map/ppermute | solution.py:108
  249.6 22.9 %copy-start.1 = (bf16[11,32,8,256]{3,2,0,1:T(8,128)(2,1)S(1)}, bf16[11,32,8,256]{3,2,0,1:T(8,128)(2,1)}, u32[]{:S(2)}) copy-start(bf16[11,32,8,256]{3,2,0,1:T(8,128)(2,1)} %copy-done) | copy-start | bytes 4325380
  261.4 18.5 %collective-permute-start.23 = (f32[4,8,528]{2,1,0:T(8,128)S(1)}, f32[4,8,528]{2,1,0:T(8,128)S(1)}, u32[]{:S(2)}, u32[]{:S(2)}) collective-permute-start(f32[4,8,528]{2,1,0:T(8,128)S(1)} %dynamic-slice_bitcast_fusion.5), channel_id=1, source_target_pairs={{0,2},{1,3},{2,0},{3,1},{4,6},{5,7},{6,4},{7,5},{8,10},{9,11},{10,... | collective-permute-start | bytes 202760 | tf_op jit(solution)/shard_map/ppermute | solution.py:108
  272.4 2.9 copy-start.12
  276.9 6.1 %copy-start.7 = (f32[128,2816]{1,0:T(8,128)S(1)}, f32[128,2816]{1,0:T(8,128)}, u32[]{:S(2)}) copy-start(f32[128,2816]{1,0:T(8,128)} %copy.128) | copy-start | bytes 4325380
  276.9 6.1 %copy-start.15 = (f32[128,2816]{1,0:T(8,128)S(1)}, f32[128,2816]{1,0:T(8,128)}, u32[]{:S(2)}) copy-start(f32[128,2816]{1,0:T(8,128)} %copy.131) | copy-start | bytes 4325380
  280.0 8.4 %collective-permute-start.24 = (f32[2,8,528]{2,1,0:T(8,128)S(1)}, f32[2,8,528]{2,1,0:T(8,128)S(1)}, u32[]{:S(2)}, u32[]{:S(2)}) collective-permute-start(f32[2,8,528]{2,1,0:T(8,128)S(1)} %dynamic-slice_bitcast_fusion.6), channel_id=1, source_target_pairs={{0,4},{1,5},{2,6},{3,7},{4,0},{5,1},{6,2},{7,3},{8,12},{9,13},{10,... | collective-permute-start | bytes 101384 | tf_op jit(solution)/shard_map/ppermute | solution.py:108
  285.3 10.4 %collective-permute-start.14 = (f32[3,2816]{1,0:T(4,128)S(1)}, f32[3,2816]{1,0:T(4,128)S(1)}, u32[]{:S(2)}, u32[]{:S(2)}) collective-permute-start(f32[3,2816]{1,0:T(4,128)S(1)} %slice.215), channel_id=1, source_target_pairs={{1,0},{2,1},{3,2},{4,3},{5,4},{6,5},{7,6},{8,7},{9,8},{10,9},{11,1... | collective-permute-start | bytes 101384 | tf_op jit(solution)/shard_map/ppermute | solution.py:13
  288.5 8.7 %collective-permute-start.25 = (f32[1,8,528]{2,1,0:T(8,128)S(1)}, f32[1,8,528]{2,1,0:T(8,128)S(1)}, u32[]{:S(2)}, u32[]{:S(2)}) collective-permute-start(f32[1,8,528]{2,1,0:T(8,128)S(1)} %constant_dynamic-slice_fusion), channel_id=1, source_target_pairs={{0,8},{1,9},{2,10},{3,11},{4,12},{5,13},{6,14},{7,15},{8,0},{9,1},... | collective-permute-start | bytes 50696 | tf_op jit(solution)/shard_map/ppermute | solution.py:108
